TPU v7x, 1024 devices: a whole 8x8x8 slice. The times are simulated.
1024 devices in a mesh: ctx: 64 (over x, z), head: 16 (over y, core).
Axes of the slice: x: 8, y: 8, z: 8, core: 2. Of those that a mesh axis runs over, the one named last changes fastest.
Arguments:
- queries: bfloat16 [24576, 8192], P('ctx', 'head'), may hold values from -6 to 6
- keys: bfloat16 [24576, 8192], P('ctx', 'head'), may hold values from -6 to 6
- values: bfloat16 [24576, 8192], P('ctx', 'head'), may hold values from -6 to 6
- doc_lengths: int32 [128], replicated, may hold values from 1 to 1536, 24576 in all
- norm_gain: float32 [8192], P('head'), may hold values from 0.5 to 1.5
- w_out: bfloat16 [8192, 6144], P('head'), may hold values from -0.0625 to 0.0625
Outputs:
- layer_out: bfloat16 [24576, 6144], P(('ctx', 'head'))
Inputs may be any that keep to these rules, and one draw needn't show every extreme that they name: `doc_lengths`: positive lengths of the 128 documents in order, summing to 24576; the longest has exactly 1536 tokens.
All inputs are finite; a program needn't handle non-finite values.
Results may differ from a plain program's by a relative error of at most 0.019.
Values may be sent and summed in bfloat16 or wider, within the bound.
No kernel may reach another device: no remote copies, remote signals or barrier semaphores. Data moves between devices by JAX's collectives and lax.ppermute only.
A program may use at most 64 MiB of HBM per device.

v0:
```python
import jax
import jax.numpy as jnp
from jax import lax
from jax.sharding import PartitionSpec as P

DH = 128


def carried_in(x, axis, join, neutral):
    place = lax.axis_index(axis)
    gathered = jax.tree.map(
        lambda a, kind: lax.all_gather(a.astype(kind), axis),
        x,
        jax.tree.map(lambda a: jnp.bfloat16 if a.dtype == jnp.float32 else a.dtype, x),
    )
    state = jax.tree.map(lambda a, e: jnp.zeros_like(a) + jnp.asarray(e, a.dtype), x, neutral)

    def one(turn, state):
        return join(
            state,
            jax.tree.map(
                lambda a, own: lax.dynamic_index_in_dim(a, turn, 0, False).astype(own.dtype),
                gathered,
                x,
            ),
        )

    return lax.fori_loop(0, place, one, state)


def combine_states(earlier, later):
    reset_later = later[1][0] > 0.5
    state = jnp.where(reset_later, later[0], earlier[0] + later[0])
    return (state, jnp.maximum(earlier[1], later[1]))


def local(queries, keys, values, doc_lengths, norm_gain, w_out):
    tok = queries.shape[0]
    heads_here = queries.shape[1] // DH
    first = lax.axis_index("ctx") * tok
    ends = jnp.cumsum(doc_lengths)
    offsets = jnp.arange(tok, dtype=jnp.int32)
    where_now = first + offsets
    doc = jnp.sum((ends[None, :] <= where_now[:, None]).astype(jnp.int32), axis=1)
    before_doc = jnp.sum((ends <= first - 1).astype(jnp.int32))
    continues = (first > 0) & (before_doc == doc[0])
    q_heads = queries.reshape(tok, heads_here, DH)
    k_heads = keys.reshape(tok, heads_here, DH)
    v_heads = values.reshape(tok, heads_here, DH)
    last = doc == doc[-1]
    k_last = jnp.where(last[:, None, None], k_heads, jnp.zeros_like(k_heads))
    own_state = jnp.einsum("thd,the->hde", k_last, v_heads, preferred_element_type=jnp.float32)
    whole_open = continues & (doc[-1] == doc[0])
    reset = jnp.where(whole_open, 0.0, 1.0).astype(jnp.float32).reshape(1)
    term = (own_state, reset)
    identity = (jnp.zeros_like(own_state), jnp.zeros((1,), jnp.float32))
    carried, _ = carried_in(term, "ctx", combine_states, identity)
    causal = offsets[:, None] >= offsets[None, :]
    allowed = (doc[:, None] == doc[None, :]) & causal
    scores = jnp.einsum("thd,shd->hts", q_heads, k_heads, preferred_element_type=jnp.float32)
    weights = jnp.where(allowed[None], scores, 0.0).astype(jnp.bfloat16)
    intra = jnp.einsum("hts,shd->thd", weights, v_heads, preferred_element_type=jnp.float32)
    active = (continues & (doc == doc[0])).astype(jnp.float32)
    inter = jnp.einsum(
        "thd,hde->the", q_heads.astype(jnp.float32), carried, precision=lax.Precision.HIGHEST
    )
    attn = intra + inter * active[:, None, None]
    meansq = jnp.mean(attn * attn, axis=-1, keepdims=True)
    normed = attn * lax.rsqrt(meansq + 1e-06) * norm_gain.reshape(heads_here, DH)
    hidden = normed.reshape(tok, heads_here * DH).astype(jnp.bfloat16)
    return lax.psum_scatter(
        jnp.dot(hidden, w_out, preferred_element_type=jnp.float32).astype(jnp.bfloat16),
        "head",
        scatter_dimension=0,
        tiled=True,
    )


def solution(mesh):
    placed = (P("ctx", "head"), P("ctx", "head"), P("ctx", "head"), P(), P("head"), P("head", None))
    return jax.shard_map(
        local, mesh=mesh, in_specs=placed, out_specs=P(("ctx", "head"), None), check_vma=False
    )
```

profile of v0, /device:TPU:14, one launch (start us, length us, event | category | flops | bytes accessed | tf_op | source)
XLA Modules:
  0.0 394.0 jit_solution(3287210965746525287)
XLA Ops:
  9.1 1.2 copy.36
  12.8 1.9 convolution_convert_fusion.1
  16.0 1.3 dynamic-slice
  18.0 144.3 %all-reduce = bf16[64]{0:T(256)(128)(2,1)S(1)} all-reduce(bf16[64]{0:T(256)(128)(2,1)S(1)} %dynamic-update-slice), channel_id=1, replica_groups=mesh['ctx'=64,'head'=16] {'ctx'}, use_global_device_ids=true, to_apply=%add | all-reduce | flops 64 | bytes 256
  162.4 1.8 fusion.3
  164.2 125.6 %while.12 = (s32[]{:T(128)}, f32[4,128,128]{2,1,0:T(8,128)S(1)}, s32[]{:T(128)}, bf16[64,1]{0,1:T(2,128)(2,1)S(1)}, bf16[64,4,128,128]{3,2,1,0:T(8,128)(2,1)}, /*index=5*/s32[]{:T(128)}, s32[]{:T(128)}, s32[]{:T(128)}) while((s32[]{:T(128)}, f32[4,128,128]{2,1,0:T(8,128)S(1)}, s32[]{:T(128)}, bf16[64,1]{0,1:T(2,128)(2,1)S(1)}, ...), condition=%wide.region_4.5_spmd, body=%wide.region_3.4_spmd.sunk | while | flops 196615 | bytes 655491 | solution.py:28
  164.8 1.6 add_select_fusion.2
  167.1 1.6 add_select_fusion.2
  169.3 1.6 add_select_fusion.2
  171.6 1.6 add_select_fusion.2
  173.8 1.6 add_select_fusion.2
  176.1 1.6 add_select_fusion.2
  178.3 1.6 add_select_fusion.2
  180.6 1.6 add_select_fusion.2
  182.8 1.6 add_select_fusion.2
  185.0 1.6 add_select_fusion.2
  187.3 1.6 add_select_fusion.2
  189.5 1.6 add_select_fusion.2
  191.8 1.6 add_select_fusion.2
  194.0 1.6 add_select_fusion.2
  196.3 1.6 add_select_fusion.2
  198.5 1.6 add_select_fusion.2
  200.7 1.6 add_select_fusion.2
  203.0 1.6 add_select_fusion.2
  205.2 1.6 add_select_fusion.2
  207.5 1.6 add_select_fusion.2
  209.7 1.6 add_select_fusion.2
  212.0 1.6 add_select_fusion.2
  214.2 1.6 add_select_fusion.2
  216.4 1.6 add_select_fusion.2
  218.7 1.6 add_select_fusion.2
  220.9 1.6 add_select_fusion.2
  223.2 1.6 add_select_fusion.2
  225.4 1.6 add_select_fusion.2
  227.7 1.6 add_select_fusion.2
  229.9 1.6 add_select_fusion.2
  232.1 1.6 add_select_fusion.2
  234.4 1.6 add_select_fusion.2
  236.6 1.6 add_select_fusion.2
  238.9 1.6 add_select_fusion.2
  241.1 1.6 add_select_fusion.2
  243.4 1.6 add_select_fusion.2
  245.6 1.6 add_select_fusion.2
  247.8 1.6 add_select_fusion.2
  250.1 1.6 add_select_fusion.2
  252.3 1.6 add_select_fusion.2
  254.6 1.6 add_select_fusion.2
  256.8 1.6 add_select_fusion.2
  259.1 1.6 add_select_fusion.2
  261.3 1.6 add_select_fusion.2
  263.5 1.6 add_select_fusion.2
  265.8 1.6 add_select_fusion.2
  268.0 1.6 add_select_fusion.2
  270.3 1.6 add_select_fusion.2
  272.5 1.6 add_select_fusion.2
  274.8 1.6 add_select_fusion.2
  277.0 1.6 add_select_fusion.2
  279.2 1.6 add_select_fusion.2
  281.5 1.6 add_select_fusion.2
  283.7 1.6 add_select_fusion.2
  286.0 1.6 add_select_fusion.2
  288.2 1.6 add_select_fusion.2
  290.7 7.6 %convolution_convert_fusion = bf16[384,6144]{1,0:T(8,128)(2,1)} fusion(bf16[384,512]{0,1:T(8,128)(2,1)S(1)} %bitcast.56, bf16[512,6144]{1,0:T(8,128)(2,1)} %param.13), kind=kOutput, calls=%fused_computation.2 | convolution fusion | flops 2418278400 | bytes 11403264 | tf_op jit(solution)/shard_map/dot_general | solution.py:72
  298.3 88.9 %reduce-scatter.2.cloned.1.call-done = bf16[24,6144]{1,0:T(8,128)(2,1)} async-done(((bf16[384,6144]{1,0:T(8,128)(2,1)}), bf16[24,6144]{1,0:T(8,128)(2,1)}) %reduce-scatter.2.cloned.1.call-update) | async-done | bytes 294928 | tf_op jit(solution)/shard_map/reduce_scatter | solution.py:71
  (80 shorter events, 38.5 us)
Async XLA Ops:
  6.5 155.9 %copy-start = (bf16[384,512]{1,0:T(8,128)(2,1)S(1)}, bf16[384,512]{1,0:T(8,128)(2,1)}, u32[]{:S(2)}) copy-start(bf16[384,512]{1,0:T(8,128)(2,1)} %param.8) | copy-start | bytes 1179652
  6.5 284.0 %copy-start.1 = (f32[512]{0:T(512)S(1)}, f32[512]{0:T(512)}, u32[]{:S(2)}) copy-start(f32[512]{0:T(512)} %param.12) | copy-start | bytes 6148
  6.5 157.7 %all-gather.3.cloned.1.call-start = ((), (), s32[]{:S(2)}) async-start(), calls=%async_computation.2 | async-start | bytes 8519680 | tf_op jit(solution)/shard_map/all_gather | solution.py:12
  14.7 372.5 %reduce-scatter.2.cloned.1.call-start = ((), (), s32[]{:S(2)}) async-start(), calls=%async_computation.1 | async-start | bytes 5013504 | tf_op jit(solution)/shard_map/reduce_scatter | solution.py:71
Sparse Core Ops, SparseCore 0:
  14.8 118.4 all-gather.2
  298.4 88.7 reduce-scatter.1
where the time goes:
time: 397 us; the launch traced here: 394 us
  blocking collectives  144 us (36%)
  other arithmetic  127 us (32%)
  waiting for transfers between devices  89 us (22%)
  between operations  15.9 us (4%)
  matrix products  11.9 us (3%)
  local copies, waits for them, and re-layouts  4.67 us (1%)
    unnamed x1, blocking collectives  144 us
    select_n x56, other arithmetic, combine_states(): state = jnp.where(reset_later, later[0], earlier[0] + later[0])  91.1 us
    reduce_scatter x1, waiting for transfers between devices, local(): lax.psum_scatter(jnp.dot(hidden, w_out, preferred_element_type=jnp.float3...  88.9 us
    gt x56, other arithmetic, combine_states(): reset_later = later[1][0] > 0.5  33 us
  transfers between devices with their start and end apart: 2, of which 1 were waited for; matrix products, arithmetic and copies ran while one was open for 1% of the time, Pallas kernels for 0%

commit v1 on v0

v1 whole, which is shorter than its diff:
```python
import jax
import jax.numpy as jnp
from jax import lax
from jax.sharding import PartitionSpec as P

DH = 128


def shift_from(x, axis, size, step):
    return lax.ppermute(x, axis, [(i, i + step) for i in range(size - step)])


def local(n_ctx, n_head, queries, keys, values, doc_lengths, norm_gain, w_out):
    tok = queries.shape[0]
    heads_here = queries.shape[1] // DH
    place = lax.axis_index("ctx")
    first = place * tok
    ends = jnp.cumsum(doc_lengths)

    def doc_at(p):
        return jnp.sum((ends <= p).astype(jnp.int32))

    def whole_open(j):
        return ((j > 0) & (doc_at(j * tok - 1) == doc_at(j * tok + tok - 1))).astype(jnp.float32)

    offsets = jnp.arange(tok, dtype=jnp.int32)
    where_now = first + offsets
    doc = jnp.sum((ends[None, :] <= where_now[:, None]).astype(jnp.int32), axis=1)
    continues = (place > 0) & (doc_at(first - 1) == doc[0])
    q_heads = queries.reshape(tok, heads_here, DH)
    k_heads = keys.reshape(tok, heads_here, DH)
    v_heads = values.reshape(tok, heads_here, DH)

    last = doc == doc[-1]
    k_last = jnp.where(last[:, None, None], k_heads, jnp.zeros_like(k_heads))
    own = jnp.einsum("thd,the->hde", k_last, v_heads, preferred_element_type=jnp.float32)
    wo0 = whole_open(place)
    wo1 = whole_open(place - 1)
    r1 = shift_from(own.astype(jnp.bfloat16), "ctx", n_ctx, 1).astype(jnp.float32)
    t1 = own + wo0 * r1
    r2 = shift_from(t1.astype(jnp.bfloat16), "ctx", n_ctx, 2).astype(jnp.float32)
    t2 = t1 + (wo0 * wo1) * r2
    r3 = shift_from(t2.astype(jnp.bfloat16), "ctx", n_ctx, 1).astype(jnp.float32)
    carried = r3 * continues.astype(jnp.float32)

    causal = offsets[:, None] >= offsets[None, :]
    allowed = (doc[:, None] == doc[None, :]) & causal
    scores = jnp.einsum("thd,shd->hts", q_heads, k_heads, preferred_element_type=jnp.float32)
    weights = jnp.where(allowed[None], scores, 0.0).astype(jnp.bfloat16)
    intra = jnp.einsum("hts,shd->thd", weights, v_heads, preferred_element_type=jnp.float32)
    active = (continues & (doc == doc[0])).astype(jnp.float32)
    inter = jnp.einsum(
        "thd,hde->the", q_heads.astype(jnp.float32), carried, precision=lax.Precision.HIGHEST
    )
    attn = intra + inter * active[:, None, None]
    meansq = jnp.mean(attn * attn, axis=-1, keepdims=True)
    normed = attn * lax.rsqrt(meansq + 1e-06) * norm_gain.reshape(heads_here, DH)
    hidden = normed.reshape(tok, heads_here * DH).astype(jnp.bfloat16)

    n_chip = n_head // 2
    rows = tok // n_head
    me = lax.axis_index("head")
    core = me % 2
    chip = me // 2
    by_owner = hidden.reshape(n_chip, 2, rows, hidden.shape[1])
    mine_rows = lax.dynamic_index_in_dim(by_owner, core, 1, False).reshape(n_chip * rows, -1)
    other_rows = lax.dynamic_index_in_dim(by_owner, 1 - core, 1, False).reshape(n_chip * rows, -1)
    other_part = jnp.dot(other_rows, w_out, preferred_element_type=jnp.float32).astype(jnp.bfloat16)
    sibling = lax.ppermute(other_part, "head", [(i, i ^ 1) for i in range(n_head)])
    mine_part = jnp.dot(mine_rows, w_out, preferred_element_type=jnp.float32).astype(jnp.bfloat16)
    acc = (mine_part.astype(jnp.float32) + sibling.astype(jnp.float32)).reshape(n_chip, rows, -1)

    width = acc.shape[2] // 2
    cw_own = acc[:, :, :width]
    ccw_own = acc[:, :, width:]
    cw_perm = [(i, (i + 2) % n_head) for i in range(n_head)]
    ccw_perm = [(i, (i - 2) % n_head) for i in range(n_head)]

    def chunk(a, idx):
        return lax.dynamic_index_in_dim(a, idx % n_chip, 0, False)

    cw_send = chunk(cw_own, chip - 1)
    ccw_send = chunk(ccw_own, chip + 1)
    for s in range(n_chip - 1):
        cw_recv = lax.ppermute(cw_send.astype(jnp.bfloat16), "head", cw_perm).astype(jnp.float32)
        ccw_recv = lax.ppermute(ccw_send.astype(jnp.bfloat16), "head", ccw_perm).astype(jnp.float32)
        cw_send = cw_recv + chunk(cw_own, chip - s - 2)
        ccw_send = ccw_recv + chunk(ccw_own, chip + s + 2)
    return jnp.concatenate([cw_send, ccw_send], axis=1).astype(jnp.bfloat16)


def solution(mesh):
    placed = (P("ctx", "head"), P("ctx", "head"), P("ctx", "head"), P(), P("head"), P("head", None))
    n_ctx, n_head = mesh.shape["ctx"], mesh.shape["head"]
    return jax.shard_map(
        lambda *a: local(n_ctx, n_head, *a),
        mesh=mesh,
        in_specs=placed,
        out_specs=P(("ctx", "head"), None),
        check_vma=False,
    )
```

time: 397 us -> 136 us (0.34)
  the two profiles are of different devices: /device:TPU:14 before, /device:TPU:56 now
where the time goes in v1:
time: 136 us; the launch traced here: 135 us
  starting transfers between devices  62.7 us (46%)
  waiting for transfers between devices  47.4 us (35%)
  matrix products  12.6 us (9%)
  between operations  4.55 us (3%)
  other arithmetic  4.06 us (3%)
  local copies, waits for them, and re-layouts  3.66 us (3%)
    ppermute x7, starting transfers between devices, local(): lax.ppermute(cw_send.astype(jnp.bfloat16), 'head', cw_perm)  38.4 us
    ppermute x3, waiting for transfers between devices, shift_from(): return lax.ppermute(x, axis, [(i, i + step) for i in range(size - step)])  30.9 us
    ppermute x7, starting transfers between devices, local(): lax.ppermute(ccw_send.astype(jnp.bfloat16), 'head', ccw_perm)  13.4 us
    ppermute x3, starting transfers between devices, shift_from(): return lax.ppermute(x, axis, [(i, i + step) for i in range(size - step)])  9.03 us
    ppermute x7, waiting for transfers between devices, local(): lax.ppermute(ccw_send.astype(jnp.bfloat16), 'head', ccw_perm)  6.26 us
    ppermute x7, waiting for transfers between devices, local(): lax.ppermute(cw_send.astype(jnp.bfloat16), 'head', cw_perm)  5.91 us
    dot_general x1, matrix products, local(): jnp.dot(other_rows, w_out, preferred_element_type=jnp.float32)  5.7 us
    ppermute x1, waiting for transfers between devices, local(): lax.ppermute(other_part, 'head', [(i, i ^ 1) for i in range(n_head)])  4.36 us
  transfers between devices with their start and end apart: 18, of which 13 were waited for; matrix products, arithmetic and copies ran while one was open for 1% of the time, Pallas kernels for 0%

profile of v1, /device:TPU:56, one launch (start us, length us, event | category | flops | bytes accessed | tf_op | source)
XLA Modules:
  0.0 135.0 jit_solution(3488110962481485607)
XLA Ops:
  0.0 0.0 copy-start
  0.0 0.0 copy-start.2
  0.0 0.8 copy.20
  0.8 0.2 reduce-window.8
  1.0 0.1 reduce
  1.1 0.2 convert_reduce_fusion
  1.4 0.6 fusion.49
  2.0 1.2 copy.30
  3.2 0.7 fusion.45
  5.2 1.3 broadcast_compare_fusion
  6.5 1.3 fusion.50
  7.8 5.2 %collective-permute-start = (bf16[4,128,128]{2,1,0:T(8,128)(2,1)S(1)}, bf16[4,128,128]{2,1,0:T(8,128)(2,1)S(1)}, u32[]{:S(2)}, u32[]{:S(2)}) collective-permute-start(bf16[4,128,128]{2,1,0:T(8,128)(2,1)S(1)} %get-tuple-element.17), channel_id=1, source_target_pairs={{0,16},{16,32},{32,48},{48,64},{64,80},{80,96},{96,112},{112,128},... | collective-permute-start | bytes 393224 | tf_op jit(solution)/shard_map/ppermute | solution.py:10
  15.5 13.1 %collective-permute-done = bf16[4,128,128]{2,1,0:T(8,128)(2,1)S(1)} collective-permute-done((bf16[4,128,128]{2,1,0:T(8,128)(2,1)S(1)}, bf16[4,128,128]{2,1,0:T(8,128)(2,1)S(1)}, u32[]{:S(2)}, u32[]{:S(2)}) %collective-permute-start) | collective-permute-done | bytes 131104 | tf_op jit(solution)/shard_map/ppermute | solution.py:10
  28.6 1.9 %collective-permute-start.1 = (bf16[4,128,128]{2,1,0:T(8,128)(2,1)S(1)}, bf16[4,128,128]{2,1,0:T(8,128)(2,1)S(1)}, u32[]{:S(2)}, u32[]{:S(2)}) collective-permute-start(bf16[4,128,128]{2,1,0:T(8,128)(2,1)S(1)} %fusion.38), channel_id=1, source_target_pairs={{0,32},{16,48},{32,64},{48,80},{64,96},{80,112},{96,128},{112,144}... | collective-permute-start | bytes 393224 | tf_op jit(solution)/shard_map/ppermute | solution.py:10
  30.5 0.1 fusion.7
  30.6 10.4 %collective-permute-done.1 = bf16[4,128,128]{2,1,0:T(8,128)(2,1)S(1)} collective-permute-done((bf16[4,128,128]{2,1,0:T(8,128)(2,1)S(1)}, bf16[4,128,128]{2,1,0:T(8,128)(2,1)S(1)}, u32[]{:S(2)}, u32[]{:S(2)}) %collective-permute-start.1) | collective-permute-done | bytes 131104 | tf_op jit(solution)/shard_map/ppermute | solution.py:10
  41.0 0.1 add_convert_fusion
  41.1 0.0 copy-start.1
  41.1 1.9 %collective-permute-start.2 = (bf16[4,128,128]{2,1,0:T(8,128)(2,1)S(1)}, bf16[4,128,128]{2,1,0:T(8,128)(2,1)S(1)}, u32[]{:S(2)}, u32[]{:S(2)}) collective-permute-start(bf16[4,128,128]{2,1,0:T(8,128)(2,1)S(1)} %add_convert_fusion), channel_id=1, source_target_pairs={{0,16},{16,32},{32,48},{48,64},{64,80},{80,96},{96,112},{112,128},... | collective-permute-start | bytes 393224 | tf_op jit(solution)/shard_map/ppermute | solution.py:10
  43.1 0.0 copy-done
  43.1 0.0 copy-done.2
  43.1 0.8 fusion.4
  43.9 7.4 %collective-permute-done.2 = bf16[4,128,128]{2,1,0:T(8,128)(2,1)S(1)} collective-permute-done((bf16[4,128,128]{2,1,0:T(8,128)(2,1)S(1)}, bf16[4,128,128]{2,1,0:T(8,128)(2,1)S(1)}, u32[]{:S(2)}, u32[]{:S(2)}) %collective-permute-start.2) | collective-permute-done | bytes 131104 | tf_op jit(solution)/shard_map/ppermute | solution.py:10
  51.3 0.6 multiply_reduce_fusion
  52.0 0.0 copy-done.1
  52.0 0.1 multiply_convert_fusion
  52.1 0.2 copy.28
  52.4 0.2 convert_element_type.178
  52.6 5.7 %convolution_convert_fusion = bf16[192,6144]{1,0:T(8,128)(2,1)} fusion(bf16[192,512]{1,0:T(8,128)(2,1)S(1)} %bitcast.110, bf16[512,6144]{1,0:T(8,128)(2,1)} %param.11), kind=kOutput, calls=%fused_computation | convolution fusion | flops 1209139200 | bytes 8847360 | tf_op jit(solution)/shard_map/dot_general | solution.py:68
  58.3 1.9 %collective-permute-start.3 = (bf16[192,6144]{1,0:T(8,128)(2,1)}, bf16[192,6144]{1,0:T(8,128)(2,1)S(1)}, u32[]{:S(2)}, u32[]{:S(2)}) collective-permute-start(bf16[192,6144]{1,0:T(8,128)(2,1)} %convolution_convert_fusion), channel_id=1, source_target_pairs={{0,1},{1,0},{2,3},{3,2},{4,5},{5,4},{6,7},{7,6},{8,9},{9,8},{10,11... | collective-permute-start | bytes 7077896 | tf_op jit(solution)/shard_map/ppermute | solution.py:69
  60.5 4.4 %collective-permute-done.3 = bf16[192,6144]{1,0:T(8,128)(2,1)S(1)} collective-permute-done((bf16[192,6144]{1,0:T(8,128)(2,1)}, bf16[192,6144]{1,0:T(8,128)(2,1)S(1)}, u32[]{:S(2)}, u32[]{:S(2)}) %collective-permute-start.3) | collective-permute-done | bytes 2359328 | tf_op jit(solution)/shard_map/ppermute | solution.py:69
  64.9 4.2 %convert_add_fusion = f32[192,6144]{1,0:T(8,128)S(1)} fusion(bf16[192,6144]{1,0:T(8,128)(2,1)S(1)} %collective-permute-done.3, bf16[192,512]{1,0:T(8,128)(2,1)S(1)} %bitcast.111, bf16[512,6144]{1,0:T(8,128)(2,1)} %param.11), kind=kOutput, calls=%fused_computation.3 | convolution fusion | flops 1212678144 | bytes 13565952 | tf_op jit(solution)/shard_map/dot_general | solution.py:70
  69.1 0.5 fusion.48
  69.7 4.8 %collective-permute-start.4 = (bf16[24,3072]{1,0:T(8,128)(2,1)S(1)}, bf16[24,3072]{1,0:T(8,128)(2,1)S(1)}, u32[]{:S(2)}, u32[]{:S(2)}) collective-permute-start(bf16[24,3072]{1,0:T(8,128)(2,1)S(1)} %fusion.39), channel_id=1, source_target_pairs={{0,2},{1,3},{2,4},{3,5},{4,6},{5,7},{6,8},{7,9},{8,10},{9,11},{10,... | collective-permute-start | bytes 442376 | tf_op jit(solution)/shard_map/ppermute | solution.py:85
  74.5 1.9 %collective-permute-start.11 = (bf16[24,3072]{1,0:T(8,128)(2,1)S(1)}, bf16[24,3072]{1,0:T(8,128)(2,1)S(1)}, u32[]{:S(2)}, u32[]{:S(2)}) collective-permute-start(bf16[24,3072]{1,0:T(8,128)(2,1)S(1)} %fusion.40), channel_id=1, source_target_pairs={{0,14},{1,15},{2,0},{3,1},{4,2},{5,3},{6,4},{7,5},{8,6},{9,7},{10,... | collective-permute-start | bytes 442376 | tf_op jit(solution)/shard_map/ppermute | solution.py:86
  76.4 1.4 %collective-permute-done.4 = bf16[24,3072]{1,0:T(8,128)(2,1)S(1)} collective-permute-done((bf16[24,3072]{1,0:T(8,128)(2,1)S(1)}, bf16[24,3072]{1,0:T(8,128)(2,1)S(1)}, u32[]{:S(2)}, u32[]{:S(2)}) %collective-permute-start.4) | collective-permute-done | bytes 147488 | tf_op jit(solution)/shard_map/ppermute | solution.py:85
  77.9 5.6 %collective-permute-start.5 = (bf16[24,3072]{1,0:T(8,128)(2,1)S(1)}, bf16[24,3072]{1,0:T(8,128)(2,1)S(1)}, u32[]{:S(2)}, u32[]{:S(2)}) collective-permute-start(bf16[24,3072]{1,0:T(8,128)(2,1)S(1)} %fusion.34), channel_id=1, source_target_pairs={{0,2},{1,3},{2,4},{3,5},{4,6},{5,7},{6,8},{7,9},{8,10},{9,11},{10,... | collective-permute-start | bytes 442376 | tf_op jit(solution)/shard_map/ppermute | solution.py:85
  83.5 0.0 collective-permute-done.11
  83.6 1.9 %collective-permute-start.12 = (bf16[24,3072]{1,0:T(8,128)(2,1)S(1)}, bf16[24,3072]{1,0:T(8,128)(2,1)S(1)}, u32[]{:S(2)}, u32[]{:S(2)}) collective-permute-start(bf16[24,3072]{1,0:T(8,128)(2,1)S(1)} %fusion.27), channel_id=1, source_target_pairs={{0,14},{1,15},{2,0},{3,1},{4,2},{5,3},{6,4},{7,5},{8,6},{9,7},{10,... | collective-permute-start | bytes 442376 | tf_op jit(solution)/shard_map/ppermute | solution.py:86
  85.5 0.7 collective-permute-done.5
  86.2 5.6 %collective-permute-start.6 = (bf16[24,3072]{1,0:T(8,128)(2,1)S(1)}, bf16[24,3072]{1,0:T(8,128)(2,1)S(1)}, u32[]{:S(2)}, u32[]{:S(2)}) collective-permute-start(bf16[24,3072]{1,0:T(8,128)(2,1)S(1)} %fusion.33), channel_id=1, source_target_pairs={{0,2},{1,3},{2,4},{3,5},{4,6},{5,7},{6,8},{7,9},{8,10},{9,11},{10,... | collective-permute-start | bytes 442376 | tf_op jit(solution)/shard_map/ppermute | solution.py:85
  91.8 0.0 collective-permute-done.12
  91.8 1.9 %collective-permute-start.13 = (bf16[24,3072]{1,0:T(8,128)(2,1)S(1)}, bf16[24,3072]{1,0:T(8,128)(2,1)S(1)}, u32[]{:S(2)}, u32[]{:S(2)}) collective-permute-start(bf16[24,3072]{1,0:T(8,128)(2,1)S(1)} %fusion.26), channel_id=1, source_target_pairs={{0,14},{1,15},{2,0},{3,1},{4,2},{5,3},{6,4},{7,5},{8,6},{9,7},{10,... | collective-permute-start | bytes 442376 | tf_op jit(solution)/shard_map/ppermute | solution.py:86
  93.8 0.7 collective-permute-done.6
  94.5 5.6 %collective-permute-start.7 = (bf16[24,3072]{1,0:T(8,128)(2,1)S(1)}, bf16[24,3072]{1,0:T(8,128)(2,1)S(1)}, u32[]{:S(2)}, u32[]{:S(2)}) collective-permute-start(bf16[24,3072]{1,0:T(8,128)(2,1)S(1)} %fusion.32), channel_id=1, source_target_pairs={{0,2},{1,3},{2,4},{3,5},{4,6},{5,7},{6,8},{7,9},{8,10},{9,11},{10,... | collective-permute-start | bytes 442376 | tf_op jit(solution)/shard_map/ppermute | solution.py:85
  100.1 0.0 collective-permute-done.13
  100.1 1.9 %collective-permute-start.14 = (bf16[24,3072]{1,0:T(8,128)(2,1)S(1)}, bf16[24,3072]{1,0:T(8,128)(2,1)S(1)}, u32[]{:S(2)}, u32[]{:S(2)}) collective-permute-start(bf16[24,3072]{1,0:T(8,128)(2,1)S(1)} %fusion.25), channel_id=1, source_target_pairs={{0,14},{1,15},{2,0},{3,1},{4,2},{5,3},{6,4},{7,5},{8,6},{9,7},{10,... | collective-permute-start | bytes 442376 | tf_op jit(solution)/shard_map/ppermute | solution.py:86
  102.0 0.7 collective-permute-done.7
  102.7 5.6 %collective-permute-start.8 = (bf16[24,3072]{1,0:T(8,128)(2,1)S(1)}, bf16[24,3072]{1,0:T(8,128)(2,1)S(1)}, u32[]{:S(2)}, u32[]{:S(2)}) collective-permute-start(bf16[24,3072]{1,0:T(8,128)(2,1)S(1)} %fusion.31), channel_id=1, source_target_pairs={{0,2},{1,3},{2,4},{3,5},{4,6},{5,7},{6,8},{7,9},{8,10},{9,11},{10,... | collective-permute-start | bytes 442376 | tf_op jit(solution)/shard_map/ppermute | solution.py:85
  108.3 0.0 collective-permute-done.14
  108.4 1.9 %collective-permute-start.15 = (bf16[24,3072]{1,0:T(8,128)(2,1)S(1)}, bf16[24,3072]{1,0:T(8,128)(2,1)S(1)}, u32[]{:S(2)}, u32[]{:S(2)}) collective-permute-start(bf16[24,3072]{1,0:T(8,128)(2,1)S(1)} %fusion.24), channel_id=1, source_target_pairs={{0,14},{1,15},{2,0},{3,1},{4,2},{5,3},{6,4},{7,5},{8,6},{9,7},{10,... | collective-permute-start | bytes 442376 | tf_op jit(solution)/shard_map/ppermute | solution.py:86
  110.3 0.7 collective-permute-done.8
  111.0 5.6 %collective-permute-start.9 = (bf16[24,3072]{1,0:T(8,128)(2,1)S(1)}, bf16[24,3072]{1,0:T(8,128)(2,1)S(1)}, u32[]{:S(2)}, u32[]{:S(2)}) collective-permute-start(bf16[24,3072]{1,0:T(8,128)(2,1)S(1)} %fusion.30), channel_id=1, source_target_pairs={{0,2},{1,3},{2,4},{3,5},{4,6},{5,7},{6,8},{7,9},{8,10},{9,11},{10,... | collective-permute-start | bytes 442376 | tf_op jit(solution)/shard_map/ppermute | solution.py:85
  116.6 0.0 collective-permute-done.15
  116.7 1.9 %collective-permute-start.16 = (bf16[24,3072]{1,0:T(8,128)(2,1)S(1)}, bf16[24,3072]{1,0:T(8,128)(2,1)S(1)}, u32[]{:S(2)}, u32[]{:S(2)}) collective-permute-start(bf16[24,3072]{1,0:T(8,128)(2,1)S(1)} %fusion.23), channel_id=1, source_target_pairs={{0,14},{1,15},{2,0},{3,1},{4,2},{5,3},{6,4},{7,5},{8,6},{9,7},{10,... | collective-permute-start | bytes 442376 | tf_op jit(solution)/shard_map/ppermute | solution.py:86
  118.6 1.4 %collective-permute-done.9 = bf16[24,3072]{1,0:T(8,128)(2,1)S(1)} collective-permute-done((bf16[24,3072]{1,0:T(8,128)(2,1)S(1)}, bf16[24,3072]{1,0:T(8,128)(2,1)S(1)}, u32[]{:S(2)}, u32[]{:S(2)}) %collective-permute-start.9) | collective-permute-done | bytes 147488 | tf_op jit(solution)/shard_map/ppermute | solution.py:85
  120.0 5.6 %collective-permute-start.10 = (bf16[24,3072]{1,0:T(8,128)(2,1)S(1)}, bf16[24,3072]{1,0:T(8,128)(2,1)S(1)}, u32[]{:S(2)}, u32[]{:S(2)}) collective-permute-start(bf16[24,3072]{1,0:T(8,128)(2,1)S(1)} %fusion.29), channel_id=1, source_target_pairs={{0,2},{1,3},{2,4},{3,5},{4,6},{5,7},{6,8},{7,9},{8,10},{9,11},{10,... | collective-permute-start | bytes 442376 | tf_op jit(solution)/shard_map/ppermute | solution.py:85
  125.6 0.3 collective-permute-done.16
  126.0 1.9 %collective-permute-start.17 = (bf16[24,3072]{1,0:T(8,128)(2,1)S(1)}, bf16[24,3072]{1,0:T(8,128)(2,1)S(1)}, u32[]{:S(2)}, u32[]{:S(2)}) collective-permute-start(bf16[24,3072]{1,0:T(8,128)(2,1)S(1)} %fusion.22), channel_id=1, source_target_pairs={{0,14},{1,15},{2,0},{3,1},{4,2},{5,3},{6,4},{7,5},{8,6},{9,7},{10,... | collective-permute-start | bytes 442376 | tf_op jit(solution)/shard_map/ppermute | solution.py:86
  127.9 0.4 collective-permute-done.10
  128.3 5.9 %collective-permute-done.17 = bf16[24,3072]{1,0:T(8,128)(2,1)S(1)} collective-permute-done((bf16[24,3072]{1,0:T(8,128)(2,1)S(1)}, bf16[24,3072]{1,0:T(8,128)(2,1)S(1)}, u32[]{:S(2)}, u32[]{:S(2)}) %collective-permute-start.17) | collective-permute-done | bytes 147488 | tf_op jit(solution)/shard_map/ppermute | solution.py:86
  134.3 0.7 pad_maximum_fusion
  (20 shorter events, 0.6 us)
Async XLA Ops:
  0.0 43.1 %copy-start = (bf16[384,512]{1,0:T(8,128)(2,1)S(1)}, bf16[384,512]{1,0:T(8,128)(2,1)}, u32[]{:S(2)}) copy-start(bf16[384,512]{1,0:T(8,128)(2,1)} %param.6) | copy-start | bytes 1179652
  0.0 43.1 %copy-start.2 = (bf16[384,512]{1,0:T(8,128)(2,1)S(1)}, bf16[384,512]{1,0:T(8,128)(2,1)}, u32[]{:S(2)}) copy-start(bf16[384,512]{1,0:T(8,128)(2,1)} %param.8) | copy-start | bytes 1179652
  7.8 20.8 %collective-permute-start = (bf16[4,128,128]{2,1,0:T(8,128)(2,1)S(1)}, bf16[4,128,128]{2,1,0:T(8,128)(2,1)S(1)}, u32[]{:S(2)}, u32[]{:S(2)}) collective-permute-start(bf16[4,128,128]{2,1,0:T(8,128)(2,1)S(1)} %get-tuple-element.17), channel_id=1, source_target_pairs={{0,16},{16,32},{32,48},{48,64},{64,80},{80,96},{96,112},{112,128},... | collective-permute-start | bytes 393224 | tf_op jit(solution)/shard_map/ppermute | solution.py:10
  28.6 12.5 %collective-permute-start.1 = (bf16[4,128,128]{2,1,0:T(8,128)(2,1)S(1)}, bf16[4,128,128]{2,1,0:T(8,128)(2,1)S(1)}, u32[]{:S(2)}, u32[]{:S(2)}) collective-permute-start(bf16[4,128,128]{2,1,0:T(8,128)(2,1)S(1)} %fusion.38), channel_id=1, source_target_pairs={{0,32},{16,48},{32,64},{48,80},{64,96},{80,112},{96,128},{112,144}... | collective-permute-start | bytes 393224 | tf_op jit(solution)/shard_map/ppermute | solution.py:10
  41.1 10.8 %copy-start.1 = (f32[512]{0:T(512)S(1)}, f32[512]{0:T(512)}, u32[]{:S(2)}) copy-start(f32[512]{0:T(512)} %param.10) | copy-start | bytes 6148
  41.1 10.2 %collective-permute-start.2 = (bf16[4,128,128]{2,1,0:T(8,128)(2,1)S(1)}, bf16[4,128,128]{2,1,0:T(8,128)(2,1)S(1)}, u32[]{:S(2)}, u32[]{:S(2)}) collective-permute-start(bf16[4,128,128]{2,1,0:T(8,128)(2,1)S(1)} %add_convert_fusion), channel_id=1, source_target_pairs={{0,16},{16,32},{32,48},{48,64},{64,80},{80,96},{96,112},{112,128},... | collective-permute-start | bytes 393224 | tf_op jit(solution)/shard_map/ppermute | solution.py:10
  58.3 6.6 %collective-permute-start.3 = (bf16[192,6144]{1,0:T(8,128)(2,1)}, bf16[192,6144]{1,0:T(8,128)(2,1)S(1)}, u32[]{:S(2)}, u32[]{:S(2)}) collective-permute-start(bf16[192,6144]{1,0:T(8,128)(2,1)} %convolution_convert_fusion), channel_id=1, source_target_pairs={{0,1},{1,0},{2,3},{3,2},{4,5},{5,4},{6,7},{7,6},{8,9},{9,8},{10,11... | collective-permute-start | bytes 7077896 | tf_op jit(solution)/shard_map/ppermute | solution.py:69
  69.7 8.2 %collective-permute-start.4 = (bf16[24,3072]{1,0:T(8,128)(2,1)S(1)}, bf16[24,3072]{1,0:T(8,128)(2,1)S(1)}, u32[]{:S(2)}, u32[]{:S(2)}) collective-permute-start(bf16[24,3072]{1,0:T(8,128)(2,1)S(1)} %fusion.39), channel_id=1, source_target_pairs={{0,2},{1,3},{2,4},{3,5},{4,6},{5,7},{6,8},{7,9},{8,10},{9,11},{10,... | collective-permute-start | bytes 442376 | tf_op jit(solution)/shard_map/ppermute | solution.py:85
  74.5 9.0 %collective-permute-start.11 = (bf16[24,3072]{1,0:T(8,128)(2,1)S(1)}, bf16[24,3072]{1,0:T(8,128)(2,1)S(1)}, u32[]{:S(2)}, u32[]{:S(2)}) collective-permute-start(bf16[24,3072]{1,0:T(8,128)(2,1)S(1)} %fusion.40), channel_id=1, source_target_pairs={{0,14},{1,15},{2,0},{3,1},{4,2},{5,3},{6,4},{7,5},{8,6},{9,7},{10,... | collective-permute-start | bytes 442376 | tf_op jit(solution)/shard_map/ppermute | solution.py:86
  77.9 8.3 %collective-permute-start.5 = (bf16[24,3072]{1,0:T(8,128)(2,1)S(1)}, bf16[24,3072]{1,0:T(8,128)(2,1)S(1)}, u32[]{:S(2)}, u32[]{:S(2)}) collective-permute-start(bf16[24,3072]{1,0:T(8,128)(2,1)S(1)} %fusion.34), channel_id=1, source_target_pairs={{0,2},{1,3},{2,4},{3,5},{4,6},{5,7},{6,8},{7,9},{8,10},{9,11},{10,... | collective-permute-start | bytes 442376 | tf_op jit(solution)/shard_map/ppermute | solution.py:85
  83.6 8.2 %collective-permute-start.12 = (bf16[24,3072]{1,0:T(8,128)(2,1)S(1)}, bf16[24,3072]{1,0:T(8,128)(2,1)S(1)}, u32[]{:S(2)}, u32[]{:S(2)}) collective-permute-start(bf16[24,3072]{1,0:T(8,128)(2,1)S(1)} %fusion.27), channel_id=1, source_target_pairs={{0,14},{1,15},{2,0},{3,1},{4,2},{5,3},{6,4},{7,5},{8,6},{9,7},{10,... | collective-permute-start | bytes 442376 | tf_op jit(solution)/shard_map/ppermute | solution.py:86
  86.2 8.2 %collective-permute-start.6 = (bf16[24,3072]{1,0:T(8,128)(2,1)S(1)}, bf16[24,3072]{1,0:T(8,128)(2,1)S(1)}, u32[]{:S(2)}, u32[]{:S(2)}) collective-permute-start(bf16[24,3072]{1,0:T(8,128)(2,1)S(1)} %fusion.33), channel_id=1, source_target_pairs={{0,2},{1,3},{2,4},{3,5},{4,6},{5,7},{6,8},{7,9},{8,10},{9,11},{10,... | collective-permute-start | bytes 442376 | tf_op jit(solution)/shard_map/ppermute | solution.py:85
  91.8 8.2 %collective-permute-start.13 = (bf16[24,3072]{1,0:T(8,128)(2,1)S(1)}, bf16[24,3072]{1,0:T(8,128)(2,1)S(1)}, u32[]{:S(2)}, u32[]{:S(2)}) collective-permute-start(bf16[24,3072]{1,0:T(8,128)(2,1)S(1)} %fusion.26), channel_id=1, source_target_pairs={{0,14},{1,15},{2,0},{3,1},{4,2},{5,3},{6,4},{7,5},{8,6},{9,7},{10,... | collective-permute-start | bytes 442376 | tf_op jit(solution)/shard_map/ppermute | solution.py:86
  94.5 8.2 %collective-permute-start.7 = (bf16[24,3072]{1,0:T(8,128)(2,1)S(1)}, bf16[24,3072]{1,0:T(8,128)(2,1)S(1)}, u32[]{:S(2)}, u32[]{:S(2)}) collective-permute-start(bf16[24,3072]{1,0:T(8,128)(2,1)S(1)} %fusion.32), channel_id=1, source_target_pairs={{0,2},{1,3},{2,4},{3,5},{4,6},{5,7},{6,8},{7,9},{8,10},{9,11},{10,... | collective-permute-start | bytes 442376 | tf_op jit(solution)/shard_map/ppermute | solution.py:85
  100.1 8.2 %collective-permute-start.14 = (bf16[24,3072]{1,0:T(8,128)(2,1)S(1)}, bf16[24,3072]{1,0:T(8,128)(2,1)S(1)}, u32[]{:S(2)}, u32[]{:S(2)}) collective-permute-start(bf16[24,3072]{1,0:T(8,128)(2,1)S(1)} %fusion.25), channel_id=1, source_target_pairs={{0,14},{1,15},{2,0},{3,1},{4,2},{5,3},{6,4},{7,5},{8,6},{9,7},{10,... | collective-permute-start | bytes 442376 | tf_op jit(solution)/shard_map/ppermute | solution.py:86
  102.7 8.2 %collective-permute-start.8 = (bf16[24,3072]{1,0:T(8,128)(2,1)S(1)}, bf16[24,3072]{1,0:T(8,128)(2,1)S(1)}, u32[]{:S(2)}, u32[]{:S(2)}) collective-permute-start(bf16[24,3072]{1,0:T(8,128)(2,1)S(1)} %fusion.31), channel_id=1, source_target_pairs={{0,2},{1,3},{2,4},{3,5},{4,6},{5,7},{6,8},{7,9},{8,10},{9,11},{10,... | collective-permute-start | bytes 442376 | tf_op jit(solution)/shard_map/ppermute | solution.py:85
  108.4 8.2 %collective-permute-start.15 = (bf16[24,3072]{1,0:T(8,128)(2,1)S(1)}, bf16[24,3072]{1,0:T(8,128)(2,1)S(1)}, u32[]{:S(2)}, u32[]{:S(2)}) collective-permute-start(bf16[24,3072]{1,0:T(8,128)(2,1)S(1)} %fusion.24), channel_id=1, source_target_pairs={{0,14},{1,15},{2,0},{3,1},{4,2},{5,3},{6,4},{7,5},{8,6},{9,7},{10,... | collective-permute-start | bytes 442376 | tf_op jit(solution)/shard_map/ppermute | solution.py:86
  111.0 9.0 %collective-permute-start.9 = (bf16[24,3072]{1,0:T(8,128)(2,1)S(1)}, bf16[24,3072]{1,0:T(8,128)(2,1)S(1)}, u32[]{:S(2)}, u32[]{:S(2)}) collective-permute-start(bf16[24,3072]{1,0:T(8,128)(2,1)S(1)} %fusion.30), channel_id=1, source_target_pairs={{0,2},{1,3},{2,4},{3,5},{4,6},{5,7},{6,8},{7,9},{8,10},{9,11},{10,... | collective-permute-start | bytes 442376 | tf_op jit(solution)/shard_map/ppermute | solution.py:85
  116.7 9.3 %collective-permute-start.16 = (bf16[24,3072]{1,0:T(8,128)(2,1)S(1)}, bf16[24,3072]{1,0:T(8,128)(2,1)S(1)}, u32[]{:S(2)}, u32[]{:S(2)}) collective-permute-start(bf16[24,3072]{1,0:T(8,128)(2,1)S(1)} %fusion.23), channel_id=1, source_target_pairs={{0,14},{1,15},{2,0},{3,1},{4,2},{5,3},{6,4},{7,5},{8,6},{9,7},{10,... | collective-permute-start | bytes 442376 | tf_op jit(solution)/shard_map/ppermute | solution.py:86
  120.0 8.3 %collective-permute-start.10 = (bf16[24,3072]{1,0:T(8,128)(2,1)S(1)}, bf16[24,3072]{1,0:T(8,128)(2,1)S(1)}, u32[]{:S(2)}, u32[]{:S(2)}) collective-permute-start(bf16[24,3072]{1,0:T(8,128)(2,1)S(1)} %fusion.29), channel_id=1, source_target_pairs={{0,2},{1,3},{2,4},{3,5},{4,6},{5,7},{6,8},{7,9},{8,10},{9,11},{10,... | collective-permute-start | bytes 442376 | tf_op jit(solution)/shard_map/ppermute | solution.py:85
  126.0 8.2 %collective-permute-start.17 = (bf16[24,3072]{1,0:T(8,128)(2,1)S(1)}, bf16[24,3072]{1,0:T(8,128)(2,1)S(1)}, u32[]{:S(2)}, u32[]{:S(2)}) collective-permute-start(bf16[24,3072]{1,0:T(8,128)(2,1)S(1)} %fusion.22), channel_id=1, source_target_pairs={{0,14},{1,15},{2,0},{3,1},{4,2},{5,3},{6,4},{7,5},{8,6},{9,7},{10,... | collective-permute-start | bytes 442376 | tf_op jit(solution)/shard_map/ppermute | solution.py:86

commit v2 on v1

--- a/solution.py
+++ b/solution.py
@@ -36,12 +36,13 @@
     own = jnp.einsum("thd,the->hde", k_last, v_heads, preferred_element_type=jnp.float32)
     wo0 = whole_open(place)
     wo1 = whole_open(place - 1)
-    r1 = shift_from(own.astype(jnp.bfloat16), "ctx", n_ctx, 1).astype(jnp.float32)
-    t1 = own + wo0 * r1
-    r2 = shift_from(t1.astype(jnp.bfloat16), "ctx", n_ctx, 2).astype(jnp.float32)
-    t2 = t1 + (wo0 * wo1) * r2
-    r3 = shift_from(t2.astype(jnp.bfloat16), "ctx", n_ctx, 1).astype(jnp.float32)
-    carried = r3 * continues.astype(jnp.float32)
+    wo2 = whole_open(place - 2)
+    own_b = own.astype(jnp.bfloat16)
+    r1 = shift_from(own_b, "ctx", n_ctx, 1).astype(jnp.float32)
+    r2 = shift_from(own_b, "ctx", n_ctx, 2).astype(jnp.float32)
+    pair = own + wo0 * r1
+    r3 = shift_from(pair.astype(jnp.bfloat16), "ctx", n_ctx, 3).astype(jnp.float32)
+    carried = (r1 + wo1 * (r2 + wo2 * r3)) * continues.astype(jnp.float32)
 
     causal = offsets[:, None] >= offsets[None, :]
     allowed = (doc[:, None] == doc[None, :]) & causal
@@ -67,26 +68,30 @@
     other_rows = lax.dynamic_index_in_dim(by_owner, 1 - core, 1, False).reshape(n_chip * rows, -1)
     other_part = jnp.dot(other_rows, w_out, preferred_element_type=jnp.float32).astype(jnp.bfloat16)
     sibling = lax.ppermute(other_part, "head", [(i, i ^ 1) for i in range(n_head)])
-    mine_part = jnp.dot(mine_rows, w_out, preferred_element_type=jnp.float32).astype(jnp.bfloat16)
+    mine_part = lax.optimization_barrier(
+        jnp.dot(mine_rows, w_out, preferred_element_type=jnp.float32).astype(jnp.bfloat16)
+    )
     acc = (mine_part.astype(jnp.float32) + sibling.astype(jnp.float32)).reshape(n_chip, rows, -1)
 
-    width = acc.shape[2] // 2
-    cw_own = acc[:, :, :width]
-    ccw_own = acc[:, :, width:]
     cw_perm = [(i, (i + 2) % n_head) for i in range(n_head)]
     ccw_perm = [(i, (i - 2) % n_head) for i in range(n_head)]
 
-    def chunk(a, idx):
-        return lax.dynamic_index_in_dim(a, idx % n_chip, 0, False)
+    def chunk(idx):
+        return lax.dynamic_index_in_dim(acc, idx % n_chip, 0, False)
 
-    cw_send = chunk(cw_own, chip - 1)
-    ccw_send = chunk(ccw_own, chip + 1)
-    for s in range(n_chip - 1):
+    cw_steps = n_chip // 2
+    ccw_steps = n_chip - 1 - cw_steps
+    cw_send = chunk(chip + cw_steps)
+    ccw_send = chunk(chip - ccw_steps)
+    for s in range(cw_steps):
         cw_recv = lax.ppermute(cw_send.astype(jnp.bfloat16), "head", cw_perm).astype(jnp.float32)
-        ccw_recv = lax.ppermute(ccw_send.astype(jnp.bfloat16), "head", ccw_perm).astype(jnp.float32)
-        cw_send = cw_recv + chunk(cw_own, chip - s - 2)
-        ccw_send = ccw_recv + chunk(ccw_own, chip + s + 2)
-    return jnp.concatenate([cw_send, ccw_send], axis=1).astype(jnp.bfloat16)
+        if s < ccw_steps:
+            ccw_recv = lax.ppermute(ccw_send.astype(jnp.bfloat16), "head", ccw_perm).astype(jnp.float32)
+        if s < cw_steps - 1:
+            cw_send = cw_recv + chunk(chip + cw_steps - 1 - s)
+        if s < ccw_steps - 1:
+            ccw_send = ccw_recv + chunk(chip - ccw_steps + 1 + s)
+    return (cw_recv + ccw_recv + chunk(chip)).astype(jnp.bfloat16)
 
 
 def solution(mesh):

time: 136 us -> 121 us (0.89)
  the two profiles are of different devices: /device:TPU:56 before, /device:TPU:14 now
where the time goes in v2:
time: 121 us; the launch traced here: 120 us
  waiting for transfers between devices  44.5 us (37%)
  starting transfers between devices  41.5 us (34%)
  matrix products  12.1 us (10%)
  other arithmetic  10.9 us (9%)
  between operations  5.42 us (4%)
  local copies, waits for them, and re-layouts  5.25 us (4%)
    ppermute x4, waiting for transfers between devices, local(): lax.ppermute(cw_send.astype(jnp.bfloat16), 'head', cw_perm)  24.2 us
    ppermute x3, waiting for transfers between devices, shift_from(): return lax.ppermute(x, axis, [(i, i + step) for i in range(size - step)])  16.5 us
    ppermute x3, starting transfers between devices, local(): lax.ppermute(ccw_send.astype(jnp.bfloat16), 'head', ccw_perm)  15.2 us
    ppermute x3, starting transfers between devices, shift_from(): return lax.ppermute(x, axis, [(i, i + step) for i in range(size - step)])  15 us
    ppermute x4, starting transfers between devices, local(): lax.ppermute(cw_send.astype(jnp.bfloat16), 'head', cw_perm)  9.34 us
    dot_general x1, matrix products, local(): jnp.dot(other_rows, w_out, preferred_element_type=jnp.float32)  4.28 us
    dot_general x1, matrix products, local(): jnp.dot(mine_rows, w_out, preferred_element_type=jnp.float32)  4.19 us
    convert_element_type x3, other arithmetic, local(): cw_send.astype(jnp.bfloat16)  3.8 us
  transfers between devices with their start and end apart: 11, of which 9 were waited for; matrix products, arithmetic and copies ran while one was open for 6% of the time, Pallas kernels for 0%

profile of v2, /device:TPU:14, one launch (start us, length us, event | category | flops | bytes accessed | tf_op | source)
XLA Modules:
  0.0 119.7 jit_solution(12522448965270524744)
XLA Ops:
  0.0 0.0 copy-start
  0.0 0.0 copy-start.2
  0.0 0.8 copy.20
  0.8 0.2 reduce-window.8
  1.0 0.1 reduce
  1.1 0.2 convert_reduce_fusion
  1.3 0.6 fusion.49
  1.9 1.2 %copy.30 = bf16[384,512]{0,1:T(8,128)(2,1)S(1)} copy(bf16[384,512]{1,0:T(8,128)(2,1)} %param.7) | data formatting | bytes 786432 | tf_op jit(solution)/shard_map/reshape | solution.py:31
  3.2 0.7 fusion.42
  5.2 1.3 %broadcast_compare_fusion = (pred[384]{0:T(512)(128)(4,1)S(1)}, f32[384]{0:T(512)S(1)}) fusion(s32[384]{0:T(512)S(1)} %convert_reduce_fusion, s32[]{:T(128)} %bitcast.2, s32[]{:T(128)} %bitcast.3, pred[]{:T(512)S(6)} %and.77), kind=kLoop, calls=%fused_computation.68 | loop fusion | flops 1536 | bytes 3465 | tf_op jit(solution)/shard_map/eq | solution.py:34
  6.6 1.3 %fusion.50 = (bf16[4,128,128]{2,1,0:T(8,128)(2,1)S(1)}, f32[4,128,128]{2,1,0:T(8,128)S(1)}) fusion(bf16[384,4,128]{0,2,1:T(8,128)(2,1)S(1)} %bitcast.84, pred[384]{0:T(512)(128)(4,1)S(1)} %get-tuple-element.19, bf16[384,512]{1,0:T(8,128)(2,1)} %param.8), kind=kOutput, calls=%fused_computation.78 | convolution fusion | flops 50593792 | bytes 1180032 | tf_op jit(solution)/shard_map/thd,the->hde/dot_general | solution.py:36
  7.8 5.2 %collective-permute-start = (bf16[4,128,128]{2,1,0:T(8,128)(2,1)S(1)}, bf16[4,128,128]{2,1,0:T(8,128)(2,1)S(1)}, u32[]{:S(2)}, u32[]{:S(2)}) collective-permute-start(bf16[4,128,128]{2,1,0:T(8,128)(2,1)S(1)} %get-tuple-element.23), channel_id=1, source_target_pairs={{0,16},{16,32},{32,48},{48,64},{64,80},{80,96},{96,112},{112,128},... | collective-permute-start | bytes 393224 | tf_op jit(solution)/shard_map/ppermute | solution.py:10
  13.0 7.9 %collective-permute-start.1 = (bf16[4,128,128]{2,1,0:T(8,128)(2,1)S(1)}, bf16[4,128,128]{2,1,0:T(8,128)(2,1)S(1)}, u32[]{:S(2)}, u32[]{:S(2)}) collective-permute-start(bf16[4,128,128]{2,1,0:T(8,128)(2,1)S(1)} %get-tuple-element.23), channel_id=1, source_target_pairs={{0,32},{16,48},{32,64},{48,80},{64,96},{80,112},{96,128},{112,144}... | collective-permute-start | bytes 393224 | tf_op jit(solution)/shard_map/ppermute | solution.py:10
  22.2 0.1 fusion.12
  22.4 8.3 %collective-permute-done = bf16[4,128,128]{2,1,0:T(8,128)(2,1)S(1)} collective-permute-done((bf16[4,128,128]{2,1,0:T(8,128)(2,1)S(1)}, bf16[4,128,128]{2,1,0:T(8,128)(2,1)S(1)}, u32[]{:S(2)}, u32[]{:S(2)}) %collective-permute-start) | collective-permute-done | bytes 131104 | tf_op jit(solution)/shard_map/ppermute | solution.py:10
  30.7 1.9 %collective-permute-start.2 = (bf16[4,128,128]{2,1,0:T(8,128)(2,1)S(1)}, bf16[4,128,128]{2,1,0:T(8,128)(2,1)S(1)}, u32[]{:S(2)}, u32[]{:S(2)}) collective-permute-start(bf16[4,128,128]{2,1,0:T(8,128)(2,1)S(1)} %fusion.29), channel_id=1, source_target_pairs={{0,48},{16,64},{32,80},{48,96},{64,112},{80,128},{96,144},{112,160... | collective-permute-start | bytes 393224 | tf_op jit(solution)/shard_map/ppermute | solution.py:10
  32.7 0.0 copy-done
  32.7 1.8 %fusion.3 = f32[384,4,128]{0,2,1:T(8,128)S(1)} fusion(bf16[384,4,128]{0,2,1:T(8,128)(2,1)S(1)} %bitcast.85, pred[384,384]{1,0:T(8,128)(4,1)S(1)} %fusion.12, bf16[384,512]{1,0:T(8,128)(2,1)} %param.8, bf16[384,512]{1,0:T(8,128)(2,1)S(1)} %copy-done), kind=kOutput, calls=%fused_computation.8 | convolution fusion | flops 303169536 | bytes 2113536 | tf_op jit(solution)/shard_map/hts,shd->thd/dot_general | solution.py:51
  36.9 0.0 collective-permute-done.1
  36.9 8.2 %collective-permute-done.2 = bf16[4,128,128]{2,1,0:T(8,128)(2,1)S(1)} collective-permute-done((bf16[4,128,128]{2,1,0:T(8,128)(2,1)S(1)}, bf16[4,128,128]{2,1,0:T(8,128)(2,1)S(1)}, u32[]{:S(2)}, u32[]{:S(2)}) %collective-permute-start.2) | collective-permute-done | bytes 131104 | tf_op jit(solution)/shard_map/ppermute | solution.py:10
  45.1 0.6 multiply_reduce_fusion
  45.7 0.0 copy-done.2
  45.7 0.1 multiply_convert_fusion
  45.9 0.2 copy.28
  46.1 0.2 convert_element_type.149
  46.3 4.3 %convolution_convert_fusion = bf16[192,6144]{1,0:T(8,128)(2,1)S(1)} fusion(bf16[192,512]{1,0:T(8,128)(2,1)S(1)} %bitcast.83, bf16[512,6144]{1,0:T(8,128)(2,1)} %param.11), kind=kOutput, calls=%fused_computation | convolution fusion | flops 1209139200 | bytes 8847360 | tf_op jit(solution)/shard_map/dot_general | solution.py:69
  50.6 1.9 %collective-permute-start.3 = (bf16[192,6144]{1,0:T(8,128)(2,1)S(1)}, bf16[192,6144]{1,0:T(8,128)(2,1)}, u32[]{:S(2)}, u32[]{:S(2)}) collective-permute-start(bf16[192,6144]{1,0:T(8,128)(2,1)S(1)} %convolution_convert_fusion), channel_id=1, source_target_pairs={{0,1},{1,0},{2,3},{3,2},{4,5},{5,4},{6,7},{7,6},{8,9},{9,8},{10,11... | collective-permute-start | bytes 7077896 | tf_op jit(solution)/shard_map/ppermute | solution.py:70
  52.6 4.2 %convolution_convert_fusion.1 = bf16[192,6144]{1,0:T(8,128)(2,1)S(1)} fusion(bf16[192,512]{1,0:T(8,128)(2,1)S(1)} %bitcast.82, bf16[512,6144]{1,0:T(8,128)(2,1)} %param.11), kind=kOutput, calls=%fused_computation.1 | convolution fusion | flops 1209139200 | bytes 8847360 | tf_op jit(solution)/shard_map/dot_general | solution.py:72
  56.8 0.4 collective-permute-done.3
  57.2 2.3 %convert_add_fusion = f32[192,6144]{1,0:T(8,128)S(1)} fusion(bf16[192,6144]{1,0:T(8,128)(2,1)} %collective-permute-done.3, bf16[192,6144]{1,0:T(8,128)(2,1)S(1)} %convolution_convert_fusion.1), kind=kLoop, calls=%fused_computation.2 | loop fusion | flops 3538944 | bytes 9437184 | tf_op jit(solution)/shard_map/add | solution.py:74
  59.5 0.0 copy-start.1
  59.5 2.1 %copy-done.1 = f32[192,6144]{1,0:T(8,128)} copy-done((f32[192,6144]{1,0:T(8,128)}, f32[192,6144]{1,0:T(8,128)S(1)}, u32[]{:S(2)}) %copy-start.1) | copy-done | bytes 4718616
  61.6 0.1 fusion.26
  61.7 3.6 %collective-permute-start.4 = (bf16[24,6144]{1,0:T(8,128)(2,1)S(1)}, bf16[24,6144]{1,0:T(8,128)(2,1)S(1)}, u32[]{:S(2)}, u32[]{:S(2)}) collective-permute-start(bf16[24,6144]{1,0:T(8,128)(2,1)S(1)} %get-tuple-element.15), channel_id=1, source_target_pairs={{0,2},{1,3},{2,4},{3,5},{4,6},{5,7},{6,8},{7,9},{8,10},{9,11},{10,... | collective-permute-start | bytes 884744 | tf_op jit(solution)/shard_map/ppermute | solution.py:87
  65.3 4.5 %collective-permute-start.8 = (bf16[24,6144]{1,0:T(8,128)(2,1)S(1)}, bf16[24,6144]{1,0:T(8,128)(2,1)S(1)}, u32[]{:S(2)}, u32[]{:S(2)}) collective-permute-start(bf16[24,6144]{1,0:T(8,128)(2,1)S(1)} %get-tuple-element.16), channel_id=1, source_target_pairs={{0,14},{1,15},{2,0},{3,1},{4,2},{5,3},{6,4},{7,5},{8,6},{9,7},{10,... | collective-permute-start | bytes 884744 | tf_op jit(solution)/shard_map/ppermute | solution.py:89
  69.8 5.3 %collective-permute-done.4 = bf16[24,6144]{1,0:T(8,128)(2,1)S(1)} collective-permute-done((bf16[24,6144]{1,0:T(8,128)(2,1)S(1)}, bf16[24,6144]{1,0:T(8,128)(2,1)S(1)}, u32[]{:S(2)}, u32[]{:S(2)}) %collective-permute-start.4) | collective-permute-done | bytes 294944 | tf_op jit(solution)/shard_map/ppermute | solution.py:87
  75.1 1.1 fusion.11
  76.3 1.9 %collective-permute-start.5 = (bf16[24,6144]{1,0:T(8,128)(2,1)S(1)}, bf16[24,6144]{1,0:T(8,128)(2,1)S(1)}, u32[]{:S(2)}, u32[]{:S(2)}) collective-permute-start(bf16[24,6144]{1,0:T(8,128)(2,1)S(1)} %fusion.11), channel_id=1, source_target_pairs={{0,2},{1,3},{2,4},{3,5},{4,6},{5,7},{6,8},{7,9},{8,10},{9,11},{10,... | collective-permute-start | bytes 884744 | tf_op jit(solution)/shard_map/ppermute | solution.py:87
  78.2 0.0 collective-permute-done.8
  78.2 9.6 %collective-permute-done.5 = bf16[24,6144]{1,0:T(8,128)(2,1)S(1)} collective-permute-done((bf16[24,6144]{1,0:T(8,128)(2,1)S(1)}, bf16[24,6144]{1,0:T(8,128)(2,1)S(1)}, u32[]{:S(2)}, u32[]{:S(2)}) %collective-permute-start.5) | collective-permute-done | bytes 294944 | tf_op jit(solution)/shard_map/ppermute | solution.py:87
  87.8 1.3 %fusion.10 = (bf16[24,6144]{1,0:T(8,128)(2,1)S(1)}, bf16[24,6144]{1,0:T(8,128)(2,1)S(1)}) fusion(f32[8,24,6144]{2,1,0:T(8,128)} %bitcast.79, s32[]{:T(128)S(6)} %select_n.94, bf16[24,6144]{1,0:T(8,128)(2,1)S(1)} %collective-permute-done.5, s32[]{:T(128)S(6)} %select_n.100, bf16[24,6144]{1,0:T(8,128)(2,1)S(1)} %collective-permute-done.8), kind=kLoop, calls=%fused_computation.22 | loop fusion | flops 884736 | bytes 2359304 | tf_op jit(solution)/shard_map/convert_element_type | solution.py:87
  89.2 1.9 %collective-permute-start.6 = (bf16[24,6144]{1,0:T(8,128)(2,1)S(1)}, bf16[24,6144]{1,0:T(8,128)(2,1)S(1)}, u32[]{:S(2)}, u32[]{:S(2)}) collective-permute-start(bf16[24,6144]{1,0:T(8,128)(2,1)S(1)} %get-tuple-element.13), channel_id=1, source_target_pairs={{0,2},{1,3},{2,4},{3,5},{4,6},{5,7},{6,8},{7,9},{8,10},{9,11},{10,... | collective-permute-start | bytes 884744 | tf_op jit(solution)/shard_map/ppermute | solution.py:87
  91.1 5.1 %collective-permute-start.9 = (bf16[24,6144]{1,0:T(8,128)(2,1)S(1)}, bf16[24,6144]{1,0:T(8,128)(2,1)S(1)}, u32[]{:S(2)}, u32[]{:S(2)}) collective-permute-start(bf16[24,6144]{1,0:T(8,128)(2,1)S(1)} %get-tuple-element.14), channel_id=1, source_target_pairs={{0,14},{1,15},{2,0},{3,1},{4,2},{5,3},{6,4},{7,5},{8,6},{9,7},{10,... | collective-permute-start | bytes 884744 | tf_op jit(solution)/shard_map/ppermute | solution.py:89
  96.3 3.6 %collective-permute-done.6 = bf16[24,6144]{1,0:T(8,128)(2,1)S(1)} collective-permute-done((bf16[24,6144]{1,0:T(8,128)(2,1)S(1)}, bf16[24,6144]{1,0:T(8,128)(2,1)S(1)}, u32[]{:S(2)}, u32[]{:S(2)}) %collective-permute-start.6) | collective-permute-done | bytes 294944 | tf_op jit(solution)/shard_map/ppermute | solution.py:87
  99.9 1.2 collective-permute-done.9
  101.1 1.3 %fusion.9 = (bf16[24,6144]{1,0:T(8,128)(2,1)S(1)}, bf16[24,6144]{1,0:T(8,128)(2,1)S(1)}) fusion(f32[8,24,6144]{2,1,0:T(8,128)} %bitcast.80, s32[]{:T(128)S(6)} %select_n.96, bf16[24,6144]{1,0:T(8,128)(2,1)S(1)} %collective-permute-done.6, s32[]{:T(128)S(6)} %select_n.102, bf16[24,6144]{1,0:T(8,128)(2,1)S(1)} %collective-permute-done.9), kind=kLoop, calls=%fused_computation.20 | loop fusion | flops 884736 | bytes 2359304 | tf_op jit(solution)/shard_map/convert_element_type | solution.py:87
  102.4 5.6 %collective-permute-start.10 = (bf16[24,6144]{1,0:T(8,128)(2,1)S(1)}, bf16[24,6144]{1,0:T(8,128)(2,1)S(1)}, u32[]{:S(2)}, u32[]{:S(2)}) collective-permute-start(bf16[24,6144]{1,0:T(8,128)(2,1)S(1)} %get-tuple-element.12), channel_id=1, source_target_pairs={{0,14},{1,15},{2,0},{3,1},{4,2},{5,3},{6,4},{7,5},{8,6},{9,7},{10,... | collective-permute-start | bytes 884744 | tf_op jit(solution)/shard_map/ppermute | solution.py:89
  108.0 1.9 %collective-permute-start.7 = (bf16[24,6144]{1,0:T(8,128)(2,1)S(1)}, bf16[24,6144]{1,0:T(8,128)(2,1)S(1)}, u32[]{:S(2)}, u32[]{:S(2)}) collective-permute-start(bf16[24,6144]{1,0:T(8,128)(2,1)S(1)} %get-tuple-element.11), channel_id=1, source_target_pairs={{0,2},{1,3},{2,4},{3,5},{4,6},{5,7},{6,8},{7,9},{8,10},{9,11},{10,... | collective-permute-start | bytes 884744 | tf_op jit(solution)/shard_map/ppermute | solution.py:87
  110.0 2.3 %collective-permute-done.10 = bf16[24,6144]{1,0:T(8,128)(2,1)S(1)} collective-permute-done((bf16[24,6144]{1,0:T(8,128)(2,1)S(1)}, bf16[24,6144]{1,0:T(8,128)(2,1)S(1)}, u32[]{:S(2)}, u32[]{:S(2)}) %collective-permute-start.10) | collective-permute-done | bytes 294944 | tf_op jit(solution)/shard_map/ppermute | solution.py:89
  112.3 5.6 %collective-permute-done.7 = bf16[24,6144]{1,0:T(8,128)(2,1)S(1)} collective-permute-done((bf16[24,6144]{1,0:T(8,128)(2,1)S(1)}, bf16[24,6144]{1,0:T(8,128)(2,1)S(1)}, u32[]{:S(2)}, u32[]{:S(2)}) %collective-permute-start.7) | collective-permute-done | bytes 294944 | tf_op jit(solution)/shard_map/ppermute | solution.py:87
  117.9 1.9 %fusion.6 = bf16[24,6144]{1,0:T(8,128)(2,1)} fusion(f32[8,24,6144]{2,1,0:T(8,128)} %bitcast.81, s32[]{:T(128)S(6)} %select_n.104, bf16[24,6144]{1,0:T(8,128)(2,1)S(1)} %collective-permute-done.10, bf16[24,6144]{1,0:T(8,128)(2,1)S(1)} %collective-permute-done.7), kind=kLoop, calls=%fused_computation.14 | loop fusion | flops 737280 | bytes 1474564 | tf_op jit(solution)/shard_map/convert_element_type | solution.py:94
  (4 shorter events, 0.1 us)
Async XLA Ops:
  0.0 32.7 %copy-start = (bf16[384,512]{1,0:T(8,128)(2,1)S(1)}, bf16[384,512]{1,0:T(8,128)(2,1)}, u32[]{:S(2)}) copy-start(bf16[384,512]{1,0:T(8,128)(2,1)} %param.6) | copy-start | bytes 1179652
  0.0 45.7 %copy-start.2 = (f32[512]{0:T(512)S(1)}, f32[512]{0:T(512)}, u32[]{:S(2)}) copy-start(f32[512]{0:T(512)} %param.10) | copy-start | bytes 6148
  7.8 22.9 %collective-permute-start = (bf16[4,128,128]{2,1,0:T(8,128)(2,1)S(1)}, bf16[4,128,128]{2,1,0:T(8,128)(2,1)S(1)}, u32[]{:S(2)}, u32[]{:S(2)}) collective-permute-start(bf16[4,128,128]{2,1,0:T(8,128)(2,1)S(1)} %get-tuple-element.23), channel_id=1, source_target_pairs={{0,16},{16,32},{32,48},{48,64},{64,80},{80,96},{96,112},{112,128},... | collective-permute-start | bytes 393224 | tf_op jit(solution)/shard_map/ppermute | solution.py:10
  13.0 23.8 %collective-permute-start.1 = (bf16[4,128,128]{2,1,0:T(8,128)(2,1)S(1)}, bf16[4,128,128]{2,1,0:T(8,128)(2,1)S(1)}, u32[]{:S(2)}, u32[]{:S(2)}) collective-permute-start(bf16[4,128,128]{2,1,0:T(8,128)(2,1)S(1)} %get-tuple-element.23), channel_id=1, source_target_pairs={{0,32},{16,48},{32,64},{48,80},{64,96},{80,112},{96,128},{112,144}... | collective-permute-start | bytes 393224 | tf_op jit(solution)/shard_map/ppermute | solution.py:10
  30.7 14.3 %collective-permute-start.2 = (bf16[4,128,128]{2,1,0:T(8,128)(2,1)S(1)}, bf16[4,128,128]{2,1,0:T(8,128)(2,1)S(1)}, u32[]{:S(2)}, u32[]{:S(2)}) collective-permute-start(bf16[4,128,128]{2,1,0:T(8,128)(2,1)S(1)} %fusion.29), channel_id=1, source_target_pairs={{0,48},{16,64},{32,80},{48,96},{64,112},{80,128},{96,144},{112,160... | collective-permute-start | bytes 393224 | tf_op jit(solution)/shard_map/ppermute | solution.py:10
  50.6 6.6 %collective-permute-start.3 = (bf16[192,6144]{1,0:T(8,128)(2,1)S(1)}, bf16[192,6144]{1,0:T(8,128)(2,1)}, u32[]{:S(2)}, u32[]{:S(2)}) collective-permute-start(bf16[192,6144]{1,0:T(8,128)(2,1)S(1)} %convolution_convert_fusion), channel_id=1, source_target_pairs={{0,1},{1,0},{2,3},{3,2},{4,5},{5,4},{6,7},{7,6},{8,9},{9,8},{10,11... | collective-permute-start | bytes 7077896 | tf_op jit(solution)/shard_map/ppermute | solution.py:70
  59.5 2.1 %copy-start.1 = (f32[192,6144]{1,0:T(8,128)}, f32[192,6144]{1,0:T(8,128)S(1)}, u32[]{:S(2)}) copy-start(f32[192,6144]{1,0:T(8,128)S(1)} %convert_add_fusion) | copy-start | bytes 14155780
  61.7 13.5 %collective-permute-start.4 = (bf16[24,6144]{1,0:T(8,128)(2,1)S(1)}, bf16[24,6144]{1,0:T(8,128)(2,1)S(1)}, u32[]{:S(2)}, u32[]{:S(2)}) collective-permute-start(bf16[24,6144]{1,0:T(8,128)(2,1)S(1)} %get-tuple-element.15), channel_id=1, source_target_pairs={{0,2},{1,3},{2,4},{3,5},{4,6},{5,7},{6,8},{7,9},{8,10},{9,11},{10,... | collective-permute-start | bytes 884744 | tf_op jit(solution)/shard_map/ppermute | solution.py:87
  65.3 12.9 %collective-permute-start.8 = (bf16[24,6144]{1,0:T(8,128)(2,1)S(1)}, bf16[24,6144]{1,0:T(8,128)(2,1)S(1)}, u32[]{:S(2)}, u32[]{:S(2)}) collective-permute-start(bf16[24,6144]{1,0:T(8,128)(2,1)S(1)} %get-tuple-element.16), channel_id=1, source_target_pairs={{0,14},{1,15},{2,0},{3,1},{4,2},{5,3},{6,4},{7,5},{8,6},{9,7},{10,... | collective-permute-start | bytes 884744 | tf_op jit(solution)/shard_map/ppermute | solution.py:89
  76.3 11.6 %collective-permute-start.5 = (bf16[24,6144]{1,0:T(8,128)(2,1)S(1)}, bf16[24,6144]{1,0:T(8,128)(2,1)S(1)}, u32[]{:S(2)}, u32[]{:S(2)}) collective-permute-start(bf16[24,6144]{1,0:T(8,128)(2,1)S(1)} %fusion.11), channel_id=1, source_target_pairs={{0,2},{1,3},{2,4},{3,5},{4,6},{5,7},{6,8},{7,9},{8,10},{9,11},{10,... | collective-permute-start | bytes 884744 | tf_op jit(solution)/shard_map/ppermute | solution.py:87
  89.2 10.7 %collective-permute-start.6 = (bf16[24,6144]{1,0:T(8,128)(2,1)S(1)}, bf16[24,6144]{1,0:T(8,128)(2,1)S(1)}, u32[]{:S(2)}, u32[]{:S(2)}) collective-permute-start(bf16[24,6144]{1,0:T(8,128)(2,1)S(1)} %get-tuple-element.13), channel_id=1, source_target_pairs={{0,2},{1,3},{2,4},{3,5},{4,6},{5,7},{6,8},{7,9},{8,10},{9,11},{10,... | collective-permute-start | bytes 884744 | tf_op jit(solution)/shard_map/ppermute | solution.py:87
  91.1 10.0 %collective-permute-start.9 = (bf16[24,6144]{1,0:T(8,128)(2,1)S(1)}, bf16[24,6144]{1,0:T(8,128)(2,1)S(1)}, u32[]{:S(2)}, u32[]{:S(2)}) collective-permute-start(bf16[24,6144]{1,0:T(8,128)(2,1)S(1)} %get-tuple-element.14), channel_id=1, source_target_pairs={{0,14},{1,15},{2,0},{3,1},{4,2},{5,3},{6,4},{7,5},{8,6},{9,7},{10,... | collective-permute-start | bytes 884744 | tf_op jit(solution)/shard_map/ppermute | solution.py:89
  102.4 9.8 %collective-permute-start.10 = (bf16[24,6144]{1,0:T(8,128)(2,1)S(1)}, bf16[24,6144]{1,0:T(8,128)(2,1)S(1)}, u32[]{:S(2)}, u32[]{:S(2)}) collective-permute-start(bf16[24,6144]{1,0:T(8,128)(2,1)S(1)} %get-tuple-element.12), channel_id=1, source_target_pairs={{0,14},{1,15},{2,0},{3,1},{4,2},{5,3},{6,4},{7,5},{8,6},{9,7},{10,... | collective-permute-start | bytes 884744 | tf_op jit(solution)/shard_map/ppermute | solution.py:89
  108.0 9.8 %collective-permute-start.7 = (bf16[24,6144]{1,0:T(8,128)(2,1)S(1)}, bf16[24,6144]{1,0:T(8,128)(2,1)S(1)}, u32[]{:S(2)}, u32[]{:S(2)}) collective-permute-start(bf16[24,6144]{1,0:T(8,128)(2,1)S(1)} %get-tuple-element.11), channel_id=1, source_target_pairs={{0,2},{1,3},{2,4},{3,5},{4,6},{5,7},{6,8},{7,9},{8,10},{9,11},{10,... | collective-permute-start | bytes 884744 | tf_op jit(solution)/shard_map/ppermute | solution.py:87

commit v3 on v2

--- a/solution.py
+++ b/solution.py
@@ -71,26 +71,35 @@
     mine_part = lax.optimization_barrier(
         jnp.dot(mine_rows, w_out, preferred_element_type=jnp.float32).astype(jnp.bfloat16)
     )
-    acc = (mine_part.astype(jnp.float32) + sibling.astype(jnp.float32)).reshape(n_chip, rows, -1)
+    mine_part = mine_part.reshape(n_chip, rows, -1)
+    sibling = sibling.reshape(n_chip, rows, -1)
+    width = mine_part.shape[2] // 2
 
     cw_perm = [(i, (i + 2) % n_head) for i in range(n_head)]
     ccw_perm = [(i, (i - 2) % n_head) for i in range(n_head)]
 
     def chunk(idx):
-        return lax.dynamic_index_in_dim(acc, idx % n_chip, 0, False)
+        idx = idx % n_chip
+        a = lax.dynamic_index_in_dim(mine_part, idx, 0, False).astype(jnp.float32)
+        return a + lax.dynamic_index_in_dim(sibling, idx, 0, False).astype(jnp.float32)
 
-    cw_steps = n_chip // 2
-    ccw_steps = n_chip - 1 - cw_steps
-    cw_send = chunk(chip + cw_steps)
-    ccw_send = chunk(chip - ccw_steps)
-    for s in range(cw_steps):
-        cw_recv = lax.ppermute(cw_send.astype(jnp.bfloat16), "head", cw_perm).astype(jnp.float32)
-        if s < ccw_steps:
-            ccw_recv = lax.ppermute(ccw_send.astype(jnp.bfloat16), "head", ccw_perm).astype(jnp.float32)
-        if s < cw_steps - 1:
-            cw_send = cw_recv + chunk(chip + cw_steps - 1 - s)
-        if s < ccw_steps - 1:
-            ccw_send = ccw_recv + chunk(chip - ccw_steps + 1 + s)
+    def send(x, perm):
+        return lax.ppermute(x.astype(jnp.bfloat16), "head", perm).astype(jnp.float32)
+
+    half = n_chip // 2
+    cw_recv = send(chunk(chip + half)[:, :width], cw_perm)
+    ccw_recv = send(chunk(chip - half)[:, width:], ccw_perm)
+    for s in range(half - 1):
+        cw_own = chunk(chip + half - 1 - s)
+        ccw_own = chunk(chip - half + 1 + s)
+        if s == 0:
+            cw_own = jnp.concatenate([cw_own[:, :width] + cw_recv, cw_own[:, width:]], axis=1)
+            ccw_own = jnp.concatenate([ccw_own[:, :width], ccw_own[:, width:] + ccw_recv], axis=1)
+        else:
+            cw_own = cw_own + cw_recv
+            ccw_own = ccw_own + ccw_recv
+        cw_recv = send(cw_own, cw_perm)
+        ccw_recv = send(ccw_own, ccw_perm)
     return (cw_recv + ccw_recv + chunk(chip)).astype(jnp.bfloat16)
 
 

time: 121 us -> 123 us (1.017)
  waiting for transfers between devices: 44.5 us -> 39.5 us
  other arithmetic: 10.9 us -> 14.9 us
  starting transfers between devices: 41.5 us -> 43.2 us
    ppermute x7 -> x8, waiting for transfers between devices: 27.6 us -> 21.5 us  [send(): lax.ppermute(x.astype(jnp.bfloat16), 'head', perm).astype(jnp.float32)]
    unnamed x6, local copies, waits for them, and re-layouts: 2.13 us -> 0.01 us
    another operation x2 -> x4, other arithmetic: 0.27 us -> 2.21 us
    slice x0 -> x4, local copies, waits for them, and re-layouts: none -> 1.93 us  [the longest x1 0.98 us: local(): ccw_own[:, :width]]
    convert_element_type x3, other arithmetic: 3.8 us -> 5.73 us  [send(): x.astype(jnp.bfloat16)]
    ppermute x7 -> x8, starting transfers between devices: 24.6 us -> 26.3 us  [send(): lax.ppermute(x.astype(jnp.bfloat16), 'head', perm).astype(jnp.float32)]
    dot_general x1, matrix products: 4.28 us -> 5.68 us  [local(): jnp.dot(other_rows, w_out, preferred_element_type=jnp.float32)]
  transfers between devices with their start and end apart: 11 -> 12, of which waited for: 9 -> 9; matrix products, arithmetic and copies ran while one was open for 6% -> 11% of each run, Pallas kernels for 0% -> 0%
where the time goes in v3:
time: 123 us; the launch traced here: 121 us
  starting transfers between devices  43.2 us (35%)
  waiting for transfers between devices  39.5 us (32%)
  other arithmetic  14.9 us (12%)
  matrix products  12.5 us (10%)
  between operations  5.48 us (4%)
  local copies, waits for them, and re-layouts  5.03 us (4%)
    ppermute x8, starting transfers between devices, send(): lax.ppermute(x.astype(jnp.bfloat16), 'head', perm).astype(jnp.float32)  26.3 us
    ppermute x8, waiting for transfers between devices, send(): lax.ppermute(x.astype(jnp.bfloat16), 'head', perm).astype(jnp.float32)  21.5 us
    ppermute x3, waiting for transfers between devices, shift_from(): return lax.ppermute(x, axis, [(i, i + step) for i in range(size - step)])  17.5 us
    ppermute x3, starting transfers between devices, shift_from(): return lax.ppermute(x, axis, [(i, i + step) for i in range(size - step)])  15 us
    convert_element_type x3, other arithmetic, send(): x.astype(jnp.bfloat16)  5.73 us
    dot_general x1, matrix products, local(): jnp.dot(other_rows, w_out, preferred_element_type=jnp.float32)  5.68 us
    dot_general x1, matrix products, local(): jnp.dot(mine_rows, w_out, preferred_element_type=jnp.float32)  4.19 us
  transfers between devices with their start and end apart: 12, of which 9 were waited for; matrix products, arithmetic and copies ran while one was open for 11% of the time, Pallas kernels for 0%

profile of v3, /device:TPU:14, one launch (start us, length us, event | category | flops | bytes accessed | tf_op | source)
XLA Modules:
  0.0 120.7 jit_solution(3054761121284219373)
XLA Ops:
  0.0 0.0 copy-start
  0.0 0.0 copy-start.2
  0.0 0.8 copy.20
  0.8 0.2 reduce-window.8
  1.0 0.1 reduce
  1.1 0.2 convert_reduce_fusion
  1.4 0.6 fusion.50
  2.0 1.2 copy.30
  3.2 0.7 fusion.43
  5.2 1.3 %broadcast_compare_fusion = (pred[384]{0:T(512)(128)(4,1)S(1)}, f32[384]{0:T(512)S(1)}) fusion(s32[384]{0:T(512)S(1)} %convert_reduce_fusion, s32[]{:T(128)} %bitcast.2, s32[]{:T(128)} %bitcast.3, pred[]{:T(512)S(6)} %and.81), kind=kLoop, calls=%fused_computation.75 | loop fusion | flops 1536 | bytes 3465 | tf_op jit(solution)/shard_map/eq | solution.py:34
  6.6 1.3 %fusion.51 = (bf16[4,128,128]{2,1,0:T(8,128)(2,1)S(1)}, f32[4,128,128]{2,1,0:T(8,128)S(1)}) fusion(bf16[384,4,128]{0,2,1:T(8,128)(2,1)S(1)} %bitcast.85, pred[384]{0:T(512)(128)(4,1)S(1)} %get-tuple-element.19, bf16[384,512]{1,0:T(8,128)(2,1)} %param.8), kind=kOutput, calls=%fused_computation.85 | convolution fusion | flops 50593792 | bytes 1180032 | tf_op jit(solution)/shard_map/thd,the->hde/dot_general | solution.py:36
  7.9 5.2 %collective-permute-start = (bf16[4,128,128]{2,1,0:T(8,128)(2,1)S(1)}, bf16[4,128,128]{2,1,0:T(8,128)(2,1)S(1)}, u32[]{:S(2)}, u32[]{:S(2)}) collective-permute-start(bf16[4,128,128]{2,1,0:T(8,128)(2,1)S(1)} %get-tuple-element.23), channel_id=1, source_target_pairs={{0,16},{16,32},{32,48},{48,64},{64,80},{80,96},{96,112},{112,128},... | collective-permute-start | bytes 393224 | tf_op jit(solution)/shard_map/ppermute | solution.py:10
  13.1 7.9 %collective-permute-start.1 = (bf16[4,128,128]{2,1,0:T(8,128)(2,1)S(1)}, bf16[4,128,128]{2,1,0:T(8,128)(2,1)S(1)}, u32[]{:S(2)}, u32[]{:S(2)}) collective-permute-start(bf16[4,128,128]{2,1,0:T(8,128)(2,1)S(1)} %get-tuple-element.23), channel_id=1, source_target_pairs={{0,32},{16,48},{32,64},{48,80},{64,96},{80,112},{96,128},{112,144}... | collective-permute-start | bytes 393224 | tf_op jit(solution)/shard_map/ppermute | solution.py:10
  22.2 0.1 fusion.11
  22.4 8.3 %collective-permute-done = bf16[4,128,128]{2,1,0:T(8,128)(2,1)S(1)} collective-permute-done((bf16[4,128,128]{2,1,0:T(8,128)(2,1)S(1)}, bf16[4,128,128]{2,1,0:T(8,128)(2,1)S(1)}, u32[]{:S(2)}, u32[]{:S(2)}) %collective-permute-start) | collective-permute-done | bytes 131104 | tf_op jit(solution)/shard_map/ppermute | solution.py:10
  30.8 0.0 copy-start.1
  30.8 1.9 %collective-permute-start.2 = (bf16[4,128,128]{2,1,0:T(8,128)(2,1)S(1)}, bf16[4,128,128]{2,1,0:T(8,128)(2,1)S(1)}, u32[]{:S(2)}, u32[]{:S(2)}) collective-permute-start(bf16[4,128,128]{2,1,0:T(8,128)(2,1)S(1)} %fusion.30), channel_id=1, source_target_pairs={{0,48},{16,64},{32,80},{48,96},{64,112},{80,128},{96,144},{112,160... | collective-permute-start | bytes 393224 | tf_op jit(solution)/shard_map/ppermute | solution.py:10
  32.7 0.0 copy-done
  32.7 0.0 copy-done.2
  32.7 0.8 fusion.3
  35.9 0.8 collective-permute-done.1
  36.7 8.4 %collective-permute-done.2 = bf16[4,128,128]{2,1,0:T(8,128)(2,1)S(1)} collective-permute-done((bf16[4,128,128]{2,1,0:T(8,128)(2,1)S(1)}, bf16[4,128,128]{2,1,0:T(8,128)(2,1)S(1)}, u32[]{:S(2)}, u32[]{:S(2)}) %collective-permute-start.2) | collective-permute-done | bytes 131104 | tf_op jit(solution)/shard_map/ppermute | solution.py:10
  45.1 0.6 multiply_reduce_fusion
  45.7 0.0 copy-done.1
  45.7 0.1 multiply_convert_fusion
  45.9 0.2 copy.28
  46.1 0.2 convert_element_type.207
  46.4 5.7 %convolution_convert_fusion = bf16[192,6144]{1,0:T(8,128)(2,1)} fusion(bf16[192,512]{1,0:T(8,128)(2,1)S(1)} %bitcast.84, bf16[512,6144]{1,0:T(8,128)(2,1)} %param.11), kind=kOutput, calls=%fused_computation | convolution fusion | flops 1209139200 | bytes 8847360 | tf_op jit(solution)/shard_map/dot_general | solution.py:69
  52.0 1.9 %collective-permute-start.3 = (bf16[192,6144]{1,0:T(8,128)(2,1)}, bf16[192,6144]{1,0:T(8,128)(2,1)}, u32[]{:S(2)}, u32[]{:S(2)}) collective-permute-start(bf16[192,6144]{1,0:T(8,128)(2,1)} %convolution_convert_fusion), channel_id=1, source_target_pairs={{0,1},{1,0},{2,3},{3,2},{4,5},{5,4},{6,7},{7,6},{8,9},{9,8},{10,11... | collective-permute-start | bytes 7077896 | tf_op jit(solution)/shard_map/ppermute | solution.py:70
  54.0 4.2 %convolution_convert_fusion.1 = bf16[192,6144]{1,0:T(8,128)(2,1)S(1)} fusion(bf16[192,512]{1,0:T(8,128)(2,1)S(1)} %bitcast.83, bf16[512,6144]{1,0:T(8,128)(2,1)} %param.11), kind=kOutput, calls=%fused_computation.1 | convolution fusion | flops 1209139200 | bytes 8847360 | tf_op jit(solution)/shard_map/dot_general | solution.py:72
  58.2 0.6 collective-permute-done.3
  58.8 2.4 %fusion.25 = (bf16[24,6144]{1,0:T(8,128)(2,1)S(1)}, bf16[24,6144]{1,0:T(8,128)(2,1)}, f32[24,6144]{1,0:T(8,128)}, f32[24,6144]{1,0:T(8,128)S(1)}) fusion(bf16[8,24,6144]{2,1,0:T(8,128)(2,1)} %bitcast.9, s32[]{:T(128)S(6)} %select_n.112, bf16[8,24,6144]{2,1,0:T(8,128)(2,1)S(1)} %bitcast.78, s32[]{:T(128)S(6)} %select_n.120, s32[]{:T(128)S(6)} %select_n.118, ...), kind=kLoop, calls=%fused_computation.41 | loop fusion | flops 2064384 | bytes 4128784 | tf_op jit(solution)/shard_map/add | solution.py:84
  61.2 3.6 %collective-permute-start.4 = (bf16[24,3072]{1,0:T(8,128)(2,1)S(1)}, bf16[24,3072]{1,0:T(8,128)(2,1)}, u32[]{:S(2)}, u32[]{:S(2)}) collective-permute-start(bf16[24,3072]{1,0:T(8,128)(2,1)S(1)} %slice.38), channel_id=1, source_target_pairs={{0,2},{1,3},{2,4},{3,5},{4,6},{5,7},{6,8},{7,9},{8,10},{9,11},{10,... | collective-permute-start | bytes 442376 | tf_op jit(solution)/shard_map/ppermute | solution.py:87
  64.8 0.9 slice.42
  65.8 4.5 %collective-permute-start.8 = (bf16[24,3072]{1,0:T(8,128)(2,1)S(1)}, bf16[24,3072]{1,0:T(8,128)(2,1)S(1)}, u32[]{:S(2)}, u32[]{:S(2)}) collective-permute-start(bf16[24,3072]{1,0:T(8,128)(2,1)S(1)} %slice.42), channel_id=1, source_target_pairs={{0,14},{1,15},{2,0},{3,1},{4,2},{5,3},{6,4},{7,5},{8,6},{9,7},{10,... | collective-permute-start | bytes 442376 | tf_op jit(solution)/shard_map/ppermute | solution.py:87
  70.3 1.0 slice.51
  71.3 0.4 collective-permute-done.4
  71.6 0.9 fusion.28
  72.6 1.9 %collective-permute-start.5 = (bf16[24,6144]{1,0:T(8,128)(2,1)S(1)}, bf16[24,6144]{1,0:T(8,128)(2,1)S(1)}, u32[]{:S(2)}, u32[]{:S(2)}) collective-permute-start(bf16[24,6144]{1,0:T(8,128)(2,1)S(1)} %pad_maximum_fusion), channel_id=1, source_target_pairs={{0,2},{1,3},{2,4},{3,5},{4,6},{5,7},{6,8},{7,9},{8,10},{9,11},{10,... | collective-permute-start | bytes 884744 | tf_op jit(solution)/shard_map/ppermute | solution.py:87
  74.5 0.0 collective-permute-done.8
  74.5 1.0 fusion.27
  75.6 5.1 %collective-permute-start.9 = (bf16[24,6144]{1,0:T(8,128)(2,1)S(1)}, bf16[24,6144]{1,0:T(8,128)(2,1)S(1)}, u32[]{:S(2)}, u32[]{:S(2)}) collective-permute-start(bf16[24,6144]{1,0:T(8,128)(2,1)S(1)} %pad_maximum_fusion.1), channel_id=1, source_target_pairs={{0,14},{1,15},{2,0},{3,1},{4,2},{5,3},{6,4},{7,5},{8,6},{9,7},{10,... | collective-permute-start | bytes 884744 | tf_op jit(solution)/shard_map/ppermute | solution.py:87
  80.7 3.5 %collective-permute-done.5 = bf16[24,6144]{1,0:T(8,128)(2,1)S(1)} collective-permute-done((bf16[24,6144]{1,0:T(8,128)(2,1)S(1)}, bf16[24,6144]{1,0:T(8,128)(2,1)S(1)}, u32[]{:S(2)}, u32[]{:S(2)}) %collective-permute-start.5) | collective-permute-done | bytes 294944 | tf_op jit(solution)/shard_map/ppermute | solution.py:87
  84.2 1.8 %fusion.9 = bf16[24,6144]{1,0:T(8,128)(2,1)} fusion(bf16[24,6144]{1,0:T(8,128)(2,1)S(1)} %collective-permute-done.5, bf16[8,24,6144]{2,1,0:T(8,128)(2,1)} %bitcast.9, s32[]{:T(128)S(6)} %select_n.108, bf16[8,24,6144]{2,1,0:T(8,128)(2,1)S(1)} %bitcast.79), kind=kLoop, calls=%fused_computation.19 | loop fusion | flops 884736 | bytes 1179652 | tf_op jit(solution)/shard_map/convert_element_type | solution.py:87
  86.0 1.9 %collective-permute-start.6 = (bf16[24,6144]{1,0:T(8,128)(2,1)}, bf16[24,6144]{1,0:T(8,128)(2,1)}, u32[]{:S(2)}, u32[]{:S(2)}) collective-permute-start(bf16[24,6144]{1,0:T(8,128)(2,1)} %fusion.9), channel_id=1, source_target_pairs={{0,2},{1,3},{2,4},{3,5},{4,6},{5,7},{6,8},{7,9},{8,10},{9,11},{10,... | collective-permute-start | bytes 884744 | tf_op jit(solution)/shard_map/ppermute | solution.py:87
  87.9 0.0 collective-permute-done.9
  88.0 9.1 %collective-permute-done.6 = bf16[24,6144]{1,0:T(8,128)(2,1)} collective-permute-done((bf16[24,6144]{1,0:T(8,128)(2,1)}, bf16[24,6144]{1,0:T(8,128)(2,1)}, u32[]{:S(2)}, u32[]{:S(2)}) %collective-permute-start.6) | collective-permute-done | bytes 294944 | tf_op jit(solution)/shard_map/ppermute | solution.py:87
  97.0 2.1 %fusion.10 = (bf16[24,6144]{1,0:T(8,128)(2,1)S(1)}, bf16[24,6144]{1,0:T(8,128)(2,1)}) fusion(bf16[24,6144]{1,0:T(8,128)(2,1)} %collective-permute-done.6, bf16[8,24,6144]{2,1,0:T(8,128)(2,1)} %bitcast.9, s32[]{:T(128)S(6)} %select_n.105, bf16[8,24,6144]{2,1,0:T(8,128)(2,1)S(1)} %bitcast.80, bf16[24,6144]{1,0:T(8,128)(2,1)S(1)} %collective-permute-done.9, ...), kind=kLoop, calls=%fused_computation.21 | loop fusion | flops 1769472 | bytes 2359304 | tf_op jit(solution)/shard_map/convert_element_type | solution.py:87
  99.1 1.9 %collective-permute-start.10 = (bf16[24,6144]{1,0:T(8,128)(2,1)}, bf16[24,6144]{1,0:T(8,128)(2,1)}, u32[]{:S(2)}, u32[]{:S(2)}) collective-permute-start(bf16[24,6144]{1,0:T(8,128)(2,1)} %get-tuple-element.12), channel_id=1, source_target_pairs={{0,14},{1,15},{2,0},{3,1},{4,2},{5,3},{6,4},{7,5},{8,6},{9,7},{10,... | collective-permute-start | bytes 884744 | tf_op jit(solution)/shard_map/ppermute | solution.py:87
  101.0 3.9 %collective-permute-start.7 = (bf16[24,6144]{1,0:T(8,128)(2,1)S(1)}, bf16[24,6144]{1,0:T(8,128)(2,1)S(1)}, u32[]{:S(2)}, u32[]{:S(2)}) collective-permute-start(bf16[24,6144]{1,0:T(8,128)(2,1)S(1)} %get-tuple-element.11), channel_id=1, source_target_pairs={{0,2},{1,3},{2,4},{3,5},{4,6},{5,7},{6,8},{7,9},{8,10},{9,11},{10,... | collective-permute-start | bytes 884744 | tf_op jit(solution)/shard_map/ppermute | solution.py:87
  104.9 3.1 %collective-permute-done.10 = bf16[24,6144]{1,0:T(8,128)(2,1)} collective-permute-done((bf16[24,6144]{1,0:T(8,128)(2,1)}, bf16[24,6144]{1,0:T(8,128)(2,1)}, u32[]{:S(2)}, u32[]{:S(2)}) %collective-permute-start.10) | collective-permute-done | bytes 294944 | tf_op jit(solution)/shard_map/ppermute | solution.py:87
  108.0 1.9 %fusion.8 = bf16[24,6144]{1,0:T(8,128)(2,1)} fusion(bf16[24,6144]{1,0:T(8,128)(2,1)} %collective-permute-done.10, bf16[8,24,6144]{2,1,0:T(8,128)(2,1)} %bitcast.9, s32[]{:T(128)S(6)} %select_n.114, bf16[8,24,6144]{2,1,0:T(8,128)(2,1)S(1)} %bitcast.81), kind=kLoop, calls=%fused_computation.17 | loop fusion | flops 884736 | bytes 1179652 | tf_op jit(solution)/shard_map/convert_element_type | solution.py:87
  109.9 3.4 %collective-permute-start.11 = (bf16[24,6144]{1,0:T(8,128)(2,1)}, bf16[24,6144]{1,0:T(8,128)(2,1)}, u32[]{:S(2)}, u32[]{:S(2)}) collective-permute-start(bf16[24,6144]{1,0:T(8,128)(2,1)} %fusion.8), channel_id=1, source_target_pairs={{0,14},{1,15},{2,0},{3,1},{4,2},{5,3},{6,4},{7,5},{8,6},{9,7},{10,... | collective-permute-start | bytes 884744 | tf_op jit(solution)/shard_map/ppermute | solution.py:87
  113.3 0.0 collective-permute-done.7
  113.4 5.5 %collective-permute-done.11 = bf16[24,6144]{1,0:T(8,128)(2,1)} collective-permute-done((bf16[24,6144]{1,0:T(8,128)(2,1)}, bf16[24,6144]{1,0:T(8,128)(2,1)}, u32[]{:S(2)}, u32[]{:S(2)}) %collective-permute-start.11) | collective-permute-done | bytes 294944 | tf_op jit(solution)/shard_map/ppermute | solution.py:87
  118.8 1.9 %fusion.6 = bf16[24,6144]{1,0:T(8,128)(2,1)} fusion(bf16[24,6144]{1,0:T(8,128)(2,1)} %collective-permute-done.11, bf16[24,6144]{1,0:T(8,128)(2,1)S(1)} %collective-permute-done.7, bf16[8,24,6144]{2,1,0:T(8,128)(2,1)} %bitcast.9, s32[]{:T(128)S(6)} %select_n.122, bf16[8,24,6144]{2,1,0:T(8,128)(2,1)S(1)} %bitcast.82), kind=kLoop, calls=%fused_computation.13 | loop fusion | flops 1179648 | bytes 1474564 | tf_op jit(solution)/shard_map/convert_element_type | solution.py:103
  (8 shorter events, 0.2 us)
Async XLA Ops:
  0.0 32.7 %copy-start = (bf16[384,512]{1,0:T(8,128)(2,1)S(1)}, bf16[384,512]{1,0:T(8,128)(2,1)}, u32[]{:S(2)}) copy-start(bf16[384,512]{1,0:T(8,128)(2,1)} %param.6) | copy-start | bytes 1179652
  0.0 32.7 %copy-start.2 = (bf16[384,512]{1,0:T(8,128)(2,1)S(1)}, bf16[384,512]{1,0:T(8,128)(2,1)}, u32[]{:S(2)}) copy-start(bf16[384,512]{1,0:T(8,128)(2,1)} %param.8) | copy-start | bytes 1179652
  7.9 22.9 %collective-permute-start = (bf16[4,128,128]{2,1,0:T(8,128)(2,1)S(1)}, bf16[4,128,128]{2,1,0:T(8,128)(2,1)S(1)}, u32[]{:S(2)}, u32[]{:S(2)}) collective-permute-start(bf16[4,128,128]{2,1,0:T(8,128)(2,1)S(1)} %get-tuple-element.23), channel_id=1, source_target_pairs={{0,16},{16,32},{32,48},{48,64},{64,80},{80,96},{96,112},{112,128},... | collective-permute-start | bytes 393224 | tf_op jit(solution)/shard_map/ppermute | solution.py:10
  13.1 23.6 %collective-permute-start.1 = (bf16[4,128,128]{2,1,0:T(8,128)(2,1)S(1)}, bf16[4,128,128]{2,1,0:T(8,128)(2,1)S(1)}, u32[]{:S(2)}, u32[]{:S(2)}) collective-permute-start(bf16[4,128,128]{2,1,0:T(8,128)(2,1)S(1)} %get-tuple-element.23), channel_id=1, source_target_pairs={{0,32},{16,48},{32,64},{48,80},{64,96},{80,112},{96,128},{112,144}... | collective-permute-start | bytes 393224 | tf_op jit(solution)/shard_map/ppermute | solution.py:10
  30.8 15.0 %copy-start.1 = (f32[512]{0:T(512)S(1)}, f32[512]{0:T(512)}, u32[]{:S(2)}) copy-start(f32[512]{0:T(512)} %param.10) | copy-start | bytes 6148
  30.8 14.3 %collective-permute-start.2 = (bf16[4,128,128]{2,1,0:T(8,128)(2,1)S(1)}, bf16[4,128,128]{2,1,0:T(8,128)(2,1)S(1)}, u32[]{:S(2)}, u32[]{:S(2)}) collective-permute-start(bf16[4,128,128]{2,1,0:T(8,128)(2,1)S(1)} %fusion.30), channel_id=1, source_target_pairs={{0,48},{16,64},{32,80},{48,96},{64,112},{80,128},{96,144},{112,160... | collective-permute-start | bytes 393224 | tf_op jit(solution)/shard_map/ppermute | solution.py:10
  52.0 6.8 %collective-permute-start.3 = (bf16[192,6144]{1,0:T(8,128)(2,1)}, bf16[192,6144]{1,0:T(8,128)(2,1)}, u32[]{:S(2)}, u32[]{:S(2)}) collective-permute-start(bf16[192,6144]{1,0:T(8,128)(2,1)} %convolution_convert_fusion), channel_id=1, source_target_pairs={{0,1},{1,0},{2,3},{3,2},{4,5},{5,4},{6,7},{7,6},{8,9},{9,8},{10,11... | collective-permute-start | bytes 7077896 | tf_op jit(solution)/shard_map/ppermute | solution.py:70
  61.2 10.4 %collective-permute-start.4 = (bf16[24,3072]{1,0:T(8,128)(2,1)S(1)}, bf16[24,3072]{1,0:T(8,128)(2,1)}, u32[]{:S(2)}, u32[]{:S(2)}) collective-permute-start(bf16[24,3072]{1,0:T(8,128)(2,1)S(1)} %slice.38), channel_id=1, source_target_pairs={{0,2},{1,3},{2,4},{3,5},{4,6},{5,7},{6,8},{7,9},{8,10},{9,11},{10,... | collective-permute-start | bytes 442376 | tf_op jit(solution)/shard_map/ppermute | solution.py:87
  65.8 8.8 %collective-permute-start.8 = (bf16[24,3072]{1,0:T(8,128)(2,1)S(1)}, bf16[24,3072]{1,0:T(8,128)(2,1)S(1)}, u32[]{:S(2)}, u32[]{:S(2)}) collective-permute-start(bf16[24,3072]{1,0:T(8,128)(2,1)S(1)} %slice.42), channel_id=1, source_target_pairs={{0,14},{1,15},{2,0},{3,1},{4,2},{5,3},{6,4},{7,5},{8,6},{9,7},{10,... | collective-permute-start | bytes 442376 | tf_op jit(solution)/shard_map/ppermute | solution.py:87
  72.6 11.6 %collective-permute-start.5 = (bf16[24,6144]{1,0:T(8,128)(2,1)S(1)}, bf16[24,6144]{1,0:T(8,128)(2,1)S(1)}, u32[]{:S(2)}, u32[]{:S(2)}) collective-permute-start(bf16[24,6144]{1,0:T(8,128)(2,1)S(1)} %pad_maximum_fusion), channel_id=1, source_target_pairs={{0,2},{1,3},{2,4},{3,5},{4,6},{5,7},{6,8},{7,9},{8,10},{9,11},{10,... | collective-permute-start | bytes 884744 | tf_op jit(solution)/shard_map/ppermute | solution.py:87
  75.6 12.4 %collective-permute-start.9 = (bf16[24,6144]{1,0:T(8,128)(2,1)S(1)}, bf16[24,6144]{1,0:T(8,128)(2,1)S(1)}, u32[]{:S(2)}, u32[]{:S(2)}) collective-permute-start(bf16[24,6144]{1,0:T(8,128)(2,1)S(1)} %pad_maximum_fusion.1), channel_id=1, source_target_pairs={{0,14},{1,15},{2,0},{3,1},{4,2},{5,3},{6,4},{7,5},{8,6},{9,7},{10,... | collective-permute-start | bytes 884744 | tf_op jit(solution)/shard_map/ppermute | solution.py:87
  86.0 11.0 %collective-permute-start.6 = (bf16[24,6144]{1,0:T(8,128)(2,1)}, bf16[24,6144]{1,0:T(8,128)(2,1)}, u32[]{:S(2)}, u32[]{:S(2)}) collective-permute-start(bf16[24,6144]{1,0:T(8,128)(2,1)} %fusion.9), channel_id=1, source_target_pairs={{0,2},{1,3},{2,4},{3,5},{4,6},{5,7},{6,8},{7,9},{8,10},{9,11},{10,... | collective-permute-start | bytes 884744 | tf_op jit(solution)/shard_map/ppermute | solution.py:87
  99.1 9.0 %collective-permute-start.10 = (bf16[24,6144]{1,0:T(8,128)(2,1)}, bf16[24,6144]{1,0:T(8,128)(2,1)}, u32[]{:S(2)}, u32[]{:S(2)}) collective-permute-start(bf16[24,6144]{1,0:T(8,128)(2,1)} %get-tuple-element.12), channel_id=1, source_target_pairs={{0,14},{1,15},{2,0},{3,1},{4,2},{5,3},{6,4},{7,5},{8,6},{9,7},{10,... | collective-permute-start | bytes 884744 | tf_op jit(solution)/shard_map/ppermute | solution.py:87
  101.0 12.3 %collective-permute-start.7 = (bf16[24,6144]{1,0:T(8,128)(2,1)S(1)}, bf16[24,6144]{1,0:T(8,128)(2,1)S(1)}, u32[]{:S(2)}, u32[]{:S(2)}) collective-permute-start(bf16[24,6144]{1,0:T(8,128)(2,1)S(1)} %get-tuple-element.11), channel_id=1, source_target_pairs={{0,2},{1,3},{2,4},{3,5},{4,6},{5,7},{6,8},{7,9},{8,10},{9,11},{10,... | collective-permute-start | bytes 884744 | tf_op jit(solution)/shard_map/ppermute | solution.py:87
  109.9 8.9 %collective-permute-start.11 = (bf16[24,6144]{1,0:T(8,128)(2,1)}, bf16[24,6144]{1,0:T(8,128)(2,1)}, u32[]{:S(2)}, u32[]{:S(2)}) collective-permute-start(bf16[24,6144]{1,0:T(8,128)(2,1)} %fusion.8), channel_id=1, source_target_pairs={{0,14},{1,15},{2,0},{3,1},{4,2},{5,3},{6,4},{7,5},{8,6},{9,7},{10,... | collective-permute-start | bytes 884744 | tf_op jit(solution)/shard_map/ppermute | solution.py:87

commit v4 on v2

--- a/solution.py
+++ b/solution.py
@@ -59,39 +59,77 @@
     hidden = normed.reshape(tok, heads_here * DH).astype(jnp.bfloat16)
 
     n_chip = n_head // 2
-    rows = tok // n_head
+    rows = tok // n_chip
+    half_rows = rows // 2
     me = lax.axis_index("head")
     core = me % 2
     chip = me // 2
-    by_owner = hidden.reshape(n_chip, 2, rows, hidden.shape[1])
-    mine_rows = lax.dynamic_index_in_dim(by_owner, core, 1, False).reshape(n_chip * rows, -1)
-    other_rows = lax.dynamic_index_in_dim(by_owner, 1 - core, 1, False).reshape(n_chip * rows, -1)
-    other_part = jnp.dot(other_rows, w_out, preferred_element_type=jnp.float32).astype(jnp.bfloat16)
-    sibling = lax.ppermute(other_part, "head", [(i, i ^ 1) for i in range(n_head)])
-    mine_part = lax.optimization_barrier(
-        jnp.dot(mine_rows, w_out, preferred_element_type=jnp.float32).astype(jnp.bfloat16)
+    dirn = 1 - 2 * core
+    width = w_out.shape[1] // 2
+    by_chip = hidden.reshape(n_chip, rows, hidden.shape[1])
+
+    def take(a, idx):
+        return lax.dynamic_index_in_dim(a, idx % n_chip, 0, False)
+
+    def halves(a, which):
+        return lax.dynamic_slice_in_dim(a, which * half_rows, half_rows, 0)
+
+    def cols(a, which):
+        return lax.dynamic_slice_in_dim(a, which * width, width, 1)
+
+    far = chip + n_chip // 2
+    steps = n_chip // 2 - 1
+    sib_rows = jnp.concatenate(
+        [take(by_chip, chip - dirn * j) for j in range(1, steps + 1)]
+        + [take(by_chip, far), halves(take(by_chip, chip), 1 - core)],
+        axis=0,
     )
-    acc = (mine_part.astype(jnp.float32) + sibling.astype(jnp.float32)).reshape(n_chip, rows, -1)
+    sib_part = jnp.dot(sib_rows, w_out, preferred_element_type=jnp.float32).astype(jnp.bfloat16)
+    far_part = sib_part[steps * rows:(steps + 1) * rows]
+    to_sib = jnp.concatenate(
+        [
+            sib_part[:steps * rows],
+            cols(far_part, 1 - core).reshape(half_rows, -1),
+            sib_part[(steps + 1) * rows:],
+        ],
+        axis=0,
+    )
+    from_sib = lax.ppermute(to_sib, "head", [(i, i ^ 1) for i in range(n_head)]).astype(jnp.float32)
+    my_rows = jnp.concatenate(
+        [take(by_chip, chip + dirn * j) for j in range(1, steps + 1)]
+        + [halves(take(by_chip, chip), core)],
+        axis=0,
+    )
+    my_part = lax.optimization_barrier(
+        jnp.dot(my_rows, w_out, preferred_element_type=jnp.float32).astype(jnp.bfloat16)
+    ).astype(jnp.float32)
 
-    cw_perm = [(i, (i + 2) % n_head) for i in range(n_head)]
-    ccw_perm = [(i, (i - 2) % n_head) for i in range(n_head)]
+    def near(j):
+        return my_part[(j - 1) * rows:j * rows] + from_sib[(j - 1) * rows:j * rows]
 
-    def chunk(idx):
-        return lax.dynamic_index_in_dim(acc, idx % n_chip, 0, False)
+    far_sum = cols(far_part, core).astype(jnp.float32) + from_sib[
+        steps * rows:steps * rows + half_rows
+    ].reshape(rows, width)
+    own_sum = my_part[steps * rows:] + from_sib[steps * rows + half_rows:]
 
-    cw_steps = n_chip // 2
-    ccw_steps = n_chip - 1 - cw_steps
-    cw_send = chunk(chip + cw_steps)
-    ccw_send = chunk(chip - ccw_steps)
-    for s in range(cw_steps):
-        cw_recv = lax.ppermute(cw_send.astype(jnp.bfloat16), "head", cw_perm).astype(jnp.float32)
-        if s < ccw_steps:
-            ccw_recv = lax.ppermute(ccw_send.astype(jnp.bfloat16), "head", ccw_perm).astype(jnp.float32)
-        if s < cw_steps - 1:
-            cw_send = cw_recv + chunk(chip + cw_steps - 1 - s)
-        if s < ccw_steps - 1:
-            ccw_send = ccw_recv + chunk(chip - ccw_steps + 1 + s)
-    return (cw_recv + ccw_recv + chunk(chip)).astype(jnp.bfloat16)
+    ring = [(i, (i + 2) % n_head) if i % 2 == 0 else (i, (i - 2) % n_head) for i in range(n_head)]
+
+    def send(x, perm):
+        return lax.ppermute(x.astype(jnp.bfloat16), "head", perm).astype(jnp.float32)
+
+    recv = send(far_sum, ring)
+    zeros = jnp.zeros((rows, width), jnp.float32)
+    for j in range(steps, 0, -1):
+        if j == steps:
+            lead = jnp.where(core == 0, jnp.concatenate([recv, zeros], axis=1),
+                             jnp.concatenate([zeros, recv], axis=1))
+            recv = send(near(j) + lead, ring)
+        else:
+            recv = send(near(j) + recv, ring)
+    other = lax.ppermute(
+        halves(recv, 1 - core).astype(jnp.bfloat16), "head", [(i, i ^ 1) for i in range(n_head)]
+    ).astype(jnp.float32)
+    return (halves(recv, core) + other + own_sum).astype(jnp.bfloat16)
 
 
 def solution(mesh):

time: 121 us -> 123 us (1.017)
  waiting for transfers between devices: 44.5 us -> 62.1 us
  starting transfers between devices: 41.5 us -> 28.2 us
  other arithmetic: 10.9 us -> 8.1 us
    ppermute x8 -> x6, waiting for transfers between devices: 28 us -> 41.4 us  [the longest x4 35.3 us: send(): lax.ppermute(x.astype(jnp.bfloat16), 'head', perm).astype(jnp.float32)]
    ppermute x8 -> x6, starting transfers between devices: 26.5 us -> 13.2 us  [the longest x4 9.39 us: send(): lax.ppermute(x.astype(jnp.bfloat16), 'head', perm).astype(jnp.float32)]
    ppermute x3, waiting for transfers between devices: 16.5 us -> 20.6 us  [shift_from(): return lax.ppermute(x, axis, [(i, i + step) for i in range(size - step)])]
    add x1 -> x0, other arithmetic: 2.31 us -> none  [local(): mine_part.astype(jnp.float32) + sibling.astype(jnp.float32)]
    convert_element_type x4 -> x9, other arithmetic: 5.66 us -> 3.62 us  [the longest x4 1.67 us: send(): x.astype(jnp.bfloat16)]
    concatenate x0 -> x1, other arithmetic: none -> 1.57 us  [local(): jnp.concatenate([sib_part[:steps * rows], cols(far_part, 1 - core).reshap...]
    unnamed x6 -> x12, local copies, waits for them, and re-layouts: 2.13 us -> 0.73 us
    reshape x0 -> x2, local copies, waits for them, and re-layouts: none -> 1.27 us  [the longest x1 1.16 us: local(): far_sum = cols(far_part, core).astype(jnp.float32) + from_sib[steps * row...]
  transfers between devices with their start and end apart: 11 -> 9, of which waited for: 9 -> 8; matrix products, arithmetic and copies ran while one was open for 6% -> 5% of each run, Pallas kernels for 0% -> 0%
where the time goes in v4:
time: 123 us; the launch traced here: 121 us
  waiting for transfers between devices  62.1 us (50%)
  starting transfers between devices  28.2 us (23%)
  matrix products  11 us (9%)
  other arithmetic  8.1 us (7%)
  local copies, waits for them, and re-layouts  6.23 us (5%)
  between operations  5.56 us (5%)
    ppermute x4, waiting for transfers between devices, send(): lax.ppermute(x.astype(jnp.bfloat16), 'head', perm).astype(jnp.float32)  35.3 us
    ppermute x3, waiting for transfers between devices, shift_from(): return lax.ppermute(x, axis, [(i, i + step) for i in range(size - step)])  20.6 us
    ppermute x3, starting transfers between devices, shift_from(): return lax.ppermute(x, axis, [(i, i + step) for i in range(size - step)])  15 us
    ppermute x4, starting transfers between devices, send(): lax.ppermute(x.astype(jnp.bfloat16), 'head', perm).astype(jnp.float32)  9.39 us
    ppermute x1, waiting for transfers between devices, local(): lax.ppermute(to_sib, 'head', [(i, i ^ 1) for i in range(n_head)])  4.57 us
    dot_general x1, matrix products, local(): jnp.dot(sib_rows, w_out, preferred_element_type=jnp.float32)  4.34 us
    dot_general x1, matrix products, local(): jnp.dot(my_rows, w_out, preferred_element_type=jnp.float32)  4.03 us
  transfers between devices with their start and end apart: 9, of which 8 were waited for; matrix products, arithmetic and copies ran while one was open for 5% of the time, Pallas kernels for 0%

profile of v4, /device:TPU:14, one launch (start us, length us, event | category | flops | bytes accessed | tf_op | source)
XLA Modules:
  0.0 121.2 jit_solution(11575837978049755302)
XLA Ops:
  0.0 0.0 copy-start
  0.0 0.0 copy-start.3
  0.0 0.8 copy.20
  0.9 0.2 reduce-window.8
  1.0 0.1 reduce
  1.1 0.2 convert_reduce_fusion
  1.4 0.6 fusion.57
  2.0 1.2 copy.30
  3.2 0.7 fusion.49
  5.3 1.3 %broadcast_compare_fusion = (pred[384]{0:T(512)(128)(4,1)S(1)}, f32[384]{0:T(512)S(1)}) fusion(s32[384]{0:T(512)S(1)} %convert_reduce_fusion, s32[]{:T(128)} %bitcast.2, s32[]{:T(128)} %bitcast.3, pred[]{:T(512)S(6)} %and.78), kind=kLoop, calls=%fused_computation.81 | loop fusion | flops 1536 | bytes 3465 | tf_op jit(solution)/shard_map/eq | solution.py:34
  6.6 1.3 %fusion.58 = (bf16[4,128,128]{2,1,0:T(8,128)(2,1)S(1)}, f32[4,128,128]{2,1,0:T(8,128)S(1)}) fusion(bf16[384,4,128]{0,2,1:T(8,128)(2,1)S(1)} %bitcast.63, pred[384]{0:T(512)(128)(4,1)S(1)} %get-tuple-element.14, bf16[384,512]{1,0:T(8,128)(2,1)} %param.8), kind=kOutput, calls=%fused_computation.92 | convolution fusion | flops 50593792 | bytes 1180032 | tf_op jit(solution)/shard_map/thd,the->hde/dot_general | solution.py:36
  7.9 7.9 %collective-permute-start.1 = (bf16[4,128,128]{2,1,0:T(8,128)(2,1)S(1)}, bf16[4,128,128]{2,1,0:T(8,128)(2,1)S(1)}, u32[]{:S(2)}, u32[]{:S(2)}) collective-permute-start(bf16[4,128,128]{2,1,0:T(8,128)(2,1)S(1)} %get-tuple-element.18), channel_id=1, source_target_pairs={{0,32},{16,48},{32,64},{48,80},{64,96},{80,112},{96,128},{112,144}... | collective-permute-start | bytes 393224 | tf_op jit(solution)/shard_map/ppermute | solution.py:10
  15.8 5.2 %collective-permute-start = (bf16[4,128,128]{2,1,0:T(8,128)(2,1)S(1)}, bf16[4,128,128]{2,1,0:T(8,128)(2,1)S(1)}, u32[]{:S(2)}, u32[]{:S(2)}) collective-permute-start(bf16[4,128,128]{2,1,0:T(8,128)(2,1)S(1)} %get-tuple-element.18), channel_id=1, source_target_pairs={{0,16},{16,32},{32,48},{48,64},{64,80},{80,96},{96,112},{112,128},... | collective-permute-start | bytes 393224 | tf_op jit(solution)/shard_map/ppermute | solution.py:10
  22.2 0.1 fusion.14
  22.4 11.8 %collective-permute-done = bf16[4,128,128]{2,1,0:T(8,128)(2,1)S(1)} collective-permute-done((bf16[4,128,128]{2,1,0:T(8,128)(2,1)S(1)}, bf16[4,128,128]{2,1,0:T(8,128)(2,1)S(1)}, u32[]{:S(2)}, u32[]{:S(2)}) %collective-permute-start) | collective-permute-done | bytes 131104 | tf_op jit(solution)/shard_map/ppermute | solution.py:10
  34.3 0.0 copy-start.2
  34.3 1.9 %collective-permute-start.2 = (bf16[4,128,128]{2,1,0:T(8,128)(2,1)S(1)}, bf16[4,128,128]{2,1,0:T(8,128)(2,1)S(1)}, u32[]{:S(2)}, u32[]{:S(2)}) collective-permute-start(bf16[4,128,128]{2,1,0:T(8,128)(2,1)S(1)} %fusion.29), channel_id=1, source_target_pairs={{0,48},{16,64},{32,80},{48,96},{64,112},{80,128},{96,144},{112,160... | collective-permute-start | bytes 393224 | tf_op jit(solution)/shard_map/ppermute | solution.py:10
  36.2 0.0 copy-done
  36.2 0.0 copy-done.3
  36.2 0.8 fusion.3
  39.5 0.0 collective-permute-done.1
  39.5 8.8 %collective-permute-done.2 = bf16[4,128,128]{2,1,0:T(8,128)(2,1)S(1)} collective-permute-done((bf16[4,128,128]{2,1,0:T(8,128)(2,1)S(1)}, bf16[4,128,128]{2,1,0:T(8,128)(2,1)S(1)}, u32[]{:S(2)}, u32[]{:S(2)}) %collective-permute-start.2) | collective-permute-done | bytes 131104 | tf_op jit(solution)/shard_map/ppermute | solution.py:10
  48.3 0.6 multiply_reduce_fusion
  48.9 0.0 copy-done.2
  49.0 0.1 multiply_convert_fusion
  49.1 0.2 copy.28
  49.4 0.2 convert_element_type.134
  49.6 4.3 %convolution_convert_fusion = bf16[216,6144]{1,0:T(8,128)(2,1)S(1)} fusion(bf16[216,512]{1,0:T(8,128)(2,1)S(1)} %bitcast_dynamic-update-slice_fusion.4, bf16[512,6144]{1,0:T(8,128)(2,1)} %param.11), kind=kOutput, calls=%fused_computation | convolution fusion | flops 1360281600 | bytes 9166848 | tf_op jit(solution)/shard_map/dot_general | solution.py:87
  54.1 0.0 copy-start.1
  54.1 0.2 slice.58
  54.2 0.7 copy-done.1
  54.9 0.1 reshape.110
  55.0 1.6 %pad_maximum_fusion = bf16[192,6144]{1,0:T(8,128)(2,1)} fusion(bf16[24,6144]{1,0:T(8,128)(2,1)S(1)} %slice.60, bf16[24,6144]{1,0:T(8,128)(2,1)S(1)} %reshape.110, bf16[144,6144]{1,0:T(8,128)(2,1)S(1)} %slice.58), kind=kLoop, calls=%fused_computation.2 | loop fusion | flops 7077888 | bytes 4718592 | tf_op jit(solution)/shard_map/concatenate | solution.py:89
  56.6 1.9 %collective-permute-start.3 = (bf16[192,6144]{1,0:T(8,128)(2,1)}, bf16[192,6144]{1,0:T(8,128)(2,1)S(1)}, u32[]{:S(2)}, u32[]{:S(2)}) collective-permute-start(bf16[192,6144]{1,0:T(8,128)(2,1)} %pad_maximum_fusion), channel_id=1, source_target_pairs={{0,1},{1,0},{2,3},{3,2},{4,5},{5,4},{6,7},{7,6},{8,9},{9,8},{10,11... | collective-permute-start | bytes 7077896 | tf_op jit(solution)/shard_map/ppermute | solution.py:97
  58.7 4.6 %collective-permute-done.3 = bf16[192,6144]{1,0:T(8,128)(2,1)S(1)} collective-permute-done((bf16[192,6144]{1,0:T(8,128)(2,1)}, bf16[192,6144]{1,0:T(8,128)(2,1)S(1)}, u32[]{:S(2)}, u32[]{:S(2)}) %collective-permute-start.3) | collective-permute-done | bytes 2359328 | tf_op jit(solution)/shard_map/ppermute | solution.py:97
  63.2 0.8 slice.66
  64.1 1.2 reshape.111
  65.2 1.0 add_convert_fusion
  66.3 3.6 %collective-permute-start.4 = (bf16[48,3072]{1,0:T(8,128)(2,1)S(1)}, bf16[48,3072]{1,0:T(8,128)(2,1)S(1)}, u32[]{:S(2)}, u32[]{:S(2)}) collective-permute-start(bf16[48,3072]{1,0:T(8,128)(2,1)S(1)} %add_convert_fusion), channel_id=1, source_target_pairs={{0,2},{1,15},{2,4},{3,1},{4,6},{5,3},{6,8},{7,5},{8,10},{9,7},{10,... | collective-permute-start | bytes 884744 | tf_op jit(solution)/shard_map/ppermute | solution.py:118
  69.9 4.0 %convolution_convert_fusion.1 = bf16[168,6144]{1,0:T(8,128)(2,1)S(1)} fusion(bf16[512,6144]{1,0:T(8,128)(2,1)} %param.11, bf16[24,512]{1,0:T(8,128)(2,1)S(1)} %dynamic-slice_bitcast_fusion.3, bf16[48,512]{1,0:T(8,128)(2,1)S(1)} %get-tuple-element.12, bf16[48,512]{1,0:T(8,128)(2,1)S(1)} %get-tuple-element.13, bf16[48,512]{1,0:T(8,128)(2,1)S(1)} %get-tuple-element.11), kind=kOutput, calls=%fused_computation.1 | convolution fusion | flops 1058684928 | bytes 8527872 | tf_op jit(solution)/shard_map/dot_general | solution.py:104
  73.9 0.5 convert_element_type.136
  74.4 0.5 convert_element_type.138
  74.9 2.2 %collective-permute-done.4 = bf16[48,3072]{1,0:T(8,128)(2,1)S(1)} collective-permute-done((bf16[48,3072]{1,0:T(8,128)(2,1)S(1)}, bf16[48,3072]{1,0:T(8,128)(2,1)S(1)}, u32[]{:S(2)}, u32[]{:S(2)}) %collective-permute-start.4) | collective-permute-done | bytes 294944 | tf_op jit(solution)/shard_map/ppermute | solution.py:118
  77.1 0.3 fusion.5
  77.4 1.9 %collective-permute-start.5 = (bf16[48,6144]{1,0:T(8,128)(2,1)S(1)}, bf16[48,6144]{1,0:T(8,128)(2,1)S(1)}, u32[]{:S(2)}, u32[]{:S(2)}) collective-permute-start(bf16[48,6144]{1,0:T(8,128)(2,1)S(1)} %fusion.5), channel_id=1, source_target_pairs={{0,2},{1,15},{2,4},{3,1},{4,6},{5,3},{6,8},{7,5},{8,10},{9,7},{10,... | collective-permute-start | bytes 1769480 | tf_op jit(solution)/shard_map/ppermute | solution.py:118
  79.3 11.1 %collective-permute-done.5 = bf16[48,6144]{1,0:T(8,128)(2,1)S(1)} collective-permute-done((bf16[48,6144]{1,0:T(8,128)(2,1)S(1)}, bf16[48,6144]{1,0:T(8,128)(2,1)S(1)}, u32[]{:S(2)}, u32[]{:S(2)}) %collective-permute-start.5) | collective-permute-done | bytes 589856 | tf_op jit(solution)/shard_map/ppermute | solution.py:118
  90.4 0.2 fusion.7
  90.6 1.9 %collective-permute-start.6 = (bf16[48,6144]{1,0:T(8,128)(2,1)S(1)}, bf16[48,6144]{1,0:T(8,128)(2,1)S(1)}, u32[]{:S(2)}, u32[]{:S(2)}) collective-permute-start(bf16[48,6144]{1,0:T(8,128)(2,1)S(1)} %fusion.7), channel_id=1, source_target_pairs={{0,2},{1,15},{2,4},{3,1},{4,6},{5,3},{6,8},{7,5},{8,10},{9,7},{10,... | collective-permute-start | bytes 1769480 | tf_op jit(solution)/shard_map/ppermute | solution.py:118
  92.5 11.1 %collective-permute-done.6 = bf16[48,6144]{1,0:T(8,128)(2,1)S(1)} collective-permute-done((bf16[48,6144]{1,0:T(8,128)(2,1)S(1)}, bf16[48,6144]{1,0:T(8,128)(2,1)S(1)}, u32[]{:S(2)}, u32[]{:S(2)}) %collective-permute-start.6) | collective-permute-done | bytes 589856 | tf_op jit(solution)/shard_map/ppermute | solution.py:118
  103.6 0.2 fusion.9
  103.8 1.9 %collective-permute-start.7 = (bf16[48,6144]{1,0:T(8,128)(2,1)S(1)}, bf16[48,6144]{1,0:T(8,128)(2,1)S(1)}, u32[]{:S(2)}, u32[]{:S(2)}) collective-permute-start(bf16[48,6144]{1,0:T(8,128)(2,1)S(1)} %fusion.9), channel_id=1, source_target_pairs={{0,2},{1,15},{2,4},{3,1},{4,6},{5,3},{6,8},{7,5},{8,10},{9,7},{10,... | collective-permute-start | bytes 1769480 | tf_op jit(solution)/shard_map/ppermute | solution.py:118
  105.7 11.1 %collective-permute-done.7 = bf16[48,6144]{1,0:T(8,128)(2,1)S(1)} collective-permute-done((bf16[48,6144]{1,0:T(8,128)(2,1)S(1)}, bf16[48,6144]{1,0:T(8,128)(2,1)S(1)}, u32[]{:S(2)}, u32[]{:S(2)}) %collective-permute-start.7) | collective-permute-done | bytes 589856 | tf_op jit(solution)/shard_map/ppermute | solution.py:118
  116.8 0.1 convert_element_type.147
  116.9 1.9 %collective-permute-start.8 = (bf16[24,6144]{1,0:T(8,128)(2,1)S(1)}, bf16[24,6144]{1,0:T(8,128)(2,1)S(1)}, u32[]{:S(2)}, u32[]{:S(2)}) collective-permute-start(bf16[24,6144]{1,0:T(8,128)(2,1)S(1)} %dynamic-slice_convert_fusion), channel_id=1, source_target_pairs={{0,1},{1,0},{2,3},{3,2},{4,5},{5,4},{6,7},{7,6},{8,9},{9,8},{10,11... | collective-permute-start | bytes 884744 | tf_op jit(solution)/shard_map/ppermute | solution.py:129
  118.8 1.5 %collective-permute-done.8 = bf16[24,6144]{1,0:T(8,128)(2,1)S(1)} collective-permute-done((bf16[24,6144]{1,0:T(8,128)(2,1)S(1)}, bf16[24,6144]{1,0:T(8,128)(2,1)S(1)}, u32[]{:S(2)}, u32[]{:S(2)}) %collective-permute-start.8) | collective-permute-done | bytes 294944 | tf_op jit(solution)/shard_map/ppermute | solution.py:129
  120.4 0.9 fusion.13
  (15 shorter events, 0.3 us)
Async XLA Ops:
  0.0 36.2 %copy-start = (bf16[384,512]{1,0:T(8,128)(2,1)S(1)}, bf16[384,512]{1,0:T(8,128)(2,1)}, u32[]{:S(2)}) copy-start(bf16[384,512]{1,0:T(8,128)(2,1)} %param.6) | copy-start | bytes 1179652
  0.0 36.2 %copy-start.3 = (bf16[384,512]{1,0:T(8,128)(2,1)S(1)}, bf16[384,512]{1,0:T(8,128)(2,1)}, u32[]{:S(2)}) copy-start(bf16[384,512]{1,0:T(8,128)(2,1)} %param.8) | copy-start | bytes 1179652
  7.9 31.7 %collective-permute-start.1 = (bf16[4,128,128]{2,1,0:T(8,128)(2,1)S(1)}, bf16[4,128,128]{2,1,0:T(8,128)(2,1)S(1)}, u32[]{:S(2)}, u32[]{:S(2)}) collective-permute-start(bf16[4,128,128]{2,1,0:T(8,128)(2,1)S(1)} %get-tuple-element.18), channel_id=1, source_target_pairs={{0,32},{16,48},{32,64},{48,80},{64,96},{80,112},{96,128},{112,144}... | collective-permute-start | bytes 393224 | tf_op jit(solution)/shard_map/ppermute | solution.py:10
  15.8 18.5 %collective-permute-start = (bf16[4,128,128]{2,1,0:T(8,128)(2,1)S(1)}, bf16[4,128,128]{2,1,0:T(8,128)(2,1)S(1)}, u32[]{:S(2)}, u32[]{:S(2)}) collective-permute-start(bf16[4,128,128]{2,1,0:T(8,128)(2,1)S(1)} %get-tuple-element.18), channel_id=1, source_target_pairs={{0,16},{16,32},{32,48},{48,64},{64,80},{80,96},{96,112},{112,128},... | collective-permute-start | bytes 393224 | tf_op jit(solution)/shard_map/ppermute | solution.py:10
  34.3 14.7 %copy-start.2 = (f32[512]{0:T(512)S(1)}, f32[512]{0:T(512)}, u32[]{:S(2)}) copy-start(f32[512]{0:T(512)} %param.10) | copy-start | bytes 6148
  34.3 14.0 %collective-permute-start.2 = (bf16[4,128,128]{2,1,0:T(8,128)(2,1)S(1)}, bf16[4,128,128]{2,1,0:T(8,128)(2,1)S(1)}, u32[]{:S(2)}, u32[]{:S(2)}) collective-permute-start(bf16[4,128,128]{2,1,0:T(8,128)(2,1)S(1)} %fusion.29), channel_id=1, source_target_pairs={{0,48},{16,64},{32,80},{48,96},{64,112},{80,128},{96,144},{112,160... | collective-permute-start | bytes 393224 | tf_op jit(solution)/shard_map/ppermute | solution.py:10
  54.1 0.8 copy-start.1
  56.6 6.6 %collective-permute-start.3 = (bf16[192,6144]{1,0:T(8,128)(2,1)}, bf16[192,6144]{1,0:T(8,128)(2,1)S(1)}, u32[]{:S(2)}, u32[]{:S(2)}) collective-permute-start(bf16[192,6144]{1,0:T(8,128)(2,1)} %pad_maximum_fusion), channel_id=1, source_target_pairs={{0,1},{1,0},{2,3},{3,2},{4,5},{5,4},{6,7},{7,6},{8,9},{9,8},{10,11... | collective-permute-start | bytes 7077896 | tf_op jit(solution)/shard_map/ppermute | solution.py:97
  66.3 10.8 %collective-permute-start.4 = (bf16[48,3072]{1,0:T(8,128)(2,1)S(1)}, bf16[48,3072]{1,0:T(8,128)(2,1)S(1)}, u32[]{:S(2)}, u32[]{:S(2)}) collective-permute-start(bf16[48,3072]{1,0:T(8,128)(2,1)S(1)} %add_convert_fusion), channel_id=1, source_target_pairs={{0,2},{1,15},{2,4},{3,1},{4,6},{5,3},{6,8},{7,5},{8,10},{9,7},{10,... | collective-permute-start | bytes 884744 | tf_op jit(solution)/shard_map/ppermute | solution.py:118
  77.4 13.0 %collective-permute-start.5 = (bf16[48,6144]{1,0:T(8,128)(2,1)S(1)}, bf16[48,6144]{1,0:T(8,128)(2,1)S(1)}, u32[]{:S(2)}, u32[]{:S(2)}) collective-permute-start(bf16[48,6144]{1,0:T(8,128)(2,1)S(1)} %fusion.5), channel_id=1, source_target_pairs={{0,2},{1,15},{2,4},{3,1},{4,6},{5,3},{6,8},{7,5},{8,10},{9,7},{10,... | collective-permute-start | bytes 1769480 | tf_op jit(solution)/shard_map/ppermute | solution.py:118
  90.6 13.0 %collective-permute-start.6 = (bf16[48,6144]{1,0:T(8,128)(2,1)S(1)}, bf16[48,6144]{1,0:T(8,128)(2,1)S(1)}, u32[]{:S(2)}, u32[]{:S(2)}) collective-permute-start(bf16[48,6144]{1,0:T(8,128)(2,1)S(1)} %fusion.7), channel_id=1, source_target_pairs={{0,2},{1,15},{2,4},{3,1},{4,6},{5,3},{6,8},{7,5},{8,10},{9,7},{10,... | collective-permute-start | bytes 1769480 | tf_op jit(solution)/shard_map/ppermute | solution.py:118
  103.8 13.0 %collective-permute-start.7 = (bf16[48,6144]{1,0:T(8,128)(2,1)S(1)}, bf16[48,6144]{1,0:T(8,128)(2,1)S(1)}, u32[]{:S(2)}, u32[]{:S(2)}) collective-permute-start(bf16[48,6144]{1,0:T(8,128)(2,1)S(1)} %fusion.9), channel_id=1, source_target_pairs={{0,2},{1,15},{2,4},{3,1},{4,6},{5,3},{6,8},{7,5},{8,10},{9,7},{10,... | collective-permute-start | bytes 1769480 | tf_op jit(solution)/shard_map/ppermute | solution.py:118
  116.9 3.5 %collective-permute-start.8 = (bf16[24,6144]{1,0:T(8,128)(2,1)S(1)}, bf16[24,6144]{1,0:T(8,128)(2,1)S(1)}, u32[]{:S(2)}, u32[]{:S(2)}) collective-permute-start(bf16[24,6144]{1,0:T(8,128)(2,1)S(1)} %dynamic-slice_convert_fusion), channel_id=1, source_target_pairs={{0,1},{1,0},{2,3},{3,2},{4,5},{5,4},{6,7},{7,6},{8,9},{9,8},{10,11... | collective-permute-start | bytes 884744 | tf_op jit(solution)/shard_map/ppermute | solution.py:129

commit v5 on v4

--- a/solution.py
+++ b/solution.py
@@ -31,18 +31,19 @@
     k_heads = keys.reshape(tok, heads_here, DH)
     v_heads = values.reshape(tok, heads_here, DH)
 
-    last = doc == doc[-1]
+    last_doc = doc_at(first + tok - 1)
+    last_start = jnp.where(last_doc > 0, ends[jnp.maximum(last_doc - 1, 0)], 0)
+    last = where_now >= last_start
     k_last = jnp.where(last[:, None, None], k_heads, jnp.zeros_like(k_heads))
     own = jnp.einsum("thd,the->hde", k_last, v_heads, preferred_element_type=jnp.float32)
-    wo0 = whole_open(place)
     wo1 = whole_open(place - 1)
     wo2 = whole_open(place - 2)
     own_b = own.astype(jnp.bfloat16)
     r1 = shift_from(own_b, "ctx", n_ctx, 1).astype(jnp.float32)
     r2 = shift_from(own_b, "ctx", n_ctx, 2).astype(jnp.float32)
-    pair = own + wo0 * r1
-    r3 = shift_from(pair.astype(jnp.bfloat16), "ctx", n_ctx, 3).astype(jnp.float32)
-    carried = (r1 + wo1 * (r2 + wo2 * r3)) * continues.astype(jnp.float32)
+    near = r1 + wo1 * r2
+    r3 = shift_from(near.astype(jnp.bfloat16), "ctx", n_ctx, 2).astype(jnp.float32)
+    carried = (near + (wo1 * wo2) * r3) * continues.astype(jnp.float32)
 
     causal = offsets[:, None] >= offsets[None, :]
     allowed = (doc[:, None] == doc[None, :]) & causal
@@ -65,7 +66,6 @@
     core = me % 2
     chip = me // 2
     dirn = 1 - 2 * core
-    width = w_out.shape[1] // 2
     by_chip = hidden.reshape(n_chip, rows, hidden.shape[1])
 
     def take(a, idx):
@@ -73,9 +73,6 @@
 
     def halves(a, which):
         return lax.dynamic_slice_in_dim(a, which * half_rows, half_rows, 0)
-
-    def cols(a, which):
-        return lax.dynamic_slice_in_dim(a, which * width, width, 1)
 
     far = chip + n_chip // 2
     steps = n_chip // 2 - 1
@@ -89,7 +86,7 @@
     to_sib = jnp.concatenate(
         [
             sib_part[:steps * rows],
-            cols(far_part, 1 - core).reshape(half_rows, -1),
+            halves(far_part, 1 - core),
             sib_part[(steps + 1) * rows:],
         ],
         axis=0,
@@ -107,9 +104,9 @@
     def near(j):
         return my_part[(j - 1) * rows:j * rows] + from_sib[(j - 1) * rows:j * rows]
 
-    far_sum = cols(far_part, core).astype(jnp.float32) + from_sib[
+    far_sum = halves(far_part, core).astype(jnp.float32) + from_sib[
         steps * rows:steps * rows + half_rows
-    ].reshape(rows, width)
+    ]
     own_sum = my_part[steps * rows:] + from_sib[steps * rows + half_rows:]
 
     ring = [(i, (i + 2) % n_head) if i % 2 == 0 else (i, (i - 2) % n_head) for i in range(n_head)]
@@ -118,11 +115,11 @@
         return lax.ppermute(x.astype(jnp.bfloat16), "head", perm).astype(jnp.float32)
 
     recv = send(far_sum, ring)
-    zeros = jnp.zeros((rows, width), jnp.float32)
+    zeros = jnp.zeros_like(recv)
     for j in range(steps, 0, -1):
         if j == steps:
-            lead = jnp.where(core == 0, jnp.concatenate([recv, zeros], axis=1),
-                             jnp.concatenate([zeros, recv], axis=1))
+            lead = jnp.where(core == 0, jnp.concatenate([recv, zeros], axis=0),
+                             jnp.concatenate([zeros, recv], axis=0))
             recv = send(near(j) + lead, ring)
         else:
             recv = send(near(j) + recv, ring)

time: 123 us -> 116 us (0.943)
  waiting for transfers between devices: 62.1 us -> 57.4 us
  other arithmetic: 8.1 us -> 6.48 us
    ppermute x3, waiting for transfers between devices: 20.6 us -> 16.9 us  [shift_from(): return lax.ppermute(x, axis, [(i, i + step) for i in range(size - step)])]
    ppermute x1, waiting for transfers between devices: 4.57 us -> 2.98 us  [local(): lax.ppermute(to_sib, 'head', [(i, i ^ 1) for i in range(n_head)])]
    eq x1 -> x0, other arithmetic: 1.34 us -> none  [local(): last = doc == doc[-1]]
  transfers between devices with their start and end apart: 9 -> 9, of which waited for: 8 -> 9; matrix products, arithmetic and copies ran while one was open for 5% -> 7% of each run, Pallas kernels for 0% -> 0%
where the time goes in v5:
time: 116 us; the launch traced here: 115 us
  waiting for transfers between devices  57.4 us (49%)
  starting transfers between devices  28.2 us (24%)
  matrix products  11.1 us (10%)
  other arithmetic  6.48 us (6%)
  between operations  6.31 us (5%)
  local copies, waits for them, and re-layouts  5.46 us (5%)
    ppermute x4, waiting for transfers between devices, send(): lax.ppermute(x.astype(jnp.bfloat16), 'head', perm).astype(jnp.float32)  35.9 us
    ppermute x3, waiting for transfers between devices, shift_from(): return lax.ppermute(x, axis, [(i, i + step) for i in range(size - step)])  16.9 us
    ppermute x3, starting transfers between devices, shift_from(): return lax.ppermute(x, axis, [(i, i + step) for i in range(size - step)])  15 us
    ppermute x4, starting transfers between devices, send(): lax.ppermute(x.astype(jnp.bfloat16), 'head', perm).astype(jnp.float32)  9.35 us
    dot_general x1, matrix products, local(): jnp.dot(sib_rows, w_out, preferred_element_type=jnp.float32)  4.37 us
    dot_general x1, matrix products, local(): jnp.dot(my_rows, w_out, preferred_element_type=jnp.float32)  4.04 us
    ppermute x1, waiting for transfers between devices, local(): lax.ppermute(to_sib, 'head', [(i, i ^ 1) for i in range(n_head)])  2.98 us
  transfers between devices with their start and end apart: 9, of which 9 were waited for; matrix products, arithmetic and copies ran while one was open for 7% of the time, Pallas kernels for 0%

profile of v5, /device:TPU:14, one launch (start us, length us, event | category | flops | bytes accessed | tf_op | source)
XLA Modules:
  0.0 114.9 jit_solution(11358315162199810455)
XLA Ops:
  0.0 0.0 copy-start
  0.0 0.0 copy-start.3
  0.0 0.8 copy.20
  0.8 0.2 reduce-window.4
  1.0 0.1 reduce
  1.1 0.7 fusion.48
  3.2 0.5 constant_dynamic-slice_fusion.1
  4.4 1.2 %copy.30 = bf16[384,512]{0,1:T(8,128)(2,1)S(1)} copy(bf16[384,512]{1,0:T(8,128)(2,1)} %param.7) | data formatting | bytes 786432 | tf_op jit(solution)/shard_map/reshape | solution.py:31
  5.6 1.3 %convolution_convert_fusion.2 = bf16[4,128,128]{2,1,0:T(8,128)(2,1)S(1)} fusion(bf16[384,4,128]{0,2,1:T(8,128)(2,1)S(1)} %bitcast.61, pred[384]{0:T(512)(128)(4,1)S(1)} %broadcast_compare_fusion, bf16[384,512]{1,0:T(8,128)(2,1)} %param.8), kind=kOutput, calls=%fused_computation.20 | convolution fusion | flops 50593792 | bytes 917888 | tf_op jit(solution)/shard_map/thd,the->hde/dot_general | solution.py:38
  6.8 5.2 %collective-permute-start = (bf16[4,128,128]{2,1,0:T(8,128)(2,1)S(1)}, bf16[4,128,128]{2,1,0:T(8,128)(2,1)S(1)}, u32[]{:S(2)}, u32[]{:S(2)}) collective-permute-start(bf16[4,128,128]{2,1,0:T(8,128)(2,1)S(1)} %convolution_convert_fusion.2), channel_id=1, source_target_pairs={{0,16},{16,32},{32,48},{48,64},{64,80},{80,96},{96,112},{112,128},... | collective-permute-start | bytes 393224 | tf_op jit(solution)/shard_map/ppermute | solution.py:10
  12.0 7.9 %collective-permute-start.1 = (bf16[4,128,128]{2,1,0:T(8,128)(2,1)S(1)}, bf16[4,128,128]{2,1,0:T(8,128)(2,1)S(1)}, u32[]{:S(2)}, u32[]{:S(2)}) collective-permute-start(bf16[4,128,128]{2,1,0:T(8,128)(2,1)S(1)} %convolution_convert_fusion.2), channel_id=1, source_target_pairs={{0,32},{16,48},{32,64},{48,80},{64,96},{80,112},{96,128},{112,144}... | collective-permute-start | bytes 393224 | tf_op jit(solution)/shard_map/ppermute | solution.py:10
  19.9 0.2 convert_reduce_fusion
  20.2 0.1 fusion.15
  20.3 0.0 copy-done
  20.3 0.0 copy-done.3
  20.3 0.0 copy-start.2
  20.4 0.8 fusion.3
  21.2 0.5 slice.40
  25.6 4.1 %collective-permute-done = bf16[4,128,128]{2,1,0:T(8,128)(2,1)S(1)} collective-permute-done((bf16[4,128,128]{2,1,0:T(8,128)(2,1)S(1)}, bf16[4,128,128]{2,1,0:T(8,128)(2,1)S(1)}, u32[]{:S(2)}, u32[]{:S(2)}) %collective-permute-start) | collective-permute-done | bytes 131104 | tf_op jit(solution)/shard_map/ppermute | solution.py:10
  29.7 4.4 %collective-permute-done.1 = bf16[4,128,128]{2,1,0:T(8,128)(2,1)S(1)} collective-permute-done((bf16[4,128,128]{2,1,0:T(8,128)(2,1)S(1)}, bf16[4,128,128]{2,1,0:T(8,128)(2,1)S(1)}, u32[]{:S(2)}, u32[]{:S(2)}) %collective-permute-start.1) | collective-permute-done | bytes 131104 | tf_op jit(solution)/shard_map/ppermute | solution.py:10
  34.2 1.9 %collective-permute-start.2 = (bf16[4,128,128]{2,1,0:T(8,128)(2,1)S(1)}, bf16[4,128,128]{2,1,0:T(8,128)(2,1)S(1)}, u32[]{:S(2)}, u32[]{:S(2)}) collective-permute-start(bf16[4,128,128]{2,1,0:T(8,128)(2,1)S(1)} %fusion.32), channel_id=1, source_target_pairs={{0,32},{16,48},{32,64},{48,80},{64,96},{80,112},{96,128},{112,144}... | collective-permute-start | bytes 393224 | tf_op jit(solution)/shard_map/ppermute | solution.py:10
  36.1 0.7 and_convert_fusion
  36.8 8.4 %collective-permute-done.2 = bf16[4,128,128]{2,1,0:T(8,128)(2,1)S(1)} collective-permute-done((bf16[4,128,128]{2,1,0:T(8,128)(2,1)S(1)}, bf16[4,128,128]{2,1,0:T(8,128)(2,1)S(1)}, u32[]{:S(2)}, u32[]{:S(2)}) %collective-permute-start.2) | collective-permute-done | bytes 131104 | tf_op jit(solution)/shard_map/ppermute | solution.py:10
  45.2 0.7 multiply_reduce_fusion
  45.8 0.0 copy-done.2
  45.8 0.1 multiply_convert_fusion
  46.0 0.2 copy.28
  46.3 0.2 convert_element_type.126
  46.4 0.0 copy-start.1
  46.5 4.4 %convolution_convert_fusion = bf16[216,6144]{1,0:T(8,128)(2,1)S(1)} fusion(bf16[216,512]{1,0:T(8,128)(2,1)S(1)} %bitcast_dynamic-update-slice_fusion.4, bf16[512,6144]{1,0:T(8,128)(2,1)} %param.11), kind=kOutput, calls=%fused_computation | convolution fusion | flops 1360281600 | bytes 9166848 | tf_op jit(solution)/shard_map/dot_general | solution.py:84
  50.9 0.0 copy-done.1
  50.9 0.1 slice.54
  51.2 1.6 %pad_maximum_fusion = bf16[192,6144]{1,0:T(8,128)(2,1)} fusion(bf16[24,6144]{1,0:T(8,128)(2,1)S(1)} %slice.56, bf16[24,6144]{1,0:T(8,128)(2,1)S(1)} %constant_dynamic-slice_fusion, bf16[144,6144]{1,0:T(8,128)(2,1)S(1)} %slice.54), kind=kLoop, calls=%fused_computation.2 | loop fusion | flops 7077888 | bytes 4718592 | tf_op jit(solution)/shard_map/concatenate | solution.py:86
  52.8 1.9 %collective-permute-start.3 = (bf16[192,6144]{1,0:T(8,128)(2,1)}, bf16[192,6144]{1,0:T(8,128)(2,1)S(1)}, u32[]{:S(2)}, u32[]{:S(2)}) collective-permute-start(bf16[192,6144]{1,0:T(8,128)(2,1)} %pad_maximum_fusion), channel_id=1, source_target_pairs={{0,1},{1,0},{2,3},{3,2},{4,5},{5,4},{6,7},{7,6},{8,9},{9,8},{10,11... | collective-permute-start | bytes 7077896 | tf_op jit(solution)/shard_map/ppermute | solution.py:94
  54.8 0.8 dynamic-slice_bitcast_fusion.3
  55.6 0.9 dynamic-slice_bitcast_fusion.2
  56.5 3.0 %collective-permute-done.3 = bf16[192,6144]{1,0:T(8,128)(2,1)S(1)} collective-permute-done((bf16[192,6144]{1,0:T(8,128)(2,1)}, bf16[192,6144]{1,0:T(8,128)(2,1)S(1)}, u32[]{:S(2)}, u32[]{:S(2)}) %collective-permute-start.3) | collective-permute-done | bytes 2359328 | tf_op jit(solution)/shard_map/ppermute | solution.py:94
  59.4 0.5 convert_element_type.130
  60.0 0.1 fusion.14
  60.0 3.6 %collective-permute-start.4 = (bf16[24,6144]{1,0:T(8,128)(2,1)S(1)}, bf16[24,6144]{1,0:T(8,128)(2,1)S(1)}, u32[]{:S(2)}, u32[]{:S(2)}) collective-permute-start(bf16[24,6144]{1,0:T(8,128)(2,1)S(1)} %fusion.14), channel_id=1, source_target_pairs={{0,2},{1,15},{2,4},{3,1},{4,6},{5,3},{6,8},{7,5},{8,10},{9,7},{10,... | collective-permute-start | bytes 884744 | tf_op jit(solution)/shard_map/ppermute | solution.py:115
  63.6 4.0 %convolution_convert_fusion.1 = bf16[168,6144]{1,0:T(8,128)(2,1)S(1)} fusion(bf16[512,6144]{1,0:T(8,128)(2,1)} %param.11, bf16[24,512]{1,0:T(8,128)(2,1)S(1)} %dynamic-slice_bitcast_fusion.3, bf16[48,512]{1,0:T(8,128)(2,1)S(1)} %get-tuple-element.12, bf16[48,512]{1,0:T(8,128)(2,1)S(1)} %get-tuple-element.13, bf16[48,512]{1,0:T(8,128)(2,1)S(1)} %get-tuple-element.11), kind=kOutput, calls=%fused_computation.1 | convolution fusion | flops 1058684928 | bytes 8527872 | tf_op jit(solution)/shard_map/dot_general | solution.py:101
  67.7 0.5 convert_element_type.128
  68.1 2.8 %collective-permute-done.4 = bf16[24,6144]{1,0:T(8,128)(2,1)S(1)} collective-permute-done((bf16[24,6144]{1,0:T(8,128)(2,1)S(1)}, bf16[24,6144]{1,0:T(8,128)(2,1)S(1)}, u32[]{:S(2)}, u32[]{:S(2)}) %collective-permute-start.4) | collective-permute-done | bytes 294944 | tf_op jit(solution)/shard_map/ppermute | solution.py:115
  70.9 0.2 fusion.5
  71.1 1.9 %collective-permute-start.5 = (bf16[48,6144]{1,0:T(8,128)(2,1)S(1)}, bf16[48,6144]{1,0:T(8,128)(2,1)S(1)}, u32[]{:S(2)}, u32[]{:S(2)}) collective-permute-start(bf16[48,6144]{1,0:T(8,128)(2,1)S(1)} %fusion.5), channel_id=1, source_target_pairs={{0,2},{1,15},{2,4},{3,1},{4,6},{5,3},{6,8},{7,5},{8,10},{9,7},{10,... | collective-permute-start | bytes 1769480 | tf_op jit(solution)/shard_map/ppermute | solution.py:115
  73.0 11.1 %collective-permute-done.5 = bf16[48,6144]{1,0:T(8,128)(2,1)S(1)} collective-permute-done((bf16[48,6144]{1,0:T(8,128)(2,1)S(1)}, bf16[48,6144]{1,0:T(8,128)(2,1)S(1)}, u32[]{:S(2)}, u32[]{:S(2)}) %collective-permute-start.5) | collective-permute-done | bytes 589856 | tf_op jit(solution)/shard_map/ppermute | solution.py:115
  84.1 0.2 fusion.7
  84.3 1.9 %collective-permute-start.6 = (bf16[48,6144]{1,0:T(8,128)(2,1)S(1)}, bf16[48,6144]{1,0:T(8,128)(2,1)S(1)}, u32[]{:S(2)}, u32[]{:S(2)}) collective-permute-start(bf16[48,6144]{1,0:T(8,128)(2,1)S(1)} %fusion.7), channel_id=1, source_target_pairs={{0,2},{1,15},{2,4},{3,1},{4,6},{5,3},{6,8},{7,5},{8,10},{9,7},{10,... | collective-permute-start | bytes 1769480 | tf_op jit(solution)/shard_map/ppermute | solution.py:115
  86.2 11.1 %collective-permute-done.6 = bf16[48,6144]{1,0:T(8,128)(2,1)S(1)} collective-permute-done((bf16[48,6144]{1,0:T(8,128)(2,1)S(1)}, bf16[48,6144]{1,0:T(8,128)(2,1)S(1)}, u32[]{:S(2)}, u32[]{:S(2)}) %collective-permute-start.6) | collective-permute-done | bytes 589856 | tf_op jit(solution)/shard_map/ppermute | solution.py:115
  97.3 0.2 fusion.9
  97.5 1.9 %collective-permute-start.7 = (bf16[48,6144]{1,0:T(8,128)(2,1)S(1)}, bf16[48,6144]{1,0:T(8,128)(2,1)S(1)}, u32[]{:S(2)}, u32[]{:S(2)}) collective-permute-start(bf16[48,6144]{1,0:T(8,128)(2,1)S(1)} %fusion.9), channel_id=1, source_target_pairs={{0,2},{1,15},{2,4},{3,1},{4,6},{5,3},{6,8},{7,5},{8,10},{9,7},{10,... | collective-permute-start | bytes 1769480 | tf_op jit(solution)/shard_map/ppermute | solution.py:115
  99.4 11.1 %collective-permute-done.7 = bf16[48,6144]{1,0:T(8,128)(2,1)S(1)} collective-permute-done((bf16[48,6144]{1,0:T(8,128)(2,1)S(1)}, bf16[48,6144]{1,0:T(8,128)(2,1)S(1)}, u32[]{:S(2)}, u32[]{:S(2)}) %collective-permute-start.7) | collective-permute-done | bytes 589856 | tf_op jit(solution)/shard_map/ppermute | solution.py:115
  110.5 0.1 convert_element_type.139
  110.6 1.9 %collective-permute-start.8 = (bf16[24,6144]{1,0:T(8,128)(2,1)S(1)}, bf16[24,6144]{1,0:T(8,128)(2,1)S(1)}, u32[]{:S(2)}, u32[]{:S(2)}) collective-permute-start(bf16[24,6144]{1,0:T(8,128)(2,1)S(1)} %dynamic-slice_convert_fusion), channel_id=1, source_target_pairs={{0,1},{1,0},{2,3},{3,2},{4,5},{5,4},{6,7},{7,6},{8,9},{9,8},{10,11... | collective-permute-start | bytes 884744 | tf_op jit(solution)/shard_map/ppermute | solution.py:126
  112.5 1.5 %collective-permute-done.8 = bf16[24,6144]{1,0:T(8,128)(2,1)S(1)} collective-permute-done((bf16[24,6144]{1,0:T(8,128)(2,1)S(1)}, bf16[24,6144]{1,0:T(8,128)(2,1)S(1)}, u32[]{:S(2)}, u32[]{:S(2)}) %collective-permute-start.8) | collective-permute-done | bytes 294944 | tf_op jit(solution)/shard_map/ppermute | solution.py:126
  114.1 0.9 fusion.13
  (14 shorter events, 0.3 us)
Async XLA Ops:
  0.0 20.3 %copy-start = (bf16[384,512]{1,0:T(8,128)(2,1)S(1)}, bf16[384,512]{1,0:T(8,128)(2,1)}, u32[]{:S(2)}) copy-start(bf16[384,512]{1,0:T(8,128)(2,1)} %param.6) | copy-start | bytes 1179652
  0.0 20.3 %copy-start.3 = (bf16[384,512]{1,0:T(8,128)(2,1)S(1)}, bf16[384,512]{1,0:T(8,128)(2,1)}, u32[]{:S(2)}) copy-start(bf16[384,512]{1,0:T(8,128)(2,1)} %param.8) | copy-start | bytes 1179652
  6.8 22.9 %collective-permute-start = (bf16[4,128,128]{2,1,0:T(8,128)(2,1)S(1)}, bf16[4,128,128]{2,1,0:T(8,128)(2,1)S(1)}, u32[]{:S(2)}, u32[]{:S(2)}) collective-permute-start(bf16[4,128,128]{2,1,0:T(8,128)(2,1)S(1)} %convolution_convert_fusion.2), channel_id=1, source_target_pairs={{0,16},{16,32},{32,48},{48,64},{64,80},{80,96},{96,112},{112,128},... | collective-permute-start | bytes 393224 | tf_op jit(solution)/shard_map/ppermute | solution.py:10
  12.0 22.1 %collective-permute-start.1 = (bf16[4,128,128]{2,1,0:T(8,128)(2,1)S(1)}, bf16[4,128,128]{2,1,0:T(8,128)(2,1)S(1)}, u32[]{:S(2)}, u32[]{:S(2)}) collective-permute-start(bf16[4,128,128]{2,1,0:T(8,128)(2,1)S(1)} %convolution_convert_fusion.2), channel_id=1, source_target_pairs={{0,32},{16,48},{32,64},{48,80},{64,96},{80,112},{96,128},{112,144}... | collective-permute-start | bytes 393224 | tf_op jit(solution)/shard_map/ppermute | solution.py:10
  20.3 25.5 %copy-start.2 = (f32[512]{0:T(512)S(1)}, f32[512]{0:T(512)}, u32[]{:S(2)}) copy-start(f32[512]{0:T(512)} %param.10) | copy-start | bytes 6148
  34.2 11.0 %collective-permute-start.2 = (bf16[4,128,128]{2,1,0:T(8,128)(2,1)S(1)}, bf16[4,128,128]{2,1,0:T(8,128)(2,1)S(1)}, u32[]{:S(2)}, u32[]{:S(2)}) collective-permute-start(bf16[4,128,128]{2,1,0:T(8,128)(2,1)S(1)} %fusion.32), channel_id=1, source_target_pairs={{0,32},{16,48},{32,64},{48,80},{64,96},{80,112},{96,128},{112,144}... | collective-permute-start | bytes 393224 | tf_op jit(solution)/shard_map/ppermute | solution.py:10
  46.4 4.5 %copy-start.1 = (bf16[8,48,512]{2,1,0:T(8,128)(2,1)}, bf16[8,48,512]{2,1,0:T(8,128)(2,1)S(1)}, u32[]{:S(2)}) copy-start(bf16[8,48,512]{2,1,0:T(8,128)(2,1)S(1)} %convert_element_type.126) | copy-start | bytes 1179652
  52.8 6.6 %collective-permute-start.3 = (bf16[192,6144]{1,0:T(8,128)(2,1)}, bf16[192,6144]{1,0:T(8,128)(2,1)S(1)}, u32[]{:S(2)}, u32[]{:S(2)}) collective-permute-start(bf16[192,6144]{1,0:T(8,128)(2,1)} %pad_maximum_fusion), channel_id=1, source_target_pairs={{0,1},{1,0},{2,3},{3,2},{4,5},{5,4},{6,7},{7,6},{8,9},{9,8},{10,11... | collective-permute-start | bytes 7077896 | tf_op jit(solution)/shard_map/ppermute | solution.py:94
  60.0 10.9 %collective-permute-start.4 = (bf16[24,6144]{1,0:T(8,128)(2,1)S(1)}, bf16[24,6144]{1,0:T(8,128)(2,1)S(1)}, u32[]{:S(2)}, u32[]{:S(2)}) collective-permute-start(bf16[24,6144]{1,0:T(8,128)(2,1)S(1)} %fusion.14), channel_id=1, source_target_pairs={{0,2},{1,15},{2,4},{3,1},{4,6},{5,3},{6,8},{7,5},{8,10},{9,7},{10,... | collective-permute-start | bytes 884744 | tf_op jit(solution)/shard_map/ppermute | solution.py:115
  71.1 13.0 %collective-permute-start.5 = (bf16[48,6144]{1,0:T(8,128)(2,1)S(1)}, bf16[48,6144]{1,0:T(8,128)(2,1)S(1)}, u32[]{:S(2)}, u32[]{:S(2)}) collective-permute-start(bf16[48,6144]{1,0:T(8,128)(2,1)S(1)} %fusion.5), channel_id=1, source_target_pairs={{0,2},{1,15},{2,4},{3,1},{4,6},{5,3},{6,8},{7,5},{8,10},{9,7},{10,... | collective-permute-start | bytes 1769480 | tf_op jit(solution)/shard_map/ppermute | solution.py:115
  84.3 13.0 %collective-permute-start.6 = (bf16[48,6144]{1,0:T(8,128)(2,1)S(1)}, bf16[48,6144]{1,0:T(8,128)(2,1)S(1)}, u32[]{:S(2)}, u32[]{:S(2)}) collective-permute-start(bf16[48,6144]{1,0:T(8,128)(2,1)S(1)} %fusion.7), channel_id=1, source_target_pairs={{0,2},{1,15},{2,4},{3,1},{4,6},{5,3},{6,8},{7,5},{8,10},{9,7},{10,... | collective-permute-start | bytes 1769480 | tf_op jit(solution)/shard_map/ppermute | solution.py:115
  97.5 13.0 %collective-permute-start.7 = (bf16[48,6144]{1,0:T(8,128)(2,1)S(1)}, bf16[48,6144]{1,0:T(8,128)(2,1)S(1)}, u32[]{:S(2)}, u32[]{:S(2)}) collective-permute-start(bf16[48,6144]{1,0:T(8,128)(2,1)S(1)} %fusion.9), channel_id=1, source_target_pairs={{0,2},{1,15},{2,4},{3,1},{4,6},{5,3},{6,8},{7,5},{8,10},{9,7},{10,... | collective-permute-start | bytes 1769480 | tf_op jit(solution)/shard_map/ppermute | solution.py:115
  110.6 3.5 %collective-permute-start.8 = (bf16[24,6144]{1,0:T(8,128)(2,1)S(1)}, bf16[24,6144]{1,0:T(8,128)(2,1)S(1)}, u32[]{:S(2)}, u32[]{:S(2)}) collective-permute-start(bf16[24,6144]{1,0:T(8,128)(2,1)S(1)} %dynamic-slice_convert_fusion), channel_id=1, source_target_pairs={{0,1},{1,0},{2,3},{3,2},{4,5},{5,4},{6,7},{7,6},{8,9},{9,8},{10,11... | collective-permute-start | bytes 884744 | tf_op jit(solution)/shard_map/ppermute | solution.py:126

commit v6 on v5

--- a/solution.py
+++ b/solution.py
@@ -76,22 +76,17 @@
 
     far = chip + n_chip // 2
     steps = n_chip // 2 - 1
+    pair = [(i, i ^ 1) for i in range(n_head)]
+    far_part = jnp.dot(take(by_chip, far), w_out, preferred_element_type=jnp.float32).astype(jnp.bfloat16)
+    far_sib = lax.ppermute(halves(far_part, 1 - core), "head", pair)
+    far_sum = halves(far_part, core).astype(jnp.float32) + far_sib.astype(jnp.float32)
     sib_rows = jnp.concatenate(
         [take(by_chip, chip - dirn * j) for j in range(1, steps + 1)]
-        + [take(by_chip, far), halves(take(by_chip, chip), 1 - core)],
+        + [halves(take(by_chip, chip), 1 - core)],
         axis=0,
     )
-    sib_part = jnp.dot(sib_rows, w_out, preferred_element_type=jnp.float32).astype(jnp.bfloat16)
-    far_part = sib_part[steps * rows:(steps + 1) * rows]
-    to_sib = jnp.concatenate(
-        [
-            sib_part[:steps * rows],
-            halves(far_part, 1 - core),
-            sib_part[(steps + 1) * rows:],
-        ],
-        axis=0,
-    )
-    from_sib = lax.ppermute(to_sib, "head", [(i, i ^ 1) for i in range(n_head)]).astype(jnp.float32)
+    to_sib = jnp.dot(sib_rows, w_out, preferred_element_type=jnp.float32).astype(jnp.bfloat16)
+    from_sib = lax.ppermute(to_sib, "head", pair).astype(jnp.float32)
     my_rows = jnp.concatenate(
         [take(by_chip, chip + dirn * j) for j in range(1, steps + 1)]
         + [halves(take(by_chip, chip), core)],
@@ -104,10 +99,7 @@
     def near(j):
         return my_part[(j - 1) * rows:j * rows] + from_sib[(j - 1) * rows:j * rows]
 
-    far_sum = halves(far_part, core).astype(jnp.float32) + from_sib[
-        steps * rows:steps * rows + half_rows
-    ]
-    own_sum = my_part[steps * rows:] + from_sib[steps * rows + half_rows:]
+    own_sum = my_part[steps * rows:] + from_sib[steps * rows:]
 
     ring = [(i, (i + 2) % n_head) if i % 2 == 0 else (i, (i - 2) % n_head) for i in range(n_head)]
 
@@ -123,9 +115,7 @@
             recv = send(near(j) + lead, ring)
         else:
             recv = send(near(j) + recv, ring)
-    other = lax.ppermute(
-        halves(recv, 1 - core).astype(jnp.bfloat16), "head", [(i, i ^ 1) for i in range(n_head)]
-    ).astype(jnp.float32)
+    other = lax.ppermute(halves(recv, 1 - core).astype(jnp.bfloat16), "head", pair).astype(jnp.float32)
     return (halves(recv, core) + other + own_sum).astype(jnp.bfloat16)
 
 

time: 116 us -> 116 us (level)
  waiting for transfers between devices: 57.4 us -> 53.9 us
  starting transfers between devices: 28.2 us -> 30.6 us
  matrix products: 11.1 us -> 13.4 us
    dot_general x0 -> x1, matrix products: none -> 4.14 us  [local(): jnp.dot(take(by_chip, far), w_out, preferred_element_type=jnp.float32)]
    ppermute x2 -> x3, waiting for transfers between devices: 4.53 us -> 1.55 us  [the longest x1 1.55 us: local(): lax.ppermute(halves(recv, 1 - core).astype(jnp.bfloat16), 'head', pair)]
    ppermute x2 -> x3, starting transfers between devices: 3.83 us -> 6.22 us  [the longest x1 2.39 us: local(): from_sib = lax.ppermute(to_sib, 'head', pair).astype(jnp.float32)]
    dot_general x1, matrix products: 4.37 us -> 2.59 us  [local(): jnp.dot(sib_rows, w_out, preferred_element_type=jnp.float32)]
    concatenate x1 -> x0, other arithmetic: 1.64 us -> none  [local(): jnp.concatenate([sib_part[:steps * rows], halves(far_part, 1 - core), sib...]
  transfers between devices with their start and end apart: 9 -> 10, of which waited for: 9 -> 8; matrix products, arithmetic and copies ran while one was open for 7% -> 10% of each run, Pallas kernels for 0% -> 0%
where the time goes in v6:
time: 116 us; the launch traced here: 115 us
  waiting for transfers between devices  53.9 us (46%)
  starting transfers between devices  30.6 us (26%)
  matrix products  13.4 us (12%)
  between operations  6.13 us (5%)
  other arithmetic  5.69 us (5%)
  local copies, waits for them, and re-layouts  4.99 us (4%)
    ppermute x4, waiting for transfers between devices, send(): lax.ppermute(x.astype(jnp.bfloat16), 'head', perm).astype(jnp.float32)  35.9 us
    ppermute x3, waiting for transfers between devices, shift_from(): return lax.ppermute(x, axis, [(i, i + step) for i in range(size - step)])  16.5 us
    ppermute x3, starting transfers between devices, shift_from(): return lax.ppermute(x, axis, [(i, i + step) for i in range(size - step)])  15 us
    ppermute x4, starting transfers between devices, send(): lax.ppermute(x.astype(jnp.bfloat16), 'head', perm).astype(jnp.float32)  9.36 us
    dot_general x1, matrix products, local(): jnp.dot(take(by_chip, far), w_out, preferred_element_type=jnp.float32)  4.14 us
    dot_general x1, matrix products, local(): jnp.dot(my_rows, w_out, preferred_element_type=jnp.float32)  4.03 us
    dot_general x1, matrix products, local(): jnp.dot(sib_rows, w_out, preferred_element_type=jnp.float32)  2.59 us
    ppermute x1, starting transfers between devices, local(): from_sib = lax.ppermute(to_sib, 'head', pair).astype(jnp.float32)  2.39 us
  transfers between devices with their start and end apart: 10, of which 8 were waited for; matrix products, arithmetic and copies ran while one was open for 10% of the time, Pallas kernels for 0%

profile of v6, /device:TPU:14, one launch (start us, length us, event | category | flops | bytes accessed | tf_op | source)
XLA Modules:
  0.0 114.8 jit_solution(3471119650336856043)
XLA Ops:
  0.0 0.0 copy-start
  0.0 0.0 copy-start.4
  0.0 0.8 copy.20
  0.8 0.2 reduce-window.4
  1.0 0.1 reduce
  1.1 0.7 fusion.57
  3.2 1.2 %copy.30 = bf16[384,512]{0,1:T(8,128)(2,1)S(1)} copy(bf16[384,512]{1,0:T(8,128)(2,1)} %param.7) | data formatting | bytes 786432 | tf_op jit(solution)/shard_map/reshape | solution.py:31
  4.4 0.5 constant_dynamic-slice_fusion.1
  5.6 1.3 %convolution_convert_fusion.3 = bf16[4,128,128]{2,1,0:T(8,128)(2,1)S(1)} fusion(bf16[384,4,128]{0,2,1:T(8,128)(2,1)S(1)} %bitcast.64, pred[384]{0:T(512)(128)(4,1)S(1)} %broadcast_compare_fusion, bf16[384,512]{1,0:T(8,128)(2,1)} %param.8), kind=kOutput, calls=%fused_computation.20 | convolution fusion | flops 50593792 | bytes 917888 | tf_op jit(solution)/shard_map/thd,the->hde/dot_general | solution.py:38
  6.8 7.9 %collective-permute-start.1 = (bf16[4,128,128]{2,1,0:T(8,128)(2,1)S(1)}, bf16[4,128,128]{2,1,0:T(8,128)(2,1)S(1)}, u32[]{:S(2)}, u32[]{:S(2)}) collective-permute-start(bf16[4,128,128]{2,1,0:T(8,128)(2,1)S(1)} %convolution_convert_fusion.3), channel_id=1, source_target_pairs={{0,32},{16,48},{32,64},{48,80},{64,96},{80,112},{96,128},{112,144}... | collective-permute-start | bytes 393224 | tf_op jit(solution)/shard_map/ppermute | solution.py:10
  14.7 5.2 %collective-permute-start = (bf16[4,128,128]{2,1,0:T(8,128)(2,1)S(1)}, bf16[4,128,128]{2,1,0:T(8,128)(2,1)S(1)}, u32[]{:S(2)}, u32[]{:S(2)}) collective-permute-start(bf16[4,128,128]{2,1,0:T(8,128)(2,1)S(1)} %convolution_convert_fusion.3), channel_id=1, source_target_pairs={{0,16},{16,32},{32,48},{48,64},{64,80},{80,96},{96,112},{112,128},... | collective-permute-start | bytes 393224 | tf_op jit(solution)/shard_map/ppermute | solution.py:10
  20.0 0.2 convert_reduce_fusion
  20.2 0.1 fusion.14
  20.3 0.0 copy-done
  20.3 0.0 copy-done.4
  20.4 0.8 fusion.3
  21.1 0.0 copy-start.3
  21.2 0.5 slice.28
  25.5 3.8 %collective-permute-done.1 = bf16[4,128,128]{2,1,0:T(8,128)(2,1)S(1)} collective-permute-done((bf16[4,128,128]{2,1,0:T(8,128)(2,1)S(1)}, bf16[4,128,128]{2,1,0:T(8,128)(2,1)S(1)}, u32[]{:S(2)}, u32[]{:S(2)}) %collective-permute-start.1) | collective-permute-done | bytes 131104 | tf_op jit(solution)/shard_map/ppermute | solution.py:10
  29.3 3.9 %collective-permute-done = bf16[4,128,128]{2,1,0:T(8,128)(2,1)S(1)} collective-permute-done((bf16[4,128,128]{2,1,0:T(8,128)(2,1)S(1)}, bf16[4,128,128]{2,1,0:T(8,128)(2,1)S(1)}, u32[]{:S(2)}, u32[]{:S(2)}) %collective-permute-start) | collective-permute-done | bytes 131104 | tf_op jit(solution)/shard_map/ppermute | solution.py:10
  33.3 1.9 %collective-permute-start.2 = (bf16[4,128,128]{2,1,0:T(8,128)(2,1)S(1)}, bf16[4,128,128]{2,1,0:T(8,128)(2,1)S(1)}, u32[]{:S(2)}, u32[]{:S(2)}) collective-permute-start(bf16[4,128,128]{2,1,0:T(8,128)(2,1)S(1)} %fusion.31), channel_id=1, source_target_pairs={{0,32},{16,48},{32,64},{48,80},{64,96},{80,112},{96,128},{112,144}... | collective-permute-start | bytes 393224 | tf_op jit(solution)/shard_map/ppermute | solution.py:10
  35.2 0.7 and_convert_fusion
  35.8 8.8 %collective-permute-done.2 = bf16[4,128,128]{2,1,0:T(8,128)(2,1)S(1)} collective-permute-done((bf16[4,128,128]{2,1,0:T(8,128)(2,1)S(1)}, bf16[4,128,128]{2,1,0:T(8,128)(2,1)S(1)}, u32[]{:S(2)}, u32[]{:S(2)}) %collective-permute-start.2) | collective-permute-done | bytes 131104 | tf_op jit(solution)/shard_map/ppermute | solution.py:10
  44.6 0.0 slice-start
  44.6 0.6 multiply_reduce_fusion
  45.3 0.0 copy-done.3
  45.3 0.1 multiply_convert_fusion
  45.4 0.2 copy.28
  45.7 0.2 convert_element_type.132
  45.8 0.0 slice-start.1
  45.9 4.1 %convolution_convert_fusion.2 = bf16[48,6144]{1,0:T(8,128)(2,1)S(1)} fusion(bf16[512,6144]{1,0:T(8,128)(2,1)} %param.11, bf16[8,48,512]{2,1,0:T(8,128)(2,1)S(1)} %convert_element_type.132, s32[]{:T(128)S(6)} %select_n.134), kind=kOutput, calls=%fused_computation.2 | convolution fusion | flops 302284800 | bytes 6930436 | tf_op jit(solution)/shard_map/dot_general | solution.py:80
  50.0 0.7 constant_dynamic-slice_fusion
  50.8 1.9 %collective-permute-start.4 = (bf16[24,6144]{1,0:T(8,128)(2,1)}, bf16[24,6144]{1,0:T(8,128)(2,1)}, u32[]{:S(2)}, u32[]{:S(2)}) collective-permute-start(bf16[24,6144]{1,0:T(8,128)(2,1)} %constant_dynamic-slice_fusion), channel_id=1, source_target_pairs={{0,1},{1,0},{2,3},{3,2},{4,5},{5,4},{6,7},{7,6},{8,9},{9,8},{10,11... | collective-permute-start | bytes 884744 | tf_op jit(solution)/shard_map/ppermute | solution.py:81
  52.7 0.7 dynamic-slice_bitcast_fusion.5
  53.4 0.0 slice-done
  53.4 0.0 slice-done.1
  53.4 0.0 copy-start.1
  53.4 0.0 copy-start.2
  53.4 2.6 %convolution_convert_fusion = bf16[168,6144]{1,0:T(8,128)(2,1)} fusion(bf16[512,6144]{1,0:T(8,128)(2,1)S(1)} %bitcast.63, bf16[24,512]{1,0:T(8,128)(2,1)S(1)} %get-tuple-element.18, bf16[48,512]{1,0:T(8,128)(2,1)S(1)} %get-tuple-element.12, bf16[48,512]{1,0:T(8,128)(2,1)S(1)} %get-tuple-element.13, bf16[48,512]{1,0:T(8,128)(2,1)S(1)} %get-tuple-element.14), kind=kOutput, calls=%fused_computation | convolution fusion | flops 1058684928 | bytes 8527872 | tf_op jit(solution)/shard_map/dot_general | solution.py:88
  56.0 2.4 %collective-permute-start.3 = (bf16[168,6144]{1,0:T(8,128)(2,1)}, bf16[168,6144]{1,0:T(8,128)(2,1)S(1)}, u32[]{:S(2)}, u32[]{:S(2)}) collective-permute-start(bf16[168,6144]{1,0:T(8,128)(2,1)} %convolution_convert_fusion), channel_id=1, source_target_pairs={{0,1},{1,0},{2,3},{3,2},{4,5},{5,4},{6,7},{7,6},{8,9},{9,8},{10,11... | collective-permute-start | bytes 6193160 | tf_op jit(solution)/shard_map/ppermute | solution.py:89
  58.4 0.0 collective-permute-done.4
  58.4 1.0 add_convert_fusion
  59.4 3.6 %collective-permute-start.5 = (bf16[24,6144]{1,0:T(8,128)(2,1)S(1)}, bf16[24,6144]{1,0:T(8,128)(2,1)S(1)}, u32[]{:S(2)}, u32[]{:S(2)}) collective-permute-start(bf16[24,6144]{1,0:T(8,128)(2,1)S(1)} %add_convert_fusion), channel_id=1, source_target_pairs={{0,2},{1,15},{2,4},{3,1},{4,6},{5,3},{6,8},{7,5},{8,10},{9,7},{10,... | collective-permute-start | bytes 884744 | tf_op jit(solution)/shard_map/ppermute | solution.py:107
  63.1 0.0 copy-done.1
  63.1 0.0 copy-done.2
  63.1 4.0 %convolution_convert_fusion.1 = bf16[168,6144]{1,0:T(8,128)(2,1)S(1)} fusion(bf16[512,6144]{1,0:T(8,128)(2,1)} %param.11, bf16[24,512]{1,0:T(8,128)(2,1)S(1)} %get-tuple-element.17, bf16[48,512]{1,0:T(8,128)(2,1)S(1)} %copy-done.1, bf16[48,512]{1,0:T(8,128)(2,1)S(1)} %copy-done.2, bf16[48,512]{1,0:T(8,128)(2,1)S(1)} %get-tuple-element.11), kind=kOutput, calls=%fused_computation.1 | convolution fusion | flops 1058684928 | bytes 8527872 | tf_op jit(solution)/shard_map/dot_general | solution.py:96
  67.1 0.5 convert_element_type.134
  67.6 2.7 %collective-permute-done.5 = bf16[24,6144]{1,0:T(8,128)(2,1)S(1)} collective-permute-done((bf16[24,6144]{1,0:T(8,128)(2,1)S(1)}, bf16[24,6144]{1,0:T(8,128)(2,1)S(1)}, u32[]{:S(2)}, u32[]{:S(2)}) %collective-permute-start.5) | collective-permute-done | bytes 294944 | tf_op jit(solution)/shard_map/ppermute | solution.py:107
  70.4 0.0 collective-permute-done.3
  70.4 0.5 convert_element_type.136
  70.8 0.1 fusion.5
  71.0 1.9 %collective-permute-start.6 = (bf16[48,6144]{1,0:T(8,128)(2,1)S(1)}, bf16[48,6144]{1,0:T(8,128)(2,1)S(1)}, u32[]{:S(2)}, u32[]{:S(2)}) collective-permute-start(bf16[48,6144]{1,0:T(8,128)(2,1)S(1)} %fusion.5), channel_id=1, source_target_pairs={{0,2},{1,15},{2,4},{3,1},{4,6},{5,3},{6,8},{7,5},{8,10},{9,7},{10,... | collective-permute-start | bytes 1769480 | tf_op jit(solution)/shard_map/ppermute | solution.py:107
  72.9 11.1 %collective-permute-done.6 = bf16[48,6144]{1,0:T(8,128)(2,1)S(1)} collective-permute-done((bf16[48,6144]{1,0:T(8,128)(2,1)S(1)}, bf16[48,6144]{1,0:T(8,128)(2,1)S(1)}, u32[]{:S(2)}, u32[]{:S(2)}) %collective-permute-start.6) | collective-permute-done | bytes 589856 | tf_op jit(solution)/shard_map/ppermute | solution.py:107
  84.0 0.2 fusion.7
  84.2 1.9 %collective-permute-start.7 = (bf16[48,6144]{1,0:T(8,128)(2,1)S(1)}, bf16[48,6144]{1,0:T(8,128)(2,1)S(1)}, u32[]{:S(2)}, u32[]{:S(2)}) collective-permute-start(bf16[48,6144]{1,0:T(8,128)(2,1)S(1)} %fusion.7), channel_id=1, source_target_pairs={{0,2},{1,15},{2,4},{3,1},{4,6},{5,3},{6,8},{7,5},{8,10},{9,7},{10,... | collective-permute-start | bytes 1769480 | tf_op jit(solution)/shard_map/ppermute | solution.py:107
  86.1 11.1 %collective-permute-done.7 = bf16[48,6144]{1,0:T(8,128)(2,1)S(1)} collective-permute-done((bf16[48,6144]{1,0:T(8,128)(2,1)S(1)}, bf16[48,6144]{1,0:T(8,128)(2,1)S(1)}, u32[]{:S(2)}, u32[]{:S(2)}) %collective-permute-start.7) | collective-permute-done | bytes 589856 | tf_op jit(solution)/shard_map/ppermute | solution.py:107
  97.1 0.2 fusion.9
  97.3 1.9 %collective-permute-start.8 = (bf16[48,6144]{1,0:T(8,128)(2,1)S(1)}, bf16[48,6144]{1,0:T(8,128)(2,1)S(1)}, u32[]{:S(2)}, u32[]{:S(2)}) collective-permute-start(bf16[48,6144]{1,0:T(8,128)(2,1)S(1)} %fusion.9), channel_id=1, source_target_pairs={{0,2},{1,15},{2,4},{3,1},{4,6},{5,3},{6,8},{7,5},{8,10},{9,7},{10,... | collective-permute-start | bytes 1769480 | tf_op jit(solution)/shard_map/ppermute | solution.py:107
  99.3 11.1 %collective-permute-done.8 = bf16[48,6144]{1,0:T(8,128)(2,1)S(1)} collective-permute-done((bf16[48,6144]{1,0:T(8,128)(2,1)S(1)}, bf16[48,6144]{1,0:T(8,128)(2,1)S(1)}, u32[]{:S(2)}, u32[]{:S(2)}) %collective-permute-start.8) | collective-permute-done | bytes 589856 | tf_op jit(solution)/shard_map/ppermute | solution.py:107
  110.3 0.1 convert_element_type.147
  110.5 1.9 %collective-permute-start.9 = (bf16[24,6144]{1,0:T(8,128)(2,1)S(1)}, bf16[24,6144]{1,0:T(8,128)(2,1)S(1)}, u32[]{:S(2)}, u32[]{:S(2)}) collective-permute-start(bf16[24,6144]{1,0:T(8,128)(2,1)S(1)} %dynamic-slice_convert_fusion), channel_id=1, source_target_pairs={{0,1},{1,0},{2,3},{3,2},{4,5},{5,4},{6,7},{7,6},{8,9},{9,8},{10,11... | collective-permute-start | bytes 884744 | tf_op jit(solution)/shard_map/ppermute | solution.py:118
  112.4 1.5 %collective-permute-done.9 = bf16[24,6144]{1,0:T(8,128)(2,1)S(1)} collective-permute-done((bf16[24,6144]{1,0:T(8,128)(2,1)S(1)}, bf16[24,6144]{1,0:T(8,128)(2,1)S(1)}, u32[]{:S(2)}, u32[]{:S(2)}) %collective-permute-start.9) | collective-permute-done | bytes 294944 | tf_op jit(solution)/shard_map/ppermute | solution.py:118
  113.9 0.9 fusion.13
  (8 shorter events, 0.2 us)
Async XLA Ops:
  0.0 20.3 %copy-start = (bf16[384,512]{1,0:T(8,128)(2,1)S(1)}, bf16[384,512]{1,0:T(8,128)(2,1)}, u32[]{:S(2)}) copy-start(bf16[384,512]{1,0:T(8,128)(2,1)} %param.6) | copy-start | bytes 1179652
  0.0 20.3 %copy-start.4 = (bf16[384,512]{1,0:T(8,128)(2,1)S(1)}, bf16[384,512]{1,0:T(8,128)(2,1)}, u32[]{:S(2)}) copy-start(bf16[384,512]{1,0:T(8,128)(2,1)} %param.8) | copy-start | bytes 1179652
  6.8 22.4 %collective-permute-start.1 = (bf16[4,128,128]{2,1,0:T(8,128)(2,1)S(1)}, bf16[4,128,128]{2,1,0:T(8,128)(2,1)S(1)}, u32[]{:S(2)}, u32[]{:S(2)}) collective-permute-start(bf16[4,128,128]{2,1,0:T(8,128)(2,1)S(1)} %convolution_convert_fusion.3), channel_id=1, source_target_pairs={{0,32},{16,48},{32,64},{48,80},{64,96},{80,112},{96,128},{112,144}... | collective-permute-start | bytes 393224 | tf_op jit(solution)/shard_map/ppermute | solution.py:10
  14.7 18.5 %collective-permute-start = (bf16[4,128,128]{2,1,0:T(8,128)(2,1)S(1)}, bf16[4,128,128]{2,1,0:T(8,128)(2,1)S(1)}, u32[]{:S(2)}, u32[]{:S(2)}) collective-permute-start(bf16[4,128,128]{2,1,0:T(8,128)(2,1)S(1)} %convolution_convert_fusion.3), channel_id=1, source_target_pairs={{0,16},{16,32},{32,48},{48,64},{64,80},{80,96},{96,112},{112,128},... | collective-permute-start | bytes 393224 | tf_op jit(solution)/shard_map/ppermute | solution.py:10
  21.1 24.1 %copy-start.3 = (f32[512]{0:T(512)S(1)}, f32[512]{0:T(512)}, u32[]{:S(2)}) copy-start(f32[512]{0:T(512)} %param.10) | copy-start | bytes 6148
  33.3 11.4 %collective-permute-start.2 = (bf16[4,128,128]{2,1,0:T(8,128)(2,1)S(1)}, bf16[4,128,128]{2,1,0:T(8,128)(2,1)S(1)}, u32[]{:S(2)}, u32[]{:S(2)}) collective-permute-start(bf16[4,128,128]{2,1,0:T(8,128)(2,1)S(1)} %fusion.31), channel_id=1, source_target_pairs={{0,32},{16,48},{32,64},{48,80},{64,96},{80,112},{96,128},{112,144}... | collective-permute-start | bytes 393224 | tf_op jit(solution)/shard_map/ppermute | solution.py:10
  44.6 8.8 %slice-start = ((s8[6291456]{0:T(1024)(128)(4,1)}), s8[2097152]{0:T(1024)(128)(4,1)S(1)}, s32[]{:S(2)}) async-start(s8[6291456]{0:T(1024)(128)(4,1)} %bitcast.62), calls=%async_computation | async-start | bytes 4194304
  45.8 7.5 %slice-start.1 = ((s8[6291456]{0:T(1024)(128)(4,1)}), s8[4194304]{0:T(1024)(128)(4,1)S(1)}, s32[]{:S(2)}) async-start(s8[6291456]{0:T(1024)(128)(4,1)} %bitcast.62), calls=%async_computation.1 | async-start | bytes 8388608
  50.8 7.6 %collective-permute-start.4 = (bf16[24,6144]{1,0:T(8,128)(2,1)}, bf16[24,6144]{1,0:T(8,128)(2,1)}, u32[]{:S(2)}, u32[]{:S(2)}) collective-permute-start(bf16[24,6144]{1,0:T(8,128)(2,1)} %constant_dynamic-slice_fusion), channel_id=1, source_target_pairs={{0,1},{1,0},{2,3},{3,2},{4,5},{5,4},{6,7},{7,6},{8,9},{9,8},{10,11... | collective-permute-start | bytes 884744 | tf_op jit(solution)/shard_map/ppermute | solution.py:81
  53.4 9.7 %copy-start.1 = (bf16[48,512]{1,0:T(8,128)(2,1)S(1)}, bf16[48,512]{1,0:T(8,128)(2,1)}, u32[]{:S(2)}) copy-start(bf16[48,512]{1,0:T(8,128)(2,1)} %get-tuple-element.15) | copy-start | bytes 147460
  53.4 9.7 %copy-start.2 = (bf16[48,512]{1,0:T(8,128)(2,1)S(1)}, bf16[48,512]{1,0:T(8,128)(2,1)}, u32[]{:S(2)}) copy-start(bf16[48,512]{1,0:T(8,128)(2,1)} %get-tuple-element.16) | copy-start | bytes 147460
  56.0 14.4 %collective-permute-start.3 = (bf16[168,6144]{1,0:T(8,128)(2,1)}, bf16[168,6144]{1,0:T(8,128)(2,1)S(1)}, u32[]{:S(2)}, u32[]{:S(2)}) collective-permute-start(bf16[168,6144]{1,0:T(8,128)(2,1)} %convolution_convert_fusion), channel_id=1, source_target_pairs={{0,1},{1,0},{2,3},{3,2},{4,5},{5,4},{6,7},{7,6},{8,9},{9,8},{10,11... | collective-permute-start | bytes 6193160 | tf_op jit(solution)/shard_map/ppermute | solution.py:89
  59.4 10.9 %collective-permute-start.5 = (bf16[24,6144]{1,0:T(8,128)(2,1)S(1)}, bf16[24,6144]{1,0:T(8,128)(2,1)S(1)}, u32[]{:S(2)}, u32[]{:S(2)}) collective-permute-start(bf16[24,6144]{1,0:T(8,128)(2,1)S(1)} %add_convert_fusion), channel_id=1, source_target_pairs={{0,2},{1,15},{2,4},{3,1},{4,6},{5,3},{6,8},{7,5},{8,10},{9,7},{10,... | collective-permute-start | bytes 884744 | tf_op jit(solution)/shard_map/ppermute | solution.py:107
  71.0 13.0 %collective-permute-start.6 = (bf16[48,6144]{1,0:T(8,128)(2,1)S(1)}, bf16[48,6144]{1,0:T(8,128)(2,1)S(1)}, u32[]{:S(2)}, u32[]{:S(2)}) collective-permute-start(bf16[48,6144]{1,0:T(8,128)(2,1)S(1)} %fusion.5), channel_id=1, source_target_pairs={{0,2},{1,15},{2,4},{3,1},{4,6},{5,3},{6,8},{7,5},{8,10},{9,7},{10,... | collective-permute-start | bytes 1769480 | tf_op jit(solution)/shard_map/ppermute | solution.py:107
  84.2 13.0 %collective-permute-start.7 = (bf16[48,6144]{1,0:T(8,128)(2,1)S(1)}, bf16[48,6144]{1,0:T(8,128)(2,1)S(1)}, u32[]{:S(2)}, u32[]{:S(2)}) collective-permute-start(bf16[48,6144]{1,0:T(8,128)(2,1)S(1)} %fusion.7), channel_id=1, source_target_pairs={{0,2},{1,15},{2,4},{3,1},{4,6},{5,3},{6,8},{7,5},{8,10},{9,7},{10,... | collective-permute-start | bytes 1769480 | tf_op jit(solution)/shard_map/ppermute | solution.py:107
  97.3 13.0 %collective-permute-start.8 = (bf16[48,6144]{1,0:T(8,128)(2,1)S(1)}, bf16[48,6144]{1,0:T(8,128)(2,1)S(1)}, u32[]{:S(2)}, u32[]{:S(2)}) collective-permute-start(bf16[48,6144]{1,0:T(8,128)(2,1)S(1)} %fusion.9), channel_id=1, source_target_pairs={{0,2},{1,15},{2,4},{3,1},{4,6},{5,3},{6,8},{7,5},{8,10},{9,7},{10,... | collective-permute-start | bytes 1769480 | tf_op jit(solution)/shard_map/ppermute | solution.py:107
  110.5 3.5 %collective-permute-start.9 = (bf16[24,6144]{1,0:T(8,128)(2,1)S(1)}, bf16[24,6144]{1,0:T(8,128)(2,1)S(1)}, u32[]{:S(2)}, u32[]{:S(2)}) collective-permute-start(bf16[24,6144]{1,0:T(8,128)(2,1)S(1)} %dynamic-slice_convert_fusion), channel_id=1, source_target_pairs={{0,1},{1,0},{2,3},{3,2},{4,5},{5,4},{6,7},{7,6},{8,9},{9,8},{10,11... | collective-permute-start | bytes 884744 | tf_op jit(solution)/shard_map/ppermute | solution.py:118

commit v7 on v6

--- a/solution.py
+++ b/solution.py
@@ -77,7 +77,9 @@
     far = chip + n_chip // 2
     steps = n_chip // 2 - 1
     pair = [(i, i ^ 1) for i in range(n_head)]
-    far_part = jnp.dot(take(by_chip, far), w_out, preferred_element_type=jnp.float32).astype(jnp.bfloat16)
+    far_part = lax.dot_general(
+        w_out, take(by_chip, far), (((0,), (1,)), ((), ())), preferred_element_type=jnp.float32
+    ).astype(jnp.bfloat16).T
     far_sib = lax.ppermute(halves(far_part, 1 - core), "head", pair)
     far_sum = halves(far_part, core).astype(jnp.float32) + far_sib.astype(jnp.float32)
     sib_rows = jnp.concatenate(
@@ -108,15 +110,18 @@
 
     recv = send(far_sum, ring)
     zeros = jnp.zeros_like(recv)
-    for j in range(steps, 0, -1):
+    for j in range(steps, 1, -1):
         if j == steps:
             lead = jnp.where(core == 0, jnp.concatenate([recv, zeros], axis=0),
                              jnp.concatenate([zeros, recv], axis=0))
             recv = send(near(j) + lead, ring)
         else:
             recv = send(near(j) + recv, ring)
-    other = lax.ppermute(halves(recv, 1 - core).astype(jnp.bfloat16), "head", pair).astype(jnp.float32)
-    return (halves(recv, core) + other + own_sum).astype(jnp.bfloat16)
+    last = near(1) + recv
+    cross = [(i, (i + 3) % n_head) if i % 2 == 0 else (i, (i - 3) % n_head) for i in range(n_head)]
+    same = send(halves(last, core), ring)
+    other = send(halves(last, 1 - core), cross)
+    return (same + other + own_sum).astype(jnp.bfloat16)
 
 
 def solution(mesh):

time: 116 us -> 111 us (0.957)
  waiting for transfers between devices: 53.9 us -> 49.2 us
    ppermute x4 -> x5, waiting for transfers between devices: 35.9 us -> 32.8 us  [send(): lax.ppermute(x.astype(jnp.bfloat16), 'head', perm).astype(jnp.float32)]
    ppermute x1 -> x0, starting transfers between devices: 1.92 us -> none  [local(): lax.ppermute(halves(recv, 1 - core).astype(jnp.bfloat16), 'head', pair)]
    ppermute x4 -> x5, starting transfers between devices: 9.36 us -> 11.3 us  [send(): lax.ppermute(x.astype(jnp.bfloat16), 'head', perm).astype(jnp.float32)]
    ppermute x1 -> x0, waiting for transfers between devices: 1.55 us -> none  [local(): lax.ppermute(halves(recv, 1 - core).astype(jnp.bfloat16), 'head', pair)]
where the time goes in v7:
time: 111 us; the launch traced here: 110 us
  waiting for transfers between devices  49.2 us (44%)
  starting transfers between devices  30.6 us (28%)
  matrix products  13.4 us (12%)
  between operations  6.12 us (6%)
  other arithmetic  5.6 us (5%)
  local copies, waits for them, and re-layouts  5 us (5%)
    ppermute x5, waiting for transfers between devices, send(): lax.ppermute(x.astype(jnp.bfloat16), 'head', perm).astype(jnp.float32)  32.8 us
    ppermute x3, waiting for transfers between devices, shift_from(): return lax.ppermute(x, axis, [(i, i + step) for i in range(size - step)])  16.5 us
    ppermute x3, starting transfers between devices, shift_from(): return lax.ppermute(x, axis, [(i, i + step) for i in range(size - step)])  15 us
    ppermute x5, starting transfers between devices, send(): lax.ppermute(x.astype(jnp.bfloat16), 'head', perm).astype(jnp.float32)  11.3 us
    dot_general x1, matrix products, local(): lax.dot_general(w_out, take(by_chip, far), (((0,), (1,)), ((), ())), pref...  4.14 us
    dot_general x1, matrix products, local(): jnp.dot(my_rows, w_out, preferred_element_type=jnp.float32)  4.03 us
    dot_general x1, matrix products, local(): jnp.dot(sib_rows, w_out, preferred_element_type=jnp.float32)  2.59 us
    ppermute x1, starting transfers between devices, local(): from_sib = lax.ppermute(to_sib, 'head', pair).astype(jnp.float32)  2.39 us
  transfers between devices with their start and end apart: 10, of which 8 were waited for; matrix products, arithmetic and copies ran while one was open for 10% of the time, Pallas kernels for 0%

profile of v7, /device:TPU:14, one launch (start us, length us, event | category | flops | bytes accessed | tf_op | source)
XLA Modules:
  0.0 110.0 jit_solution(14754052083365658740)
XLA Ops:
  0.0 0.0 copy-start
  0.0 0.0 copy-start.4
  0.0 0.8 copy.20
  0.8 0.2 reduce-window.4
  1.0 0.1 reduce
  1.1 0.7 fusion.56
  3.2 1.2 %copy.30 = bf16[384,512]{0,1:T(8,128)(2,1)S(1)} copy(bf16[384,512]{1,0:T(8,128)(2,1)} %param.7) | data formatting | bytes 786432 | tf_op jit(solution)/shard_map/reshape | solution.py:31
  4.4 0.5 constant_dynamic-slice_fusion.1
  5.6 1.3 %convolution_convert_fusion.3 = bf16[4,128,128]{2,1,0:T(8,128)(2,1)S(1)} fusion(bf16[384,4,128]{0,2,1:T(8,128)(2,1)S(1)} %bitcast.64, pred[384]{0:T(512)(128)(4,1)S(1)} %broadcast_compare_fusion, bf16[384,512]{1,0:T(8,128)(2,1)} %param.8), kind=kOutput, calls=%fused_computation.19 | convolution fusion | flops 50593792 | bytes 917888 | tf_op jit(solution)/shard_map/thd,the->hde/dot_general | solution.py:38
  6.8 7.9 %collective-permute-start.1 = (bf16[4,128,128]{2,1,0:T(8,128)(2,1)S(1)}, bf16[4,128,128]{2,1,0:T(8,128)(2,1)S(1)}, u32[]{:S(2)}, u32[]{:S(2)}) collective-permute-start(bf16[4,128,128]{2,1,0:T(8,128)(2,1)S(1)} %convolution_convert_fusion.3), channel_id=1, source_target_pairs={{0,32},{16,48},{32,64},{48,80},{64,96},{80,112},{96,128},{112,144}... | collective-permute-start | bytes 393224 | tf_op jit(solution)/shard_map/ppermute | solution.py:10
  14.7 5.2 %collective-permute-start = (bf16[4,128,128]{2,1,0:T(8,128)(2,1)S(1)}, bf16[4,128,128]{2,1,0:T(8,128)(2,1)S(1)}, u32[]{:S(2)}, u32[]{:S(2)}) collective-permute-start(bf16[4,128,128]{2,1,0:T(8,128)(2,1)S(1)} %convolution_convert_fusion.3), channel_id=1, source_target_pairs={{0,16},{16,32},{32,48},{48,64},{64,80},{80,96},{96,112},{112,128},... | collective-permute-start | bytes 393224 | tf_op jit(solution)/shard_map/ppermute | solution.py:10
  20.0 0.2 convert_reduce_fusion
  20.2 0.1 fusion.13
  20.3 0.0 copy-done
  20.3 0.0 copy-done.4
  20.4 0.8 fusion.3
  21.1 0.0 copy-start.3
  21.2 0.5 slice.28
  25.5 3.8 %collective-permute-done.1 = bf16[4,128,128]{2,1,0:T(8,128)(2,1)S(1)} collective-permute-done((bf16[4,128,128]{2,1,0:T(8,128)(2,1)S(1)}, bf16[4,128,128]{2,1,0:T(8,128)(2,1)S(1)}, u32[]{:S(2)}, u32[]{:S(2)}) %collective-permute-start.1) | collective-permute-done | bytes 131104 | tf_op jit(solution)/shard_map/ppermute | solution.py:10
  29.3 3.9 %collective-permute-done = bf16[4,128,128]{2,1,0:T(8,128)(2,1)S(1)} collective-permute-done((bf16[4,128,128]{2,1,0:T(8,128)(2,1)S(1)}, bf16[4,128,128]{2,1,0:T(8,128)(2,1)S(1)}, u32[]{:S(2)}, u32[]{:S(2)}) %collective-permute-start) | collective-permute-done | bytes 131104 | tf_op jit(solution)/shard_map/ppermute | solution.py:10
  33.3 1.9 %collective-permute-start.2 = (bf16[4,128,128]{2,1,0:T(8,128)(2,1)S(1)}, bf16[4,128,128]{2,1,0:T(8,128)(2,1)S(1)}, u32[]{:S(2)}, u32[]{:S(2)}) collective-permute-start(bf16[4,128,128]{2,1,0:T(8,128)(2,1)S(1)} %fusion.30), channel_id=1, source_target_pairs={{0,32},{16,48},{32,64},{48,80},{64,96},{80,112},{96,128},{112,144}... | collective-permute-start | bytes 393224 | tf_op jit(solution)/shard_map/ppermute | solution.py:10
  35.2 0.7 and_convert_fusion
  35.8 8.8 %collective-permute-done.2 = bf16[4,128,128]{2,1,0:T(8,128)(2,1)S(1)} collective-permute-done((bf16[4,128,128]{2,1,0:T(8,128)(2,1)S(1)}, bf16[4,128,128]{2,1,0:T(8,128)(2,1)S(1)}, u32[]{:S(2)}, u32[]{:S(2)}) %collective-permute-start.2) | collective-permute-done | bytes 131104 | tf_op jit(solution)/shard_map/ppermute | solution.py:10
  44.6 0.0 slice-start
  44.6 0.6 multiply_reduce_fusion
  45.3 0.0 copy-done.3
  45.3 0.1 multiply_convert_fusion
  45.4 0.2 copy.28
  45.7 0.2 convert_element_type.135
  45.8 0.0 slice-start.1
  45.9 4.1 %convolution_convert_fusion.2 = bf16[48,6144]{1,0:T(8,128)(2,1)S(1)} fusion(bf16[512,6144]{1,0:T(8,128)(2,1)} %param.11, bf16[8,48,512]{2,1,0:T(8,128)(2,1)S(1)} %convert_element_type.135, s32[]{:T(128)S(6)} %select_n.134), kind=kOutput, calls=%fused_computation.2 | convolution fusion | flops 302284800 | bytes 6930436 | tf_op jit(solution)/shard_map/dot_general | solution.py:80
  50.0 0.7 constant_dynamic-slice_fusion
  50.8 1.9 %collective-permute-start.4 = (bf16[24,6144]{1,0:T(8,128)(2,1)}, bf16[24,6144]{1,0:T(8,128)(2,1)}, u32[]{:S(2)}, u32[]{:S(2)}) collective-permute-start(bf16[24,6144]{1,0:T(8,128)(2,1)} %constant_dynamic-slice_fusion), channel_id=1, source_target_pairs={{0,1},{1,0},{2,3},{3,2},{4,5},{5,4},{6,7},{7,6},{8,9},{9,8},{10,11... | collective-permute-start | bytes 884744 | tf_op jit(solution)/shard_map/ppermute | solution.py:83
  52.7 0.7 dynamic-slice_bitcast_fusion.5
  53.4 0.0 slice-done
  53.4 0.0 slice-done.1
  53.4 0.0 copy-start.1
  53.4 0.0 copy-start.2
  53.4 2.6 %convolution_convert_fusion = bf16[168,6144]{1,0:T(8,128)(2,1)} fusion(bf16[512,6144]{1,0:T(8,128)(2,1)S(1)} %bitcast.63, bf16[24,512]{1,0:T(8,128)(2,1)S(1)} %get-tuple-element.20, bf16[48,512]{1,0:T(8,128)(2,1)S(1)} %get-tuple-element.14, bf16[48,512]{1,0:T(8,128)(2,1)S(1)} %get-tuple-element.15, bf16[48,512]{1,0:T(8,128)(2,1)S(1)} %get-tuple-element.16), kind=kOutput, calls=%fused_computation | convolution fusion | flops 1058684928 | bytes 8527872 | tf_op jit(solution)/shard_map/dot_general | solution.py:90
  56.0 2.4 %collective-permute-start.3 = (bf16[168,6144]{1,0:T(8,128)(2,1)}, bf16[168,6144]{1,0:T(8,128)(2,1)S(1)}, u32[]{:S(2)}, u32[]{:S(2)}) collective-permute-start(bf16[168,6144]{1,0:T(8,128)(2,1)} %convolution_convert_fusion), channel_id=1, source_target_pairs={{0,1},{1,0},{2,3},{3,2},{4,5},{5,4},{6,7},{7,6},{8,9},{9,8},{10,11... | collective-permute-start | bytes 6193160 | tf_op jit(solution)/shard_map/ppermute | solution.py:91
  58.4 0.0 collective-permute-done.4
  58.4 1.0 add_convert_fusion
  59.4 3.6 %collective-permute-start.5 = (bf16[24,6144]{1,0:T(8,128)(2,1)S(1)}, bf16[24,6144]{1,0:T(8,128)(2,1)S(1)}, u32[]{:S(2)}, u32[]{:S(2)}) collective-permute-start(bf16[24,6144]{1,0:T(8,128)(2,1)S(1)} %add_convert_fusion), channel_id=1, source_target_pairs={{0,2},{1,15},{2,4},{3,1},{4,6},{5,3},{6,8},{7,5},{8,10},{9,7},{10,... | collective-permute-start | bytes 884744 | tf_op jit(solution)/shard_map/ppermute | solution.py:109
  63.1 0.0 copy-done.1
  63.1 0.0 copy-done.2
  63.1 4.0 %convolution_convert_fusion.1 = bf16[168,6144]{1,0:T(8,128)(2,1)S(1)} fusion(bf16[512,6144]{1,0:T(8,128)(2,1)} %param.11, bf16[24,512]{1,0:T(8,128)(2,1)S(1)} %get-tuple-element.19, bf16[48,512]{1,0:T(8,128)(2,1)S(1)} %copy-done.1, bf16[48,512]{1,0:T(8,128)(2,1)S(1)} %copy-done.2, bf16[48,512]{1,0:T(8,128)(2,1)S(1)} %get-tuple-element.13), kind=kOutput, calls=%fused_computation.1 | convolution fusion | flops 1058684928 | bytes 8527872 | tf_op jit(solution)/shard_map/dot_general | solution.py:98
  67.1 0.5 convert_element_type.137
  67.6 2.7 %collective-permute-done.5 = bf16[24,6144]{1,0:T(8,128)(2,1)S(1)} collective-permute-done((bf16[24,6144]{1,0:T(8,128)(2,1)S(1)}, bf16[24,6144]{1,0:T(8,128)(2,1)S(1)}, u32[]{:S(2)}, u32[]{:S(2)}) %collective-permute-start.5) | collective-permute-done | bytes 294944 | tf_op jit(solution)/shard_map/ppermute | solution.py:109
  70.4 0.0 collective-permute-done.3
  70.4 0.5 convert_element_type.139
  70.8 0.1 fusion.5
  71.0 1.9 %collective-permute-start.6 = (bf16[48,6144]{1,0:T(8,128)(2,1)S(1)}, bf16[48,6144]{1,0:T(8,128)(2,1)S(1)}, u32[]{:S(2)}, u32[]{:S(2)}) collective-permute-start(bf16[48,6144]{1,0:T(8,128)(2,1)S(1)} %fusion.5), channel_id=1, source_target_pairs={{0,2},{1,15},{2,4},{3,1},{4,6},{5,3},{6,8},{7,5},{8,10},{9,7},{10,... | collective-permute-start | bytes 1769480 | tf_op jit(solution)/shard_map/ppermute | solution.py:109
  72.9 11.1 %collective-permute-done.6 = bf16[48,6144]{1,0:T(8,128)(2,1)S(1)} collective-permute-done((bf16[48,6144]{1,0:T(8,128)(2,1)S(1)}, bf16[48,6144]{1,0:T(8,128)(2,1)S(1)}, u32[]{:S(2)}, u32[]{:S(2)}) %collective-permute-start.6) | collective-permute-done | bytes 589856 | tf_op jit(solution)/shard_map/ppermute | solution.py:109
  84.0 0.2 fusion.7
  84.2 1.9 %collective-permute-start.7 = (bf16[48,6144]{1,0:T(8,128)(2,1)S(1)}, bf16[48,6144]{1,0:T(8,128)(2,1)S(1)}, u32[]{:S(2)}, u32[]{:S(2)}) collective-permute-start(bf16[48,6144]{1,0:T(8,128)(2,1)S(1)} %fusion.7), channel_id=1, source_target_pairs={{0,2},{1,15},{2,4},{3,1},{4,6},{5,3},{6,8},{7,5},{8,10},{9,7},{10,... | collective-permute-start | bytes 1769480 | tf_op jit(solution)/shard_map/ppermute | solution.py:109
  86.1 11.1 %collective-permute-done.7 = bf16[48,6144]{1,0:T(8,128)(2,1)S(1)} collective-permute-done((bf16[48,6144]{1,0:T(8,128)(2,1)S(1)}, bf16[48,6144]{1,0:T(8,128)(2,1)S(1)}, u32[]{:S(2)}, u32[]{:S(2)}) %collective-permute-start.7) | collective-permute-done | bytes 589856 | tf_op jit(solution)/shard_map/ppermute | solution.py:109
  97.1 0.2 fusion.8
  97.4 1.9 %collective-permute-start.9 = (bf16[24,6144]{1,0:T(8,128)(2,1)S(1)}, bf16[24,6144]{1,0:T(8,128)(2,1)S(1)}, u32[]{:S(2)}, u32[]{:S(2)}) collective-permute-start(bf16[24,6144]{1,0:T(8,128)(2,1)S(1)} %get-tuple-element.12), channel_id=1, source_target_pairs={{0,3},{1,14},{2,5},{3,0},{4,7},{5,2},{6,9},{7,4},{8,11},{9,6},{10,... | collective-permute-start | bytes 884744 | tf_op jit(solution)/shard_map/ppermute | solution.py:109
  99.3 1.9 %collective-permute-start.8 = (bf16[24,6144]{1,0:T(8,128)(2,1)S(1)}, bf16[24,6144]{1,0:T(8,128)(2,1)S(1)}, u32[]{:S(2)}, u32[]{:S(2)}) collective-permute-start(bf16[24,6144]{1,0:T(8,128)(2,1)S(1)} %get-tuple-element.11), channel_id=1, source_target_pairs={{0,2},{1,15},{2,4},{3,1},{4,6},{5,3},{6,8},{7,5},{8,10},{9,7},{10,... | collective-permute-start | bytes 884744 | tf_op jit(solution)/shard_map/ppermute | solution.py:109
  101.3 4.2 %collective-permute-done.9 = bf16[24,6144]{1,0:T(8,128)(2,1)S(1)} collective-permute-done((bf16[24,6144]{1,0:T(8,128)(2,1)S(1)}, bf16[24,6144]{1,0:T(8,128)(2,1)S(1)}, u32[]{:S(2)}, u32[]{:S(2)}) %collective-permute-start.9) | collective-permute-done | bytes 294944 | tf_op jit(solution)/shard_map/ppermute | solution.py:109
  105.4 3.7 %collective-permute-done.8 = bf16[24,6144]{1,0:T(8,128)(2,1)S(1)} collective-permute-done((bf16[24,6144]{1,0:T(8,128)(2,1)S(1)}, bf16[24,6144]{1,0:T(8,128)(2,1)S(1)}, u32[]{:S(2)}, u32[]{:S(2)}) %collective-permute-start.8) | collective-permute-done | bytes 294944 | tf_op jit(solution)/shard_map/ppermute | solution.py:109
  109.2 0.8 fusion.12
  (8 shorter events, 0.2 us)
Async XLA Ops:
  0.0 20.3 %copy-start = (bf16[384,512]{1,0:T(8,128)(2,1)S(1)}, bf16[384,512]{1,0:T(8,128)(2,1)}, u32[]{:S(2)}) copy-start(bf16[384,512]{1,0:T(8,128)(2,1)} %param.6) | copy-start | bytes 1179652
  0.0 20.3 %copy-start.4 = (bf16[384,512]{1,0:T(8,128)(2,1)S(1)}, bf16[384,512]{1,0:T(8,128)(2,1)}, u32[]{:S(2)}) copy-start(bf16[384,512]{1,0:T(8,128)(2,1)} %param.8) | copy-start | bytes 1179652
  6.8 22.4 %collective-permute-start.1 = (bf16[4,128,128]{2,1,0:T(8,128)(2,1)S(1)}, bf16[4,128,128]{2,1,0:T(8,128)(2,1)S(1)}, u32[]{:S(2)}, u32[]{:S(2)}) collective-permute-start(bf16[4,128,128]{2,1,0:T(8,128)(2,1)S(1)} %convolution_convert_fusion.3), channel_id=1, source_target_pairs={{0,32},{16,48},{32,64},{48,80},{64,96},{80,112},{96,128},{112,144}... | collective-permute-start | bytes 393224 | tf_op jit(solution)/shard_map/ppermute | solution.py:10
  14.7 18.5 %collective-permute-start = (bf16[4,128,128]{2,1,0:T(8,128)(2,1)S(1)}, bf16[4,128,128]{2,1,0:T(8,128)(2,1)S(1)}, u32[]{:S(2)}, u32[]{:S(2)}) collective-permute-start(bf16[4,128,128]{2,1,0:T(8,128)(2,1)S(1)} %convolution_convert_fusion.3), channel_id=1, source_target_pairs={{0,16},{16,32},{32,48},{48,64},{64,80},{80,96},{96,112},{112,128},... | collective-permute-start | bytes 393224 | tf_op jit(solution)/shard_map/ppermute | solution.py:10
  21.1 24.1 %copy-start.3 = (f32[512]{0:T(512)S(1)}, f32[512]{0:T(512)}, u32[]{:S(2)}) copy-start(f32[512]{0:T(512)} %param.10) | copy-start | bytes 6148
  33.3 11.4 %collective-permute-start.2 = (bf16[4,128,128]{2,1,0:T(8,128)(2,1)S(1)}, bf16[4,128,128]{2,1,0:T(8,128)(2,1)S(1)}, u32[]{:S(2)}, u32[]{:S(2)}) collective-permute-start(bf16[4,128,128]{2,1,0:T(8,128)(2,1)S(1)} %fusion.30), channel_id=1, source_target_pairs={{0,32},{16,48},{32,64},{48,80},{64,96},{80,112},{96,128},{112,144}... | collective-permute-start | bytes 393224 | tf_op jit(solution)/shard_map/ppermute | solution.py:10
  44.6 8.8 %slice-start = ((s8[6291456]{0:T(1024)(128)(4,1)}), s8[2097152]{0:T(1024)(128)(4,1)S(1)}, s32[]{:S(2)}) async-start(s8[6291456]{0:T(1024)(128)(4,1)} %bitcast.62), calls=%async_computation | async-start | bytes 4194304
  45.8 7.5 %slice-start.1 = ((s8[6291456]{0:T(1024)(128)(4,1)}), s8[4194304]{0:T(1024)(128)(4,1)S(1)}, s32[]{:S(2)}) async-start(s8[6291456]{0:T(1024)(128)(4,1)} %bitcast.62), calls=%async_computation.1 | async-start | bytes 8388608
  50.8 7.6 %collective-permute-start.4 = (bf16[24,6144]{1,0:T(8,128)(2,1)}, bf16[24,6144]{1,0:T(8,128)(2,1)}, u32[]{:S(2)}, u32[]{:S(2)}) collective-permute-start(bf16[24,6144]{1,0:T(8,128)(2,1)} %constant_dynamic-slice_fusion), channel_id=1, source_target_pairs={{0,1},{1,0},{2,3},{3,2},{4,5},{5,4},{6,7},{7,6},{8,9},{9,8},{10,11... | collective-permute-start | bytes 884744 | tf_op jit(solution)/shard_map/ppermute | solution.py:83
  53.4 9.7 %copy-start.1 = (bf16[48,512]{1,0:T(8,128)(2,1)S(1)}, bf16[48,512]{1,0:T(8,128)(2,1)}, u32[]{:S(2)}) copy-start(bf16[48,512]{1,0:T(8,128)(2,1)} %get-tuple-element.17) | copy-start | bytes 147460
  53.4 9.7 %copy-start.2 = (bf16[48,512]{1,0:T(8,128)(2,1)S(1)}, bf16[48,512]{1,0:T(8,128)(2,1)}, u32[]{:S(2)}) copy-start(bf16[48,512]{1,0:T(8,128)(2,1)} %get-tuple-element.18) | copy-start | bytes 147460
  56.0 14.4 %collective-permute-start.3 = (bf16[168,6144]{1,0:T(8,128)(2,1)}, bf16[168,6144]{1,0:T(8,128)(2,1)S(1)}, u32[]{:S(2)}, u32[]{:S(2)}) collective-permute-start(bf16[168,6144]{1,0:T(8,128)(2,1)} %convolution_convert_fusion), channel_id=1, source_target_pairs={{0,1},{1,0},{2,3},{3,2},{4,5},{5,4},{6,7},{7,6},{8,9},{9,8},{10,11... | collective-permute-start | bytes 6193160 | tf_op jit(solution)/shard_map/ppermute | solution.py:91
  59.4 10.9 %collective-permute-start.5 = (bf16[24,6144]{1,0:T(8,128)(2,1)S(1)}, bf16[24,6144]{1,0:T(8,128)(2,1)S(1)}, u32[]{:S(2)}, u32[]{:S(2)}) collective-permute-start(bf16[24,6144]{1,0:T(8,128)(2,1)S(1)} %add_convert_fusion), channel_id=1, source_target_pairs={{0,2},{1,15},{2,4},{3,1},{4,6},{5,3},{6,8},{7,5},{8,10},{9,7},{10,... | collective-permute-start | bytes 884744 | tf_op jit(solution)/shard_map/ppermute | solution.py:109
  71.0 13.0 %collective-permute-start.6 = (bf16[48,6144]{1,0:T(8,128)(2,1)S(1)}, bf16[48,6144]{1,0:T(8,128)(2,1)S(1)}, u32[]{:S(2)}, u32[]{:S(2)}) collective-permute-start(bf16[48,6144]{1,0:T(8,128)(2,1)S(1)} %fusion.5), channel_id=1, source_target_pairs={{0,2},{1,15},{2,4},{3,1},{4,6},{5,3},{6,8},{7,5},{8,10},{9,7},{10,... | collective-permute-start | bytes 1769480 | tf_op jit(solution)/shard_map/ppermute | solution.py:109
  84.2 13.0 %collective-permute-start.7 = (bf16[48,6144]{1,0:T(8,128)(2,1)S(1)}, bf16[48,6144]{1,0:T(8,128)(2,1)S(1)}, u32[]{:S(2)}, u32[]{:S(2)}) collective-permute-start(bf16[48,6144]{1,0:T(8,128)(2,1)S(1)} %fusion.7), channel_id=1, source_target_pairs={{0,2},{1,15},{2,4},{3,1},{4,6},{5,3},{6,8},{7,5},{8,10},{9,7},{10,... | collective-permute-start | bytes 1769480 | tf_op jit(solution)/shard_map/ppermute | solution.py:109
  97.4 8.0 %collective-permute-start.9 = (bf16[24,6144]{1,0:T(8,128)(2,1)S(1)}, bf16[24,6144]{1,0:T(8,128)(2,1)S(1)}, u32[]{:S(2)}, u32[]{:S(2)}) collective-permute-start(bf16[24,6144]{1,0:T(8,128)(2,1)S(1)} %get-tuple-element.12), channel_id=1, source_target_pairs={{0,3},{1,14},{2,5},{3,0},{4,7},{5,2},{6,9},{7,4},{8,11},{9,6},{10,... | collective-permute-start | bytes 884744 | tf_op jit(solution)/shard_map/ppermute | solution.py:109
  99.3 9.8 %collective-permute-start.8 = (bf16[24,6144]{1,0:T(8,128)(2,1)S(1)}, bf16[24,6144]{1,0:T(8,128)(2,1)S(1)}, u32[]{:S(2)}, u32[]{:S(2)}) collective-permute-start(bf16[24,6144]{1,0:T(8,128)(2,1)S(1)} %get-tuple-element.11), channel_id=1, source_target_pairs={{0,2},{1,15},{2,4},{3,1},{4,6},{5,3},{6,8},{7,5},{8,10},{9,7},{10,... | collective-permute-start | bytes 884744 | tf_op jit(solution)/shard_map/ppermute | solution.py:109

commit v8 on v7

--- a/solution.py
+++ b/solution.py
@@ -2,6 +2,7 @@
 import jax.numpy as jnp
 from jax import lax
 from jax.sharding import PartitionSpec as P
+
 
 DH = 128
 
@@ -15,7 +16,7 @@
     heads_here = queries.shape[1] // DH
     place = lax.axis_index("ctx")
     first = place * tok
-    ends = jnp.cumsum(doc_lengths)
+    ends = jnp.cumsum(doc_lengths.reshape(1, -1), axis=1).reshape(-1)
 
     def doc_at(p):
         return jnp.sum((ends <= p).astype(jnp.int32))
@@ -127,8 +128,12 @@
 def solution(mesh):
     placed = (P("ctx", "head"), P("ctx", "head"), P("ctx", "head"), P(), P("head"), P("head", None))
     n_ctx, n_head = mesh.shape["ctx"], mesh.shape["head"]
+
+    def body(*a):
+        return local(n_ctx, n_head, *a)
+
     return jax.shard_map(
-        lambda *a: local(n_ctx, n_head, *a),
+        body,
         mesh=mesh,
         in_specs=placed,
         out_specs=P(("ctx", "head"), None),

time: 111 us -> 110 us (level)
  waiting for transfers between devices: 49.2 us -> 47.9 us
    ppermute x3, waiting for transfers between devices: 16.5 us -> 15.1 us  [shift_from(): return lax.ppermute(x, axis, [(i, i + step) for i in range(size - step)])]
  transfers between devices with their start and end apart: 10 -> 10, of which waited for: 8 -> 8; matrix products, arithmetic and copies ran while one was open for 10% -> 11% of each run, Pallas kernels for 0% -> 0%
where the time goes in v8:
time: 110 us
  waiting for transfers between devices  47.9 us (44%)
  starting transfers between devices  30.6 us (28%)
  matrix products  14.4 us (13%)
  other arithmetic  6.35 us (6%)
  between operations  6.11 us (6%)
  local copies, waits for them, and re-layouts  4.23 us (4%)
    ppermute x5, waiting for transfers between devices, send(): lax.ppermute(x.astype(jnp.bfloat16), 'head', perm).astype(jnp.float32)  32.7 us
    ppermute x3, waiting for transfers between devices, shift_from(): return lax.ppermute(x, axis, [(i, i + step) for i in range(size - step)])  15.1 us
    ppermute x3, starting transfers between devices, shift_from(): return lax.ppermute(x, axis, [(i, i + step) for i in range(size - step)])  15 us
    ppermute x5, starting transfers between devices, send(): lax.ppermute(x.astype(jnp.bfloat16), 'head', perm).astype(jnp.float32)  11.3 us
    dot_general x1, matrix products, local(): lax.dot_general(w_out, take(by_chip, far), (((0,), (1,)), ((), ())), pref...  4.14 us
    dot_general x1, matrix products, local(): jnp.dot(my_rows, w_out, preferred_element_type=jnp.float32)  4.03 us
    dot_general x1, matrix products, local(): jnp.dot(sib_rows, w_out, preferred_element_type=jnp.float32)  2.59 us
    ppermute x1, starting transfers between devices, local(): from_sib = lax.ppermute(to_sib, 'head', pair).astype(jnp.float32)  2.39 us
  transfers between devices with their start and end apart: 10, of which 8 were waited for; matrix products, arithmetic and copies ran while one was open for 11% of the time, Pallas kernels for 0%

profile of v8, /device:TPU:14, one launch (start us, length us, event | category | flops | bytes accessed | tf_op | source)
XLA Modules:
  0.0 109.6 jit_solution(17438545115966658979)
XLA Ops:
  0.0 0.0 copy-start
  0.0 1.0 reduce_window_sum.11
  1.0 0.8 fusion.56
  3.1 1.2 %copy.27 = bf16[384,512]{0,1:T(8,128)(2,1)S(1)} copy(bf16[384,512]{1,0:T(8,128)(2,1)} %param.7) | data formatting | bytes 786432 | tf_op jit(solution)/shard_map/reshape | solution.py:32
  4.3 0.6 constant_dynamic-slice_fusion.1
  5.5 1.3 %convolution_convert_fusion.3 = bf16[4,128,128]{2,1,0:T(8,128)(2,1)S(1)} fusion(bf16[384,4,128]{0,2,1:T(8,128)(2,1)S(1)} %bitcast.71, pred[384]{0:T(512)(128)(4,1)S(1)} %broadcast_compare_fusion, bf16[384,512]{1,0:T(8,128)(2,1)} %param.8), kind=kOutput, calls=%fused_computation.19 | convolution fusion | flops 50593792 | bytes 917888 | tf_op jit(solution)/shard_map/thd,the->hde/dot_general | solution.py:39
  6.8 7.9 %collective-permute-start.1 = (bf16[4,128,128]{2,1,0:T(8,128)(2,1)S(1)}, bf16[4,128,128]{2,1,0:T(8,128)(2,1)S(1)}, u32[]{:S(2)}, u32[]{:S(2)}) collective-permute-start(bf16[4,128,128]{2,1,0:T(8,128)(2,1)S(1)} %convolution_convert_fusion.3), channel_id=1, source_target_pairs={{0,32},{16,48},{32,64},{48,80},{64,96},{80,112},{96,128},{112,144}... | collective-permute-start | bytes 393224 | tf_op jit(solution)/shard_map/ppermute | solution.py:11
  14.7 5.2 %collective-permute-start = (bf16[4,128,128]{2,1,0:T(8,128)(2,1)S(1)}, bf16[4,128,128]{2,1,0:T(8,128)(2,1)S(1)}, u32[]{:S(2)}, u32[]{:S(2)}) collective-permute-start(bf16[4,128,128]{2,1,0:T(8,128)(2,1)S(1)} %convolution_convert_fusion.3), channel_id=1, source_target_pairs={{0,16},{16,32},{32,48},{48,64},{64,80},{80,96},{96,112},{112,128},... | collective-permute-start | bytes 393224 | tf_op jit(solution)/shard_map/ppermute | solution.py:11
  19.9 0.2 convert_reduce_fusion
  20.2 0.1 fusion.13
  20.3 0.0 copy-done
  20.3 1.8 %fusion.3 = f32[384,4,128]{0,2,1:T(8,128)S(1)} fusion(bf16[384,4,128]{0,2,1:T(8,128)(2,1)S(1)} %bitcast.72, pred[384,384]{1,0:T(8,128)(4,1)S(1)} %fusion.13, bf16[384,512]{1,0:T(8,128)(2,1)} %param.8, bf16[384,512]{1,0:T(8,128)(2,1)S(1)} %copy-done), kind=kOutput, calls=%fused_computation.8 | convolution fusion | flops 303169536 | bytes 2113536 | tf_op jit(solution)/shard_map/hts,shd->thd/dot_general | solution.py:53
  22.1 0.0 copy-start.3
  22.1 0.5 slice.28
  26.5 2.8 %collective-permute-done.1 = bf16[4,128,128]{2,1,0:T(8,128)(2,1)S(1)} collective-permute-done((bf16[4,128,128]{2,1,0:T(8,128)(2,1)S(1)}, bf16[4,128,128]{2,1,0:T(8,128)(2,1)S(1)}, u32[]{:S(2)}, u32[]{:S(2)}) %collective-permute-start.1) | collective-permute-done | bytes 131104 | tf_op jit(solution)/shard_map/ppermute | solution.py:11
  29.2 4.0 %collective-permute-done = bf16[4,128,128]{2,1,0:T(8,128)(2,1)S(1)} collective-permute-done((bf16[4,128,128]{2,1,0:T(8,128)(2,1)S(1)}, bf16[4,128,128]{2,1,0:T(8,128)(2,1)S(1)}, u32[]{:S(2)}, u32[]{:S(2)}) %collective-permute-start) | collective-permute-done | bytes 131104 | tf_op jit(solution)/shard_map/ppermute | solution.py:11
  33.2 1.9 %collective-permute-start.2 = (bf16[4,128,128]{2,1,0:T(8,128)(2,1)S(1)}, bf16[4,128,128]{2,1,0:T(8,128)(2,1)S(1)}, u32[]{:S(2)}, u32[]{:S(2)}) collective-permute-start(bf16[4,128,128]{2,1,0:T(8,128)(2,1)S(1)} %fusion.30), channel_id=1, source_target_pairs={{0,32},{16,48},{32,64},{48,80},{64,96},{80,112},{96,128},{112,144}... | collective-permute-start | bytes 393224 | tf_op jit(solution)/shard_map/ppermute | solution.py:11
  35.2 0.7 and_convert_fusion
  35.8 8.4 %collective-permute-done.2 = bf16[4,128,128]{2,1,0:T(8,128)(2,1)S(1)} collective-permute-done((bf16[4,128,128]{2,1,0:T(8,128)(2,1)S(1)}, bf16[4,128,128]{2,1,0:T(8,128)(2,1)S(1)}, u32[]{:S(2)}, u32[]{:S(2)}) %collective-permute-start.2) | collective-permute-done | bytes 131104 | tf_op jit(solution)/shard_map/ppermute | solution.py:11
  44.2 0.0 slice-start
  44.2 0.6 multiply_reduce_fusion
  44.9 0.0 copy-done.3
  44.9 0.1 multiply_convert_fusion
  45.0 0.2 copy.25
  45.3 0.2 convert_element_type.135
  45.4 0.0 slice-start.1
  45.5 4.1 %convolution_convert_fusion.2 = bf16[48,6144]{1,0:T(8,128)(2,1)S(1)} fusion(bf16[512,6144]{1,0:T(8,128)(2,1)} %param.11, bf16[8,48,512]{2,1,0:T(8,128)(2,1)S(1)} %convert_element_type.135, s32[]{:T(128)S(6)} %select_n.134), kind=kOutput, calls=%fused_computation.2 | convolution fusion | flops 302284800 | bytes 6930436 | tf_op jit(solution)/shard_map/dot_general | solution.py:81
  49.6 0.7 constant_dynamic-slice_fusion
  50.4 1.9 %collective-permute-start.4 = (bf16[24,6144]{1,0:T(8,128)(2,1)}, bf16[24,6144]{1,0:T(8,128)(2,1)}, u32[]{:S(2)}, u32[]{:S(2)}) collective-permute-start(bf16[24,6144]{1,0:T(8,128)(2,1)} %constant_dynamic-slice_fusion), channel_id=1, source_target_pairs={{0,1},{1,0},{2,3},{3,2},{4,5},{5,4},{6,7},{7,6},{8,9},{9,8},{10,11... | collective-permute-start | bytes 884744 | tf_op jit(solution)/shard_map/ppermute | solution.py:84
  52.3 0.7 dynamic-slice_bitcast_fusion.5
  53.0 0.0 slice-done
  53.0 0.0 slice-done.1
  53.0 0.0 copy-start.1
  53.0 0.0 copy-start.2
  53.0 2.6 %convolution_convert_fusion = bf16[168,6144]{1,0:T(8,128)(2,1)} fusion(bf16[512,6144]{1,0:T(8,128)(2,1)S(1)} %bitcast.70, bf16[24,512]{1,0:T(8,128)(2,1)S(1)} %get-tuple-element.20, bf16[48,512]{1,0:T(8,128)(2,1)S(1)} %get-tuple-element.14, bf16[48,512]{1,0:T(8,128)(2,1)S(1)} %get-tuple-element.15, bf16[48,512]{1,0:T(8,128)(2,1)S(1)} %get-tuple-element.16), kind=kOutput, calls=%fused_computation | convolution fusion | flops 1058684928 | bytes 8527872 | tf_op jit(solution)/shard_map/dot_general | solution.py:91
  55.6 2.4 %collective-permute-start.3 = (bf16[168,6144]{1,0:T(8,128)(2,1)}, bf16[168,6144]{1,0:T(8,128)(2,1)S(1)}, u32[]{:S(2)}, u32[]{:S(2)}) collective-permute-start(bf16[168,6144]{1,0:T(8,128)(2,1)} %convolution_convert_fusion), channel_id=1, source_target_pairs={{0,1},{1,0},{2,3},{3,2},{4,5},{5,4},{6,7},{7,6},{8,9},{9,8},{10,11... | collective-permute-start | bytes 6193160 | tf_op jit(solution)/shard_map/ppermute | solution.py:92
  58.0 0.0 collective-permute-done.4
  58.0 1.0 add_convert_fusion
  59.0 3.6 %collective-permute-start.5 = (bf16[24,6144]{1,0:T(8,128)(2,1)S(1)}, bf16[24,6144]{1,0:T(8,128)(2,1)S(1)}, u32[]{:S(2)}, u32[]{:S(2)}) collective-permute-start(bf16[24,6144]{1,0:T(8,128)(2,1)S(1)} %add_convert_fusion), channel_id=1, source_target_pairs={{0,2},{1,15},{2,4},{3,1},{4,6},{5,3},{6,8},{7,5},{8,10},{9,7},{10,... | collective-permute-start | bytes 884744 | tf_op jit(solution)/shard_map/ppermute | solution.py:110
  62.7 0.0 copy-done.1
  62.7 0.0 copy-done.2
  62.7 4.0 %convolution_convert_fusion.1 = bf16[168,6144]{1,0:T(8,128)(2,1)S(1)} fusion(bf16[512,6144]{1,0:T(8,128)(2,1)} %param.11, bf16[24,512]{1,0:T(8,128)(2,1)S(1)} %get-tuple-element.19, bf16[48,512]{1,0:T(8,128)(2,1)S(1)} %copy-done.1, bf16[48,512]{1,0:T(8,128)(2,1)S(1)} %copy-done.2, bf16[48,512]{1,0:T(8,128)(2,1)S(1)} %get-tuple-element.13), kind=kOutput, calls=%fused_computation.1 | convolution fusion | flops 1058684928 | bytes 8527872 | tf_op jit(solution)/shard_map/dot_general | solution.py:99
  66.7 0.5 convert_element_type.137
  67.2 2.7 %collective-permute-done.5 = bf16[24,6144]{1,0:T(8,128)(2,1)S(1)} collective-permute-done((bf16[24,6144]{1,0:T(8,128)(2,1)S(1)}, bf16[24,6144]{1,0:T(8,128)(2,1)S(1)}, u32[]{:S(2)}, u32[]{:S(2)}) %collective-permute-start.5) | collective-permute-done | bytes 294944 | tf_op jit(solution)/shard_map/ppermute | solution.py:110
  69.9 0.0 collective-permute-done.3
  70.0 0.5 convert_element_type.139
  70.4 0.1 fusion.5
  70.6 1.9 %collective-permute-start.6 = (bf16[48,6144]{1,0:T(8,128)(2,1)S(1)}, bf16[48,6144]{1,0:T(8,128)(2,1)S(1)}, u32[]{:S(2)}, u32[]{:S(2)}) collective-permute-start(bf16[48,6144]{1,0:T(8,128)(2,1)S(1)} %fusion.5), channel_id=1, source_target_pairs={{0,2},{1,15},{2,4},{3,1},{4,6},{5,3},{6,8},{7,5},{8,10},{9,7},{10,... | collective-permute-start | bytes 1769480 | tf_op jit(solution)/shard_map/ppermute | solution.py:110
  72.5 11.1 %collective-permute-done.6 = bf16[48,6144]{1,0:T(8,128)(2,1)S(1)} collective-permute-done((bf16[48,6144]{1,0:T(8,128)(2,1)S(1)}, bf16[48,6144]{1,0:T(8,128)(2,1)S(1)}, u32[]{:S(2)}, u32[]{:S(2)}) %collective-permute-start.6) | collective-permute-done | bytes 589856 | tf_op jit(solution)/shard_map/ppermute | solution.py:110
  83.6 0.2 fusion.7
  83.7 1.9 %collective-permute-start.7 = (bf16[48,6144]{1,0:T(8,128)(2,1)S(1)}, bf16[48,6144]{1,0:T(8,128)(2,1)S(1)}, u32[]{:S(2)}, u32[]{:S(2)}) collective-permute-start(bf16[48,6144]{1,0:T(8,128)(2,1)S(1)} %fusion.7), channel_id=1, source_target_pairs={{0,2},{1,15},{2,4},{3,1},{4,6},{5,3},{6,8},{7,5},{8,10},{9,7},{10,... | collective-permute-start | bytes 1769480 | tf_op jit(solution)/shard_map/ppermute | solution.py:110
  85.7 11.1 %collective-permute-done.7 = bf16[48,6144]{1,0:T(8,128)(2,1)S(1)} collective-permute-done((bf16[48,6144]{1,0:T(8,128)(2,1)S(1)}, bf16[48,6144]{1,0:T(8,128)(2,1)S(1)}, u32[]{:S(2)}, u32[]{:S(2)}) %collective-permute-start.7) | collective-permute-done | bytes 589856 | tf_op jit(solution)/shard_map/ppermute | solution.py:110
  96.7 0.2 fusion.8
  97.0 1.9 %collective-permute-start.9 = (bf16[24,6144]{1,0:T(8,128)(2,1)S(1)}, bf16[24,6144]{1,0:T(8,128)(2,1)S(1)}, u32[]{:S(2)}, u32[]{:S(2)}) collective-permute-start(bf16[24,6144]{1,0:T(8,128)(2,1)S(1)} %get-tuple-element.12), channel_id=1, source_target_pairs={{0,3},{1,14},{2,5},{3,0},{4,7},{5,2},{6,9},{7,4},{8,11},{9,6},{10,... | collective-permute-start | bytes 884744 | tf_op jit(solution)/shard_map/ppermute | solution.py:110
  98.9 1.9 %collective-permute-start.8 = (bf16[24,6144]{1,0:T(8,128)(2,1)S(1)}, bf16[24,6144]{1,0:T(8,128)(2,1)S(1)}, u32[]{:S(2)}, u32[]{:S(2)}) collective-permute-start(bf16[24,6144]{1,0:T(8,128)(2,1)S(1)} %get-tuple-element.11), channel_id=1, source_target_pairs={{0,2},{1,15},{2,4},{3,1},{4,6},{5,3},{6,8},{7,5},{8,10},{9,7},{10,... | collective-permute-start | bytes 884744 | tf_op jit(solution)/shard_map/ppermute | solution.py:110
  100.8 4.2 %collective-permute-done.9 = bf16[24,6144]{1,0:T(8,128)(2,1)S(1)} collective-permute-done((bf16[24,6144]{1,0:T(8,128)(2,1)S(1)}, bf16[24,6144]{1,0:T(8,128)(2,1)S(1)}, u32[]{:S(2)}, u32[]{:S(2)}) %collective-permute-start.9) | collective-permute-done | bytes 294944 | tf_op jit(solution)/shard_map/ppermute | solution.py:110
  105.0 3.7 %collective-permute-done.8 = bf16[24,6144]{1,0:T(8,128)(2,1)S(1)} collective-permute-done((bf16[24,6144]{1,0:T(8,128)(2,1)S(1)}, bf16[24,6144]{1,0:T(8,128)(2,1)S(1)}, u32[]{:S(2)}, u32[]{:S(2)}) %collective-permute-start.8) | collective-permute-done | bytes 294944 | tf_op jit(solution)/shard_map/ppermute | solution.py:110
  108.7 0.8 fusion.12
  (8 shorter events, 0.2 us)
Async XLA Ops:
  0.0 20.3 %copy-start = (bf16[384,512]{1,0:T(8,128)(2,1)S(1)}, bf16[384,512]{1,0:T(8,128)(2,1)}, u32[]{:S(2)}) copy-start(bf16[384,512]{1,0:T(8,128)(2,1)} %param.6) | copy-start | bytes 1179652
  6.8 22.4 %collective-permute-start.1 = (bf16[4,128,128]{2,1,0:T(8,128)(2,1)S(1)}, bf16[4,128,128]{2,1,0:T(8,128)(2,1)S(1)}, u32[]{:S(2)}, u32[]{:S(2)}) collective-permute-start(bf16[4,128,128]{2,1,0:T(8,128)(2,1)S(1)} %convolution_convert_fusion.3), channel_id=1, source_target_pairs={{0,32},{16,48},{32,64},{48,80},{64,96},{80,112},{96,128},{112,144}... | collective-permute-start | bytes 393224 | tf_op jit(solution)/shard_map/ppermute | solution.py:11
  14.7 18.5 %collective-permute-start = (bf16[4,128,128]{2,1,0:T(8,128)(2,1)S(1)}, bf16[4,128,128]{2,1,0:T(8,128)(2,1)S(1)}, u32[]{:S(2)}, u32[]{:S(2)}) collective-permute-start(bf16[4,128,128]{2,1,0:T(8,128)(2,1)S(1)} %convolution_convert_fusion.3), channel_id=1, source_target_pairs={{0,16},{16,32},{32,48},{48,64},{64,80},{80,96},{96,112},{112,128},... | collective-permute-start | bytes 393224 | tf_op jit(solution)/shard_map/ppermute | solution.py:11
  22.1 22.8 %copy-start.3 = (f32[512]{0:T(512)S(1)}, f32[512]{0:T(512)}, u32[]{:S(2)}) copy-start(f32[512]{0:T(512)} %param.10) | copy-start | bytes 6148
  33.2 11.0 %collective-permute-start.2 = (bf16[4,128,128]{2,1,0:T(8,128)(2,1)S(1)}, bf16[4,128,128]{2,1,0:T(8,128)(2,1)S(1)}, u32[]{:S(2)}, u32[]{:S(2)}) collective-permute-start(bf16[4,128,128]{2,1,0:T(8,128)(2,1)S(1)} %fusion.30), channel_id=1, source_target_pairs={{0,32},{16,48},{32,64},{48,80},{64,96},{80,112},{96,128},{112,144}... | collective-permute-start | bytes 393224 | tf_op jit(solution)/shard_map/ppermute | solution.py:11
  44.2 8.8 %slice-start = ((s8[6291456]{0:T(1024)(128)(4,1)}), s8[2097152]{0:T(1024)(128)(4,1)S(1)}, s32[]{:S(2)}) async-start(s8[6291456]{0:T(1024)(128)(4,1)} %bitcast.69), calls=%async_computation | async-start | bytes 4194304
  45.4 7.5 %slice-start.1 = ((s8[6291456]{0:T(1024)(128)(4,1)}), s8[4194304]{0:T(1024)(128)(4,1)S(1)}, s32[]{:S(2)}) async-start(s8[6291456]{0:T(1024)(128)(4,1)} %bitcast.69), calls=%async_computation.1 | async-start | bytes 8388608
  50.4 7.6 %collective-permute-start.4 = (bf16[24,6144]{1,0:T(8,128)(2,1)}, bf16[24,6144]{1,0:T(8,128)(2,1)}, u32[]{:S(2)}, u32[]{:S(2)}) collective-permute-start(bf16[24,6144]{1,0:T(8,128)(2,1)} %constant_dynamic-slice_fusion), channel_id=1, source_target_pairs={{0,1},{1,0},{2,3},{3,2},{4,5},{5,4},{6,7},{7,6},{8,9},{9,8},{10,11... | collective-permute-start | bytes 884744 | tf_op jit(solution)/shard_map/ppermute | solution.py:84
  53.0 9.7 %copy-start.1 = (bf16[48,512]{1,0:T(8,128)(2,1)S(1)}, bf16[48,512]{1,0:T(8,128)(2,1)}, u32[]{:S(2)}) copy-start(bf16[48,512]{1,0:T(8,128)(2,1)} %get-tuple-element.17) | copy-start | bytes 147460
  53.0 9.7 %copy-start.2 = (bf16[48,512]{1,0:T(8,128)(2,1)S(1)}, bf16[48,512]{1,0:T(8,128)(2,1)}, u32[]{:S(2)}) copy-start(bf16[48,512]{1,0:T(8,128)(2,1)} %get-tuple-element.18) | copy-start | bytes 147460
  55.6 14.4 %collective-permute-start.3 = (bf16[168,6144]{1,0:T(8,128)(2,1)}, bf16[168,6144]{1,0:T(8,128)(2,1)S(1)}, u32[]{:S(2)}, u32[]{:S(2)}) collective-permute-start(bf16[168,6144]{1,0:T(8,128)(2,1)} %convolution_convert_fusion), channel_id=1, source_target_pairs={{0,1},{1,0},{2,3},{3,2},{4,5},{5,4},{6,7},{7,6},{8,9},{9,8},{10,11... | collective-permute-start | bytes 6193160 | tf_op jit(solution)/shard_map/ppermute | solution.py:92
  59.0 10.9 %collective-permute-start.5 = (bf16[24,6144]{1,0:T(8,128)(2,1)S(1)}, bf16[24,6144]{1,0:T(8,128)(2,1)S(1)}, u32[]{:S(2)}, u32[]{:S(2)}) collective-permute-start(bf16[24,6144]{1,0:T(8,128)(2,1)S(1)} %add_convert_fusion), channel_id=1, source_target_pairs={{0,2},{1,15},{2,4},{3,1},{4,6},{5,3},{6,8},{7,5},{8,10},{9,7},{10,... | collective-permute-start | bytes 884744 | tf_op jit(solution)/shard_map/ppermute | solution.py:110
  70.6 13.0 %collective-permute-start.6 = (bf16[48,6144]{1,0:T(8,128)(2,1)S(1)}, bf16[48,6144]{1,0:T(8,128)(2,1)S(1)}, u32[]{:S(2)}, u32[]{:S(2)}) collective-permute-start(bf16[48,6144]{1,0:T(8,128)(2,1)S(1)} %fusion.5), channel_id=1, source_target_pairs={{0,2},{1,15},{2,4},{3,1},{4,6},{5,3},{6,8},{7,5},{8,10},{9,7},{10,... | collective-permute-start | bytes 1769480 | tf_op jit(solution)/shard_map/ppermute | solution.py:110
  83.7 13.0 %collective-permute-start.7 = (bf16[48,6144]{1,0:T(8,128)(2,1)S(1)}, bf16[48,6144]{1,0:T(8,128)(2,1)S(1)}, u32[]{:S(2)}, u32[]{:S(2)}) collective-permute-start(bf16[48,6144]{1,0:T(8,128)(2,1)S(1)} %fusion.7), channel_id=1, source_target_pairs={{0,2},{1,15},{2,4},{3,1},{4,6},{5,3},{6,8},{7,5},{8,10},{9,7},{10,... | collective-permute-start | bytes 1769480 | tf_op jit(solution)/shard_map/ppermute | solution.py:110
  97.0 8.0 %collective-permute-start.9 = (bf16[24,6144]{1,0:T(8,128)(2,1)S(1)}, bf16[24,6144]{1,0:T(8,128)(2,1)S(1)}, u32[]{:S(2)}, u32[]{:S(2)}) collective-permute-start(bf16[24,6144]{1,0:T(8,128)(2,1)S(1)} %get-tuple-element.12), channel_id=1, source_target_pairs={{0,3},{1,14},{2,5},{3,0},{4,7},{5,2},{6,9},{7,4},{8,11},{9,6},{10,... | collective-permute-start | bytes 884744 | tf_op jit(solution)/shard_map/ppermute | solution.py:110
  98.9 9.8 %collective-permute-start.8 = (bf16[24,6144]{1,0:T(8,128)(2,1)S(1)}, bf16[24,6144]{1,0:T(8,128)(2,1)S(1)}, u32[]{:S(2)}, u32[]{:S(2)}) collective-permute-start(bf16[24,6144]{1,0:T(8,128)(2,1)S(1)} %get-tuple-element.11), channel_id=1, source_target_pairs={{0,2},{1,15},{2,4},{3,1},{4,6},{5,3},{6,8},{7,5},{8,10},{9,7},{10,... | collective-permute-start | bytes 884744 | tf_op jit(solution)/shard_map/ppermute | solution.py:110

commit v9 on v8

--- a/solution.py
+++ b/solution.py
@@ -78,20 +78,25 @@
     far = chip + n_chip // 2
     steps = n_chip // 2 - 1
     pair = [(i, i ^ 1) for i in range(n_head)]
-    far_part = lax.dot_general(
-        w_out, take(by_chip, far), (((0,), (1,)), ((), ())), preferred_element_type=jnp.float32
-    ).astype(jnp.bfloat16).T
-    far_sib = lax.ppermute(halves(far_part, 1 - core), "head", pair)
-    far_sum = halves(far_part, core).astype(jnp.float32) + far_sib.astype(jnp.float32)
+    first_rows = jnp.concatenate(
+        [take(by_chip, far), take(by_chip, chip - dirn * steps), take(by_chip, chip + dirn * steps)],
+        axis=0,
+    )
+    first_part = jnp.dot(first_rows, w_out, preferred_element_type=jnp.float32).astype(jnp.bfloat16)
+    far_part = first_part[:rows]
+    to_sib_first = jnp.concatenate([halves(far_part, 1 - core), first_part[rows:2 * rows]], axis=0)
+    from_sib_first = lax.ppermute(to_sib_first, "head", pair).astype(jnp.float32)
+    far_sum = halves(far_part, core).astype(jnp.float32) + from_sib_first[:half_rows]
+    near_last = first_part[2 * rows:].astype(jnp.float32) + from_sib_first[half_rows:]
     sib_rows = jnp.concatenate(
-        [take(by_chip, chip - dirn * j) for j in range(1, steps + 1)]
+        [take(by_chip, chip - dirn * j) for j in range(1, steps)]
         + [halves(take(by_chip, chip), 1 - core)],
         axis=0,
     )
     to_sib = jnp.dot(sib_rows, w_out, preferred_element_type=jnp.float32).astype(jnp.bfloat16)
     from_sib = lax.ppermute(to_sib, "head", pair).astype(jnp.float32)
     my_rows = jnp.concatenate(
-        [take(by_chip, chip + dirn * j) for j in range(1, steps + 1)]
+        [take(by_chip, chip + dirn * j) for j in range(1, steps)]
         + [halves(take(by_chip, chip), core)],
         axis=0,
     )
@@ -100,9 +105,11 @@
     ).astype(jnp.float32)
 
     def near(j):
+        if j == steps:
+            return near_last
         return my_part[(j - 1) * rows:j * rows] + from_sib[(j - 1) * rows:j * rows]
 
-    own_sum = my_part[steps * rows:] + from_sib[steps * rows:]
+    own_sum = my_part[(steps - 1) * rows:] + from_sib[(steps - 1) * rows:]
 
     ring = [(i, (i + 2) % n_head) if i % 2 == 0 else (i, (i - 2) % n_head) for i in range(n_head)]
 

time: 110 us -> 110 us (level)
  the two profiles are of different devices: /device:TPU:14 before, /device:TPU:13 now
where the time goes in v9:
time: 110 us
  starting transfers between devices  46 us (42%)
  waiting for transfers between devices  35.6 us (32%)
  matrix products  11.5 us (10%)
  other arithmetic  7.38 us (7%)
  between operations  6.38 us (6%)
  local copies, waits for them, and re-layouts  2.96 us (3%)
    ppermute x5, starting transfers between devices, send(): lax.ppermute(x.astype(jnp.bfloat16), 'head', perm).astype(jnp.float32)  23.8 us
    ppermute x5, waiting for transfers between devices, send(): lax.ppermute(x.astype(jnp.bfloat16), 'head', perm).astype(jnp.float32)  19.1 us
    ppermute x3, starting transfers between devices, shift_from(): return lax.ppermute(x, axis, [(i, i + step) for i in range(size - step)])  14.5 us
    ppermute x3, waiting for transfers between devices, shift_from(): return lax.ppermute(x, axis, [(i, i + step) for i in range(size - step)])  14.2 us
    ppermute x1, starting transfers between devices, local(): lax.ppermute(to_sib_first, 'head', pair).astype(jnp.float32)  5.78 us
    dot_general x1, matrix products, local(): jnp.dot(sib_rows, w_out, preferred_element_type=jnp.float32)  3.92 us
    dot_general x1, matrix products, local(): jnp.dot(first_rows, w_out, preferred_element_type=jnp.float32)  3.88 us
    ppermute x1, waiting for transfers between devices, local(): lax.ppermute(to_sib_first, 'head', pair).astype(jnp.float32)  2.29 us
  transfers between devices with their start and end apart: 10, of which 7 were waited for; matrix products, arithmetic and copies ran while one was open for 7% of the time, Pallas kernels for 0%

profile of v9, /device:TPU:13, one launch (start us, length us, event | category | flops | bytes accessed | tf_op | source)
XLA Modules:
  0.0 109.8 jit_solution(11926909855016384031)
XLA Ops:
  0.0 0.0 copy-start
  0.0 0.0 copy-start.2
  0.0 1.0 reduce_window_sum.11
  1.0 0.8 fusion.55
  3.1 0.6 constant_dynamic-slice_fusion.1
  4.4 1.2 %copy.27 = bf16[384,512]{0,1:T(8,128)(2,1)S(1)} copy(bf16[384,512]{1,0:T(8,128)(2,1)} %param.7) | data formatting | bytes 786432 | tf_op jit(solution)/shard_map/reshape | solution.py:32
  5.6 1.3 %convolution_convert_fusion.3 = bf16[4,128,128]{2,1,0:T(8,128)(2,1)S(1)} fusion(bf16[384,4,128]{0,2,1:T(8,128)(2,1)S(1)} %bitcast.70, pred[384]{0:T(512)(128)(4,1)S(1)} %broadcast_compare_fusion, bf16[384,512]{1,0:T(8,128)(2,1)} %param.8), kind=kOutput, calls=%fused_computation.19 | convolution fusion | flops 50593792 | bytes 917888 | tf_op jit(solution)/shard_map/thd,the->hde/dot_general | solution.py:39
  6.8 4.9 %collective-permute-start = (bf16[4,128,128]{2,1,0:T(8,128)(2,1)S(1)}, bf16[4,128,128]{2,1,0:T(8,128)(2,1)S(1)}, u32[]{:S(2)}, u32[]{:S(2)}) collective-permute-start(bf16[4,128,128]{2,1,0:T(8,128)(2,1)S(1)} %convolution_convert_fusion.3), channel_id=1, source_target_pairs={{0,16},{16,32},{32,48},{48,64},{64,80},{80,96},{96,112},{112,128},... | collective-permute-start | bytes 393224 | tf_op jit(solution)/shard_map/ppermute | solution.py:11
  11.7 7.6 %collective-permute-start.1 = (bf16[4,128,128]{2,1,0:T(8,128)(2,1)S(1)}, bf16[4,128,128]{2,1,0:T(8,128)(2,1)S(1)}, u32[]{:S(2)}, u32[]{:S(2)}) collective-permute-start(bf16[4,128,128]{2,1,0:T(8,128)(2,1)S(1)} %convolution_convert_fusion.3), channel_id=1, source_target_pairs={{0,32},{16,48},{32,64},{48,80},{64,96},{80,112},{96,128},{112,144}... | collective-permute-start | bytes 393224 | tf_op jit(solution)/shard_map/ppermute | solution.py:11
  19.4 0.2 convert_reduce_fusion
  19.6 0.1 fusion.14
  19.8 0.0 copy-done
  19.8 0.0 copy-done.2
  19.8 0.8 fusion.3
  20.6 0.0 copy-start.1
  20.8 0.5 slice.37
  25.1 2.8 %collective-permute-done = bf16[4,128,128]{2,1,0:T(8,128)(2,1)S(1)} collective-permute-done((bf16[4,128,128]{2,1,0:T(8,128)(2,1)S(1)}, bf16[4,128,128]{2,1,0:T(8,128)(2,1)S(1)}, u32[]{:S(2)}, u32[]{:S(2)}) %collective-permute-start) | collective-permute-done | bytes 131104 | tf_op jit(solution)/shard_map/ppermute | solution.py:11
  27.9 4.7 %collective-permute-done.1 = bf16[4,128,128]{2,1,0:T(8,128)(2,1)S(1)} collective-permute-done((bf16[4,128,128]{2,1,0:T(8,128)(2,1)S(1)}, bf16[4,128,128]{2,1,0:T(8,128)(2,1)S(1)}, u32[]{:S(2)}, u32[]{:S(2)}) %collective-permute-start.1) | collective-permute-done | bytes 131104 | tf_op jit(solution)/shard_map/ppermute | solution.py:11
  32.7 1.9 %collective-permute-start.2 = (bf16[4,128,128]{2,1,0:T(8,128)(2,1)S(1)}, bf16[4,128,128]{2,1,0:T(8,128)(2,1)S(1)}, u32[]{:S(2)}, u32[]{:S(2)}) collective-permute-start(bf16[4,128,128]{2,1,0:T(8,128)(2,1)S(1)} %fusion.31), channel_id=1, source_target_pairs={{0,32},{16,48},{32,64},{48,80},{64,96},{80,112},{96,128},{112,144}... | collective-permute-start | bytes 393224 | tf_op jit(solution)/shard_map/ppermute | solution.py:11
  34.6 0.7 and_convert_fusion
  35.3 6.7 %collective-permute-done.2 = bf16[4,128,128]{2,1,0:T(8,128)(2,1)S(1)} collective-permute-done((bf16[4,128,128]{2,1,0:T(8,128)(2,1)S(1)}, bf16[4,128,128]{2,1,0:T(8,128)(2,1)S(1)}, u32[]{:S(2)}, u32[]{:S(2)}) %collective-permute-start.2) | collective-permute-done | bytes 131104 | tf_op jit(solution)/shard_map/ppermute | solution.py:11
  42.0 0.6 multiply_reduce_fusion
  42.6 0.0 copy-done.1
  42.6 0.1 multiply_convert_fusion
  42.8 0.2 copy.25
  43.0 0.2 convert_element_type.135
  43.2 3.9 %convolution_convert_fusion = bf16[144,6144]{1,0:T(8,128)(2,1)S(1)} fusion(bf16[512,6144]{1,0:T(8,128)(2,1)} %param.11, bf16[48,512]{1,0:T(8,128)(2,1)S(1)} %get-tuple-element.16, bf16[48,512]{1,0:T(8,128)(2,1)S(1)} %get-tuple-element.17, bf16[48,512]{1,0:T(8,128)(2,1)S(1)} %get-tuple-element.15), kind=kOutput, calls=%fused_computation | convolution fusion | flops 907296768 | bytes 8208384 | tf_op jit(solution)/shard_map/dot_general | solution.py:85
  47.1 0.1 fusion.62
  47.2 1.0 pad_maximum_fusion
  48.2 5.8 %collective-permute-start.4 = (bf16[72,6144]{1,0:T(8,128)(2,1)}, bf16[72,6144]{1,0:T(8,128)(2,1)}, u32[]{:S(2)}, u32[]{:S(2)}) collective-permute-start(bf16[72,6144]{1,0:T(8,128)(2,1)} %pad_maximum_fusion), channel_id=1, source_target_pairs={{0,1},{1,0},{2,3},{3,2},{4,5},{5,4},{6,7},{7,6},{8,9},{9,8},{10,11... | collective-permute-start | bytes 2654216 | tf_op jit(solution)/shard_map/ppermute | solution.py:88
  54.1 2.3 %collective-permute-done.4 = bf16[72,6144]{1,0:T(8,128)(2,1)} collective-permute-done((bf16[72,6144]{1,0:T(8,128)(2,1)}, bf16[72,6144]{1,0:T(8,128)(2,1)}, u32[]{:S(2)}, u32[]{:S(2)}) %collective-permute-start.4) | collective-permute-done | bytes 884768 | tf_op jit(solution)/shard_map/ppermute | solution.py:88
  56.4 1.3 %convert_element_type.142 = f32[72,6144]{1,0:T(8,128)S(1)} convert(bf16[72,6144]{1,0:T(8,128)(2,1)} %collective-permute-done.4) | non-fusion elementwise | flops 442368 | bytes 2654208 | tf_op jit(solution)/shard_map/convert_element_type | solution.py:88
  57.7 0.1 fusion.13
  57.8 5.9 %collective-permute-start.5 = (bf16[24,6144]{1,0:T(8,128)(2,1)S(1)}, bf16[24,6144]{1,0:T(8,128)(2,1)S(1)}, u32[]{:S(2)}, u32[]{:S(2)}) collective-permute-start(bf16[24,6144]{1,0:T(8,128)(2,1)S(1)} %fusion.13), channel_id=1, source_target_pairs={{0,2},{1,15},{2,4},{3,1},{4,6},{5,3},{6,8},{7,5},{8,10},{9,7},{10,... | collective-permute-start | bytes 884744 | tf_op jit(solution)/shard_map/ppermute | solution.py:117
  63.7 0.0 slice-start
  63.7 0.0 slice-start.1
  63.7 3.9 %convolution_convert_fusion.1 = bf16[120,6144]{1,0:T(8,128)(2,1)S(1)} fusion(bf16[512,6144]{1,0:T(8,128)(2,1)} %param.11, bf16[24,512]{1,0:T(8,128)(2,1)S(1)} %get-tuple-element.23, bf16[48,512]{1,0:T(8,128)(2,1)S(1)} %get-tuple-element.18, bf16[48,512]{1,0:T(8,128)(2,1)S(1)} %get-tuple-element.19), kind=kOutput, calls=%fused_computation.1 | convolution fusion | flops 756080640 | bytes 7888896 | tf_op jit(solution)/shard_map/dot_general | solution.py:96
  67.6 1.9 %collective-permute-start.3 = (bf16[120,6144]{1,0:T(8,128)(2,1)S(1)}, bf16[120,6144]{1,0:T(8,128)(2,1)S(1)}, u32[]{:S(2)}, u32[]{:S(2)}) collective-permute-start(bf16[120,6144]{1,0:T(8,128)(2,1)S(1)} %convolution_convert_fusion.1), channel_id=1, source_target_pairs={{0,1},{1,0},{2,3},{3,2},{4,5},{5,4},{6,7},{7,6},{8,9},{9,8},{10,11... | collective-permute-start | bytes 4423688 | tf_op jit(solution)/shard_map/ppermute | solution.py:97
  69.6 0.0 collective-permute-done.5
  69.6 0.2 fusion.5
  69.8 2.9 %collective-permute-start.6 = (bf16[48,6144]{1,0:T(8,128)(2,1)S(1)}, bf16[48,6144]{1,0:T(8,128)(2,1)S(1)}, u32[]{:S(2)}, u32[]{:S(2)}) collective-permute-start(bf16[48,6144]{1,0:T(8,128)(2,1)S(1)} %fusion.5), channel_id=1, source_target_pairs={{0,2},{1,15},{2,4},{3,1},{4,6},{5,3},{6,8},{7,5},{8,10},{9,7},{10,... | collective-permute-start | bytes 1769480 | tf_op jit(solution)/shard_map/ppermute | solution.py:117
  72.7 0.0 slice-done
  72.7 0.0 slice-done.1
  72.7 1.0 convolution_convert_fusion.2
  73.8 0.3 convert_element_type.137
  74.1 0.0 collective-permute-done.3
  74.1 0.3 convert_element_type.139
  74.4 6.4 %collective-permute-done.6 = bf16[48,6144]{1,0:T(8,128)(2,1)S(1)} collective-permute-done((bf16[48,6144]{1,0:T(8,128)(2,1)S(1)}, bf16[48,6144]{1,0:T(8,128)(2,1)S(1)}, u32[]{:S(2)}, u32[]{:S(2)}) %collective-permute-start.6) | collective-permute-done | bytes 589856 | tf_op jit(solution)/shard_map/ppermute | solution.py:117
  80.8 0.2 fusion.7
  80.9 3.8 %collective-permute-start.7 = (bf16[48,6144]{1,0:T(8,128)(2,1)S(1)}, bf16[48,6144]{1,0:T(8,128)(2,1)S(1)}, u32[]{:S(2)}, u32[]{:S(2)}) collective-permute-start(bf16[48,6144]{1,0:T(8,128)(2,1)S(1)} %fusion.7), channel_id=1, source_target_pairs={{0,2},{1,15},{2,4},{3,1},{4,6},{5,3},{6,8},{7,5},{8,10},{9,7},{10,... | collective-permute-start | bytes 1769480 | tf_op jit(solution)/shard_map/ppermute | solution.py:117
  84.7 7.1 %collective-permute-done.7 = bf16[48,6144]{1,0:T(8,128)(2,1)S(1)} collective-permute-done((bf16[48,6144]{1,0:T(8,128)(2,1)S(1)}, bf16[48,6144]{1,0:T(8,128)(2,1)S(1)}, u32[]{:S(2)}, u32[]{:S(2)}) %collective-permute-start.7) | collective-permute-done | bytes 589856 | tf_op jit(solution)/shard_map/ppermute | solution.py:117
  91.9 0.1 fusion.8
  92.1 4.7 %collective-permute-start.8 = (bf16[24,6144]{1,0:T(8,128)(2,1)S(1)}, bf16[24,6144]{1,0:T(8,128)(2,1)S(1)}, u32[]{:S(2)}, u32[]{:S(2)}) collective-permute-start(bf16[24,6144]{1,0:T(8,128)(2,1)S(1)} %get-tuple-element.13), channel_id=1, source_target_pairs={{0,2},{1,15},{2,4},{3,1},{4,6},{5,3},{6,8},{7,5},{8,10},{9,7},{10,... | collective-permute-start | bytes 884744 | tf_op jit(solution)/shard_map/ppermute | solution.py:117
  96.8 6.6 %collective-permute-start.9 = (bf16[24,6144]{1,0:T(8,128)(2,1)S(1)}, bf16[24,6144]{1,0:T(8,128)(2,1)S(1)}, u32[]{:S(2)}, u32[]{:S(2)}) collective-permute-start(bf16[24,6144]{1,0:T(8,128)(2,1)S(1)} %get-tuple-element.14), channel_id=1, source_target_pairs={{0,3},{1,14},{2,5},{3,0},{4,7},{5,2},{6,9},{7,4},{8,11},{9,6},{10,... | collective-permute-start | bytes 884744 | tf_op jit(solution)/shard_map/ppermute | solution.py:117
  103.4 0.0 collective-permute-done.8
  103.4 5.6 %collective-permute-done.9 = bf16[24,6144]{1,0:T(8,128)(2,1)S(1)} collective-permute-done((bf16[24,6144]{1,0:T(8,128)(2,1)S(1)}, bf16[24,6144]{1,0:T(8,128)(2,1)S(1)}, u32[]{:S(2)}, u32[]{:S(2)}) %collective-permute-start.9) | collective-permute-done | bytes 294944 | tf_op jit(solution)/shard_map/ppermute | solution.py:117
  109.0 0.8 fusion.12
  (10 shorter events, 0.3 us)
Async XLA Ops:
  0.0 19.8 %copy-start = (bf16[384,512]{1,0:T(8,128)(2,1)S(1)}, bf16[384,512]{1,0:T(8,128)(2,1)}, u32[]{:S(2)}) copy-start(bf16[384,512]{1,0:T(8,128)(2,1)} %param.6) | copy-start | bytes 1179652
  0.0 19.8 %copy-start.2 = (bf16[384,512]{1,0:T(8,128)(2,1)S(1)}, bf16[384,512]{1,0:T(8,128)(2,1)}, u32[]{:S(2)}) copy-start(bf16[384,512]{1,0:T(8,128)(2,1)} %param.8) | copy-start | bytes 1179652
  6.8 21.1 %collective-permute-start = (bf16[4,128,128]{2,1,0:T(8,128)(2,1)S(1)}, bf16[4,128,128]{2,1,0:T(8,128)(2,1)S(1)}, u32[]{:S(2)}, u32[]{:S(2)}) collective-permute-start(bf16[4,128,128]{2,1,0:T(8,128)(2,1)S(1)} %convolution_convert_fusion.3), channel_id=1, source_target_pairs={{0,16},{16,32},{32,48},{48,64},{64,80},{80,96},{96,112},{112,128},... | collective-permute-start | bytes 393224 | tf_op jit(solution)/shard_map/ppermute | solution.py:11
  11.7 20.9 %collective-permute-start.1 = (bf16[4,128,128]{2,1,0:T(8,128)(2,1)S(1)}, bf16[4,128,128]{2,1,0:T(8,128)(2,1)S(1)}, u32[]{:S(2)}, u32[]{:S(2)}) collective-permute-start(bf16[4,128,128]{2,1,0:T(8,128)(2,1)S(1)} %convolution_convert_fusion.3), channel_id=1, source_target_pairs={{0,32},{16,48},{32,64},{48,80},{64,96},{80,112},{96,128},{112,144}... | collective-permute-start | bytes 393224 | tf_op jit(solution)/shard_map/ppermute | solution.py:11
  20.6 22.0 %copy-start.1 = (f32[512]{0:T(512)S(1)}, f32[512]{0:T(512)}, u32[]{:S(2)}) copy-start(f32[512]{0:T(512)} %param.10) | copy-start | bytes 6148
  32.7 9.3 %collective-permute-start.2 = (bf16[4,128,128]{2,1,0:T(8,128)(2,1)S(1)}, bf16[4,128,128]{2,1,0:T(8,128)(2,1)S(1)}, u32[]{:S(2)}, u32[]{:S(2)}) collective-permute-start(bf16[4,128,128]{2,1,0:T(8,128)(2,1)S(1)} %fusion.31), channel_id=1, source_target_pairs={{0,32},{16,48},{32,64},{48,80},{64,96},{80,112},{96,128},{112,144}... | collective-permute-start | bytes 393224 | tf_op jit(solution)/shard_map/ppermute | solution.py:11
  48.2 8.2 %collective-permute-start.4 = (bf16[72,6144]{1,0:T(8,128)(2,1)}, bf16[72,6144]{1,0:T(8,128)(2,1)}, u32[]{:S(2)}, u32[]{:S(2)}) collective-permute-start(bf16[72,6144]{1,0:T(8,128)(2,1)} %pad_maximum_fusion), channel_id=1, source_target_pairs={{0,1},{1,0},{2,3},{3,2},{4,5},{5,4},{6,7},{7,6},{8,9},{9,8},{10,11... | collective-permute-start | bytes 2654216 | tf_op jit(solution)/shard_map/ppermute | solution.py:88
  57.8 11.8 %collective-permute-start.5 = (bf16[24,6144]{1,0:T(8,128)(2,1)S(1)}, bf16[24,6144]{1,0:T(8,128)(2,1)S(1)}, u32[]{:S(2)}, u32[]{:S(2)}) collective-permute-start(bf16[24,6144]{1,0:T(8,128)(2,1)S(1)} %fusion.13), channel_id=1, source_target_pairs={{0,2},{1,15},{2,4},{3,1},{4,6},{5,3},{6,8},{7,5},{8,10},{9,7},{10,... | collective-permute-start | bytes 884744 | tf_op jit(solution)/shard_map/ppermute | solution.py:117
  63.7 9.0 %slice-start = ((s8[6291456]{0:T(1024)(128)(4,1)}), s8[4194304]{0:T(1024)(128)(4,1)S(1)}, s32[]{:S(2)}) async-start(s8[6291456]{0:T(1024)(128)(4,1)} %bitcast.68), calls=%async_computation | async-start | bytes 8388608
  63.7 9.0 %slice-start.1 = ((s8[6291456]{0:T(1024)(128)(4,1)}), s8[2097152]{0:T(1024)(128)(4,1)S(1)}, s32[]{:S(2)}) async-start(s8[6291456]{0:T(1024)(128)(4,1)} %bitcast.68), calls=%async_computation.1 | async-start | bytes 4194304
  67.6 6.4 %collective-permute-start.3 = (bf16[120,6144]{1,0:T(8,128)(2,1)S(1)}, bf16[120,6144]{1,0:T(8,128)(2,1)S(1)}, u32[]{:S(2)}, u32[]{:S(2)}) collective-permute-start(bf16[120,6144]{1,0:T(8,128)(2,1)S(1)} %convolution_convert_fusion.1), channel_id=1, source_target_pairs={{0,1},{1,0},{2,3},{3,2},{4,5},{5,4},{6,7},{7,6},{8,9},{9,8},{10,11... | collective-permute-start | bytes 4423688 | tf_op jit(solution)/shard_map/ppermute | solution.py:97
  69.8 10.9 %collective-permute-start.6 = (bf16[48,6144]{1,0:T(8,128)(2,1)S(1)}, bf16[48,6144]{1,0:T(8,128)(2,1)S(1)}, u32[]{:S(2)}, u32[]{:S(2)}) collective-permute-start(bf16[48,6144]{1,0:T(8,128)(2,1)S(1)} %fusion.5), channel_id=1, source_target_pairs={{0,2},{1,15},{2,4},{3,1},{4,6},{5,3},{6,8},{7,5},{8,10},{9,7},{10,... | collective-permute-start | bytes 1769480 | tf_op jit(solution)/shard_map/ppermute | solution.py:117
  80.9 10.9 %collective-permute-start.7 = (bf16[48,6144]{1,0:T(8,128)(2,1)S(1)}, bf16[48,6144]{1,0:T(8,128)(2,1)S(1)}, u32[]{:S(2)}, u32[]{:S(2)}) collective-permute-start(bf16[48,6144]{1,0:T(8,128)(2,1)S(1)} %fusion.7), channel_id=1, source_target_pairs={{0,2},{1,15},{2,4},{3,1},{4,6},{5,3},{6,8},{7,5},{8,10},{9,7},{10,... | collective-permute-start | bytes 1769480 | tf_op jit(solution)/shard_map/ppermute | solution.py:117
  92.1 11.3 %collective-permute-start.8 = (bf16[24,6144]{1,0:T(8,128)(2,1)S(1)}, bf16[24,6144]{1,0:T(8,128)(2,1)S(1)}, u32[]{:S(2)}, u32[]{:S(2)}) collective-permute-start(bf16[24,6144]{1,0:T(8,128)(2,1)S(1)} %get-tuple-element.13), channel_id=1, source_target_pairs={{0,2},{1,15},{2,4},{3,1},{4,6},{5,3},{6,8},{7,5},{8,10},{9,7},{10,... | collective-permute-start | bytes 884744 | tf_op jit(solution)/shard_map/ppermute | solution.py:117
  96.8 12.2 %collective-permute-start.9 = (bf16[24,6144]{1,0:T(8,128)(2,1)S(1)}, bf16[24,6144]{1,0:T(8,128)(2,1)S(1)}, u32[]{:S(2)}, u32[]{:S(2)}) collective-permute-start(bf16[24,6144]{1,0:T(8,128)(2,1)S(1)} %get-tuple-element.14), channel_id=1, source_target_pairs={{0,3},{1,14},{2,5},{3,0},{4,7},{5,2},{6,9},{7,4},{8,11},{9,6},{10,... | collective-permute-start | bytes 884744 | tf_op jit(solution)/shard_map/ppermute | solution.py:117

commit v10 on v9

--- a/solution.py
+++ b/solution.py
@@ -79,15 +79,25 @@
     steps = n_chip // 2 - 1
     pair = [(i, i ^ 1) for i in range(n_head)]
     first_rows = jnp.concatenate(
-        [take(by_chip, far), take(by_chip, chip - dirn * steps), take(by_chip, chip + dirn * steps)],
+        [
+            halves(take(by_chip, far), 1 - core),
+            take(by_chip, chip - dirn * steps),
+            halves(take(by_chip, far), core),
+            take(by_chip, chip + dirn * steps),
+        ],
         axis=0,
     )
     first_part = jnp.dot(first_rows, w_out, preferred_element_type=jnp.float32).astype(jnp.bfloat16)
-    far_part = first_part[:rows]
-    to_sib_first = jnp.concatenate([halves(far_part, 1 - core), first_part[rows:2 * rows]], axis=0)
-    from_sib_first = lax.ppermute(to_sib_first, "head", pair).astype(jnp.float32)
-    far_sum = halves(far_part, core).astype(jnp.float32) + from_sib_first[:half_rows]
-    near_last = first_part[2 * rows:].astype(jnp.float32) + from_sib_first[half_rows:]
+    lead_rows = half_rows + rows
+    from_sib_first = lax.ppermute(first_part[:lead_rows], "head", pair)
+    far_sum = (
+        first_part[lead_rows:lead_rows + half_rows].astype(jnp.float32)
+        + from_sib_first[:half_rows].astype(jnp.float32)
+    )
+    near_last = (
+        first_part[lead_rows + half_rows:].astype(jnp.float32)
+        + from_sib_first[half_rows:].astype(jnp.float32)
+    )
     sib_rows = jnp.concatenate(
         [take(by_chip, chip - dirn * j) for j in range(1, steps)]
         + [halves(take(by_chip, chip), 1 - core)],

time: 110 us -> 109 us (level)
  other arithmetic: 7.38 us -> 5.11 us
    convert_element_type x1 -> x0, other arithmetic: 1.3 us -> none  [local(): lax.ppermute(to_sib_first, 'head', pair).astype(jnp.float32)]
  transfers between devices with their start and end apart: 10 -> 10, of which waited for: 7 -> 7; matrix products, arithmetic and copies ran while one was open for 7% -> 8% of each run, Pallas kernels for 0% -> 0%
where the time goes in v10:
time: 109 us; the launch traced here: 108 us
  starting transfers between devices  46 us (42%)
  waiting for transfers between devices  35.6 us (33%)
  matrix products  11.5 us (11%)
  between operations  6.31 us (6%)
  other arithmetic  5.11 us (5%)
  local copies, waits for them, and re-layouts  3.85 us (4%)
    ppermute x5, starting transfers between devices, send(): lax.ppermute(x.astype(jnp.bfloat16), 'head', perm).astype(jnp.float32)  23.8 us
    ppermute x5, waiting for transfers between devices, send(): lax.ppermute(x.astype(jnp.bfloat16), 'head', perm).astype(jnp.float32)  19.2 us
    ppermute x3, starting transfers between devices, shift_from(): return lax.ppermute(x, axis, [(i, i + step) for i in range(size - step)])  14.5 us
    ppermute x3, waiting for transfers between devices, shift_from(): return lax.ppermute(x, axis, [(i, i + step) for i in range(size - step)])  14.2 us
    ppermute x1, starting transfers between devices, local(): from_sib_first = lax.ppermute(first_part[:lead_rows], 'head', pair)  5.78 us
    dot_general x1, matrix products, local(): jnp.dot(sib_rows, w_out, preferred_element_type=jnp.float32)  3.92 us
    dot_general x1, matrix products, local(): jnp.dot(first_rows, w_out, preferred_element_type=jnp.float32)  3.88 us
    ppermute x1, waiting for transfers between devices, local(): from_sib_first = lax.ppermute(first_part[:lead_rows], 'head', pair)  2.24 us
  transfers between devices with their start and end apart: 10, of which 7 were waited for; matrix products, arithmetic and copies ran while one was open for 8% of the time, Pallas kernels for 0%

profile of v10, /device:TPU:13, one launch (start us, length us, event | category | flops | bytes accessed | tf_op | source)
XLA Modules:
  0.0 108.3 jit_solution(5218324208164565782)
XLA Ops:
  0.0 0.0 copy-start
  0.0 0.0 copy-start.2
  0.0 1.0 reduce_window_sum.11
  1.0 0.8 fusion.54
  3.1 0.6 constant_dynamic-slice_fusion
  4.4 1.2 %copy.27 = bf16[384,512]{0,1:T(8,128)(2,1)S(1)} copy(bf16[384,512]{1,0:T(8,128)(2,1)} %param.7) | data formatting | bytes 786432 | tf_op jit(solution)/shard_map/reshape | solution.py:32
  5.6 1.3 %convolution_convert_fusion.3 = bf16[4,128,128]{2,1,0:T(8,128)(2,1)S(1)} fusion(bf16[384,4,128]{0,2,1:T(8,128)(2,1)S(1)} %bitcast.72, pred[384]{0:T(512)(128)(4,1)S(1)} %broadcast_compare_fusion, bf16[384,512]{1,0:T(8,128)(2,1)} %param.8), kind=kOutput, calls=%fused_computation.17 | convolution fusion | flops 50593792 | bytes 917888 | tf_op jit(solution)/shard_map/thd,the->hde/dot_general | solution.py:39
  6.8 4.9 %collective-permute-start = (bf16[4,128,128]{2,1,0:T(8,128)(2,1)S(1)}, bf16[4,128,128]{2,1,0:T(8,128)(2,1)S(1)}, u32[]{:S(2)}, u32[]{:S(2)}) collective-permute-start(bf16[4,128,128]{2,1,0:T(8,128)(2,1)S(1)} %convolution_convert_fusion.3), channel_id=1, source_target_pairs={{0,16},{16,32},{32,48},{48,64},{64,80},{80,96},{96,112},{112,128},... | collective-permute-start | bytes 393224 | tf_op jit(solution)/shard_map/ppermute | solution.py:11
  11.7 7.6 %collective-permute-start.1 = (bf16[4,128,128]{2,1,0:T(8,128)(2,1)S(1)}, bf16[4,128,128]{2,1,0:T(8,128)(2,1)S(1)}, u32[]{:S(2)}, u32[]{:S(2)}) collective-permute-start(bf16[4,128,128]{2,1,0:T(8,128)(2,1)S(1)} %convolution_convert_fusion.3), channel_id=1, source_target_pairs={{0,32},{16,48},{32,64},{48,80},{64,96},{80,112},{96,128},{112,144}... | collective-permute-start | bytes 393224 | tf_op jit(solution)/shard_map/ppermute | solution.py:11
  19.4 0.2 convert_reduce_fusion
  19.6 0.1 fusion.11
  19.8 0.0 copy-done
  19.8 0.0 copy-done.2
  19.8 0.8 fusion.3
  20.6 0.0 copy-start.1
  20.7 0.5 slice.37
  25.1 2.8 %collective-permute-done = bf16[4,128,128]{2,1,0:T(8,128)(2,1)S(1)} collective-permute-done((bf16[4,128,128]{2,1,0:T(8,128)(2,1)S(1)}, bf16[4,128,128]{2,1,0:T(8,128)(2,1)S(1)}, u32[]{:S(2)}, u32[]{:S(2)}) %collective-permute-start) | collective-permute-done | bytes 131104 | tf_op jit(solution)/shard_map/ppermute | solution.py:11
  27.9 4.7 %collective-permute-done.1 = bf16[4,128,128]{2,1,0:T(8,128)(2,1)S(1)} collective-permute-done((bf16[4,128,128]{2,1,0:T(8,128)(2,1)S(1)}, bf16[4,128,128]{2,1,0:T(8,128)(2,1)S(1)}, u32[]{:S(2)}, u32[]{:S(2)}) %collective-permute-start.1) | collective-permute-done | bytes 131104 | tf_op jit(solution)/shard_map/ppermute | solution.py:11
  32.7 1.9 %collective-permute-start.2 = (bf16[4,128,128]{2,1,0:T(8,128)(2,1)S(1)}, bf16[4,128,128]{2,1,0:T(8,128)(2,1)S(1)}, u32[]{:S(2)}, u32[]{:S(2)}) collective-permute-start(bf16[4,128,128]{2,1,0:T(8,128)(2,1)S(1)} %fusion.28), channel_id=1, source_target_pairs={{0,32},{16,48},{32,64},{48,80},{64,96},{80,112},{96,128},{112,144}... | collective-permute-start | bytes 393224 | tf_op jit(solution)/shard_map/ppermute | solution.py:11
  34.6 0.7 and_convert_fusion
  35.3 6.7 %collective-permute-done.2 = bf16[4,128,128]{2,1,0:T(8,128)(2,1)S(1)} collective-permute-done((bf16[4,128,128]{2,1,0:T(8,128)(2,1)S(1)}, bf16[4,128,128]{2,1,0:T(8,128)(2,1)S(1)}, u32[]{:S(2)}, u32[]{:S(2)}) %collective-permute-start.2) | collective-permute-done | bytes 131104 | tf_op jit(solution)/shard_map/ppermute | solution.py:11
  42.0 0.6 multiply_reduce_fusion
  42.6 0.0 copy-done.1
  42.6 0.1 multiply_convert_fusion
  42.8 0.2 copy.25
  43.0 0.2 convert_element_type.138
  43.3 3.9 %convolution_convert_fusion = bf16[144,6144]{1,0:T(8,128)(2,1)S(1)} fusion(bf16[512,6144]{1,0:T(8,128)(2,1)} %param.11, bf16[48,512]{1,0:T(8,128)(2,1)S(1)} %get-tuple-element.18, bf16[24,512]{1,0:T(8,128)(2,1)S(1)} %get-tuple-element.14, bf16[48,512]{1,0:T(8,128)(2,1)S(1)} %get-tuple-element.17, bf16[24,512]{1,0:T(8,128)(2,1)S(1)} %get-tuple-element.13), kind=kOutput, calls=%fused_computation | convolution fusion | flops 907444224 | bytes 8208384 | tf_op jit(solution)/shard_map/dot_general | solution.py:90
  47.2 1.0 slice.54
  48.2 5.8 %collective-permute-start.4 = (bf16[72,6144]{1,0:T(8,128)(2,1)}, bf16[72,6144]{1,0:T(8,128)(2,1)S(1)}, u32[]{:S(2)}, u32[]{:S(2)}) collective-permute-start(bf16[72,6144]{1,0:T(8,128)(2,1)} %slice.54), channel_id=1, source_target_pairs={{0,1},{1,0},{2,3},{3,2},{4,5},{5,4},{6,7},{7,6},{8,9},{9,8},{10,11... | collective-permute-start | bytes 2654216 | tf_op jit(solution)/shard_map/ppermute | solution.py:92
  53.9 2.2 %collective-permute-done.4 = bf16[72,6144]{1,0:T(8,128)(2,1)S(1)} collective-permute-done((bf16[72,6144]{1,0:T(8,128)(2,1)}, bf16[72,6144]{1,0:T(8,128)(2,1)S(1)}, u32[]{:S(2)}, u32[]{:S(2)}) %collective-permute-start.4) | collective-permute-done | bytes 884768 | tf_op jit(solution)/shard_map/ppermute | solution.py:92
  56.2 0.1 add_convert_fusion.1
  56.3 5.9 %collective-permute-start.5 = (bf16[24,6144]{1,0:T(8,128)(2,1)S(1)}, bf16[24,6144]{1,0:T(8,128)(2,1)S(1)}, u32[]{:S(2)}, u32[]{:S(2)}) collective-permute-start(bf16[24,6144]{1,0:T(8,128)(2,1)S(1)} %add_convert_fusion.1), channel_id=1, source_target_pairs={{0,2},{1,15},{2,4},{3,1},{4,6},{5,3},{6,8},{7,5},{8,10},{9,7},{10,... | collective-permute-start | bytes 884744 | tf_op jit(solution)/shard_map/ppermute | solution.py:127
  62.2 0.0 slice-start
  62.2 0.0 slice-start.1
  62.2 3.9 %convolution_convert_fusion.1 = bf16[120,6144]{1,0:T(8,128)(2,1)S(1)} fusion(bf16[512,6144]{1,0:T(8,128)(2,1)} %param.11, bf16[24,512]{1,0:T(8,128)(2,1)S(1)} %get-tuple-element.15, bf16[48,512]{1,0:T(8,128)(2,1)S(1)} %get-tuple-element.19, bf16[48,512]{1,0:T(8,128)(2,1)S(1)} %get-tuple-element.20), kind=kOutput, calls=%fused_computation.1 | convolution fusion | flops 756080640 | bytes 7888896 | tf_op jit(solution)/shard_map/dot_general | solution.py:106
  66.1 1.9 %collective-permute-start.3 = (bf16[120,6144]{1,0:T(8,128)(2,1)S(1)}, bf16[120,6144]{1,0:T(8,128)(2,1)S(1)}, u32[]{:S(2)}, u32[]{:S(2)}) collective-permute-start(bf16[120,6144]{1,0:T(8,128)(2,1)S(1)} %convolution_convert_fusion.1), channel_id=1, source_target_pairs={{0,1},{1,0},{2,3},{3,2},{4,5},{5,4},{6,7},{7,6},{8,9},{9,8},{10,11... | collective-permute-start | bytes 4423688 | tf_op jit(solution)/shard_map/ppermute | solution.py:107
  68.0 0.0 collective-permute-done.5
  68.1 0.2 add_convert_fusion
  68.3 2.8 %collective-permute-start.6 = (bf16[48,6144]{1,0:T(8,128)(2,1)S(1)}, bf16[48,6144]{1,0:T(8,128)(2,1)S(1)}, u32[]{:S(2)}, u32[]{:S(2)}) collective-permute-start(bf16[48,6144]{1,0:T(8,128)(2,1)S(1)} %add_convert_fusion), channel_id=1, source_target_pairs={{0,2},{1,15},{2,4},{3,1},{4,6},{5,3},{6,8},{7,5},{8,10},{9,7},{10,... | collective-permute-start | bytes 1769480 | tf_op jit(solution)/shard_map/ppermute | solution.py:127
  71.2 0.0 slice-done
  71.2 0.0 slice-done.1
  71.2 1.0 convolution_convert_fusion.2
  72.3 0.3 convert_element_type.140
  72.6 0.0 collective-permute-done.3
  72.6 0.3 convert_element_type.142
  72.9 6.4 %collective-permute-done.6 = bf16[48,6144]{1,0:T(8,128)(2,1)S(1)} collective-permute-done((bf16[48,6144]{1,0:T(8,128)(2,1)S(1)}, bf16[48,6144]{1,0:T(8,128)(2,1)S(1)}, u32[]{:S(2)}, u32[]{:S(2)}) %collective-permute-start.6) | collective-permute-done | bytes 589856 | tf_op jit(solution)/shard_map/ppermute | solution.py:127
  79.3 0.2 fusion.5
  79.4 3.8 %collective-permute-start.7 = (bf16[48,6144]{1,0:T(8,128)(2,1)S(1)}, bf16[48,6144]{1,0:T(8,128)(2,1)S(1)}, u32[]{:S(2)}, u32[]{:S(2)}) collective-permute-start(bf16[48,6144]{1,0:T(8,128)(2,1)S(1)} %fusion.5), channel_id=1, source_target_pairs={{0,2},{1,15},{2,4},{3,1},{4,6},{5,3},{6,8},{7,5},{8,10},{9,7},{10,... | collective-permute-start | bytes 1769480 | tf_op jit(solution)/shard_map/ppermute | solution.py:127
  83.2 7.2 %collective-permute-done.7 = bf16[48,6144]{1,0:T(8,128)(2,1)S(1)} collective-permute-done((bf16[48,6144]{1,0:T(8,128)(2,1)S(1)}, bf16[48,6144]{1,0:T(8,128)(2,1)S(1)}, u32[]{:S(2)}, u32[]{:S(2)}) %collective-permute-start.7) | collective-permute-done | bytes 589856 | tf_op jit(solution)/shard_map/ppermute | solution.py:127
  90.4 0.1 fusion.6
  90.6 4.7 %collective-permute-start.8 = (bf16[24,6144]{1,0:T(8,128)(2,1)S(1)}, bf16[24,6144]{1,0:T(8,128)(2,1)S(1)}, u32[]{:S(2)}, u32[]{:S(2)}) collective-permute-start(bf16[24,6144]{1,0:T(8,128)(2,1)S(1)} %get-tuple-element.11), channel_id=1, source_target_pairs={{0,2},{1,15},{2,4},{3,1},{4,6},{5,3},{6,8},{7,5},{8,10},{9,7},{10,... | collective-permute-start | bytes 884744 | tf_op jit(solution)/shard_map/ppermute | solution.py:127
  95.2 6.6 %collective-permute-start.9 = (bf16[24,6144]{1,0:T(8,128)(2,1)S(1)}, bf16[24,6144]{1,0:T(8,128)(2,1)S(1)}, u32[]{:S(2)}, u32[]{:S(2)}) collective-permute-start(bf16[24,6144]{1,0:T(8,128)(2,1)S(1)} %get-tuple-element.12), channel_id=1, source_target_pairs={{0,3},{1,14},{2,5},{3,0},{4,7},{5,2},{6,9},{7,4},{8,11},{9,6},{10,... | collective-permute-start | bytes 884744 | tf_op jit(solution)/shard_map/ppermute | solution.py:127
  101.9 0.0 collective-permute-done.8
  101.9 5.6 %collective-permute-done.9 = bf16[24,6144]{1,0:T(8,128)(2,1)S(1)} collective-permute-done((bf16[24,6144]{1,0:T(8,128)(2,1)S(1)}, bf16[24,6144]{1,0:T(8,128)(2,1)S(1)}, u32[]{:S(2)}, u32[]{:S(2)}) %collective-permute-start.9) | collective-permute-done | bytes 294944 | tf_op jit(solution)/shard_map/ppermute | solution.py:127
  107.5 0.8 fusion.10
  (9 shorter events, 0.2 us)
Async XLA Ops:
  0.0 19.8 %copy-start = (bf16[384,512]{1,0:T(8,128)(2,1)S(1)}, bf16[384,512]{1,0:T(8,128)(2,1)}, u32[]{:S(2)}) copy-start(bf16[384,512]{1,0:T(8,128)(2,1)} %param.6) | copy-start | bytes 1179652
  0.0 19.8 %copy-start.2 = (bf16[384,512]{1,0:T(8,128)(2,1)S(1)}, bf16[384,512]{1,0:T(8,128)(2,1)}, u32[]{:S(2)}) copy-start(bf16[384,512]{1,0:T(8,128)(2,1)} %param.8) | copy-start | bytes 1179652
  6.8 21.1 %collective-permute-start = (bf16[4,128,128]{2,1,0:T(8,128)(2,1)S(1)}, bf16[4,128,128]{2,1,0:T(8,128)(2,1)S(1)}, u32[]{:S(2)}, u32[]{:S(2)}) collective-permute-start(bf16[4,128,128]{2,1,0:T(8,128)(2,1)S(1)} %convolution_convert_fusion.3), channel_id=1, source_target_pairs={{0,16},{16,32},{32,48},{48,64},{64,80},{80,96},{96,112},{112,128},... | collective-permute-start | bytes 393224 | tf_op jit(solution)/shard_map/ppermute | solution.py:11
  11.7 20.9 %collective-permute-start.1 = (bf16[4,128,128]{2,1,0:T(8,128)(2,1)S(1)}, bf16[4,128,128]{2,1,0:T(8,128)(2,1)S(1)}, u32[]{:S(2)}, u32[]{:S(2)}) collective-permute-start(bf16[4,128,128]{2,1,0:T(8,128)(2,1)S(1)} %convolution_convert_fusion.3), channel_id=1, source_target_pairs={{0,32},{16,48},{32,64},{48,80},{64,96},{80,112},{96,128},{112,144}... | collective-permute-start | bytes 393224 | tf_op jit(solution)/shard_map/ppermute | solution.py:11
  20.6 22.0 %copy-start.1 = (f32[512]{0:T(512)S(1)}, f32[512]{0:T(512)}, u32[]{:S(2)}) copy-start(f32[512]{0:T(512)} %param.10) | copy-start | bytes 6148
  32.7 9.3 %collective-permute-start.2 = (bf16[4,128,128]{2,1,0:T(8,128)(2,1)S(1)}, bf16[4,128,128]{2,1,0:T(8,128)(2,1)S(1)}, u32[]{:S(2)}, u32[]{:S(2)}) collective-permute-start(bf16[4,128,128]{2,1,0:T(8,128)(2,1)S(1)} %fusion.28), channel_id=1, source_target_pairs={{0,32},{16,48},{32,64},{48,80},{64,96},{80,112},{96,128},{112,144}... | collective-permute-start | bytes 393224 | tf_op jit(solution)/shard_map/ppermute | solution.py:11
  48.2 8.0 %collective-permute-start.4 = (bf16[72,6144]{1,0:T(8,128)(2,1)}, bf16[72,6144]{1,0:T(8,128)(2,1)S(1)}, u32[]{:S(2)}, u32[]{:S(2)}) collective-permute-start(bf16[72,6144]{1,0:T(8,128)(2,1)} %slice.54), channel_id=1, source_target_pairs={{0,1},{1,0},{2,3},{3,2},{4,5},{5,4},{6,7},{7,6},{8,9},{9,8},{10,11... | collective-permute-start | bytes 2654216 | tf_op jit(solution)/shard_map/ppermute | solution.py:92
  56.3 11.8 %collective-permute-start.5 = (bf16[24,6144]{1,0:T(8,128)(2,1)S(1)}, bf16[24,6144]{1,0:T(8,128)(2,1)S(1)}, u32[]{:S(2)}, u32[]{:S(2)}) collective-permute-start(bf16[24,6144]{1,0:T(8,128)(2,1)S(1)} %add_convert_fusion.1), channel_id=1, source_target_pairs={{0,2},{1,15},{2,4},{3,1},{4,6},{5,3},{6,8},{7,5},{8,10},{9,7},{10,... | collective-permute-start | bytes 884744 | tf_op jit(solution)/shard_map/ppermute | solution.py:127
  62.2 9.0 %slice-start = ((s8[6291456]{0:T(1024)(128)(4,1)}), s8[4194304]{0:T(1024)(128)(4,1)S(1)}, s32[]{:S(2)}) async-start(s8[6291456]{0:T(1024)(128)(4,1)} %bitcast.70), calls=%async_computation | async-start | bytes 8388608
  62.2 9.0 %slice-start.1 = ((s8[6291456]{0:T(1024)(128)(4,1)}), s8[2097152]{0:T(1024)(128)(4,1)S(1)}, s32[]{:S(2)}) async-start(s8[6291456]{0:T(1024)(128)(4,1)} %bitcast.70), calls=%async_computation.1 | async-start | bytes 4194304
  66.1 6.4 %collective-permute-start.3 = (bf16[120,6144]{1,0:T(8,128)(2,1)S(1)}, bf16[120,6144]{1,0:T(8,128)(2,1)S(1)}, u32[]{:S(2)}, u32[]{:S(2)}) collective-permute-start(bf16[120,6144]{1,0:T(8,128)(2,1)S(1)} %convolution_convert_fusion.1), channel_id=1, source_target_pairs={{0,1},{1,0},{2,3},{3,2},{4,5},{5,4},{6,7},{7,6},{8,9},{9,8},{10,11... | collective-permute-start | bytes 4423688 | tf_op jit(solution)/shard_map/ppermute | solution.py:107
  68.3 10.9 %collective-permute-start.6 = (bf16[48,6144]{1,0:T(8,128)(2,1)S(1)}, bf16[48,6144]{1,0:T(8,128)(2,1)S(1)}, u32[]{:S(2)}, u32[]{:S(2)}) collective-permute-start(bf16[48,6144]{1,0:T(8,128)(2,1)S(1)} %add_convert_fusion), channel_id=1, source_target_pairs={{0,2},{1,15},{2,4},{3,1},{4,6},{5,3},{6,8},{7,5},{8,10},{9,7},{10,... | collective-permute-start | bytes 1769480 | tf_op jit(solution)/shard_map/ppermute | solution.py:127
  79.4 10.9 %collective-permute-start.7 = (bf16[48,6144]{1,0:T(8,128)(2,1)S(1)}, bf16[48,6144]{1,0:T(8,128)(2,1)S(1)}, u32[]{:S(2)}, u32[]{:S(2)}) collective-permute-start(bf16[48,6144]{1,0:T(8,128)(2,1)S(1)} %fusion.5), channel_id=1, source_target_pairs={{0,2},{1,15},{2,4},{3,1},{4,6},{5,3},{6,8},{7,5},{8,10},{9,7},{10,... | collective-permute-start | bytes 1769480 | tf_op jit(solution)/shard_map/ppermute | solution.py:127
  90.6 11.3 %collective-permute-start.8 = (bf16[24,6144]{1,0:T(8,128)(2,1)S(1)}, bf16[24,6144]{1,0:T(8,128)(2,1)S(1)}, u32[]{:S(2)}, u32[]{:S(2)}) collective-permute-start(bf16[24,6144]{1,0:T(8,128)(2,1)S(1)} %get-tuple-element.11), channel_id=1, source_target_pairs={{0,2},{1,15},{2,4},{3,1},{4,6},{5,3},{6,8},{7,5},{8,10},{9,7},{10,... | collective-permute-start | bytes 884744 | tf_op jit(solution)/shard_map/ppermute | solution.py:127
  95.2 12.2 %collective-permute-start.9 = (bf16[24,6144]{1,0:T(8,128)(2,1)S(1)}, bf16[24,6144]{1,0:T(8,128)(2,1)S(1)}, u32[]{:S(2)}, u32[]{:S(2)}) collective-permute-start(bf16[24,6144]{1,0:T(8,128)(2,1)S(1)} %get-tuple-element.12), channel_id=1, source_target_pairs={{0,3},{1,14},{2,5},{3,0},{4,7},{5,2},{6,9},{7,4},{8,11},{9,6},{10,... | collective-permute-start | bytes 884744 | tf_op jit(solution)/shard_map/ppermute | solution.py:127
